TPU v7x, 256 devices: a whole 4x4x8 slice. The times are simulated.
256 devices in a mesh: tensor: 2 (over core), row: 16 (over x, y), col: 8 (over z).
Axes of the slice: x: 4, y: 4, z: 8, core: 2. Of those that a mesh axis runs over, the one named last changes fastest.
Arguments:
- integral_tiles: bfloat16 [8192, 8, 4096], P(('tensor', 'row', 'col')), may hold values from -6 to 6
- tile_index: int32 [8192, 3], P(('tensor', 'row', 'col')), may hold values from 0 to 127, as said below
- virtual_coeff: bfloat16 [8192, 2048], P('col'), may hold values from -0.09375 to 0.09375
- occupied_coeff: bfloat16 [2048, 512], P('row'), may hold values from -0.125 to 0.125
Outputs:
- pair_tensor: bfloat16 [2048, 32, 512], P(('row', 'col'), 'tensor')
Inputs may be any that keep to these rules, and one draw needn't show every extreme that they name: `tile_index`: the tiles of the device at index (t, r, c) of tensor, row, col all have their nu block in c * 16 .. (c + 1) * 16 - 1, their auxiliary block below 4 and their mu block below 32. A tile's owner is (tensor index a // 2, row index m // 2) in the same col. Each device holds at most 2 tiles for any one owner; in every draw some owner gets exactly 2 tiles from every device of its col. Tiles with equal indices may occur and add up.
All inputs are finite; a program needn't handle non-finite values.
Results may differ from a plain program's by a relative error of at most 0.025.
Values may be sent and summed in bfloat16 or wider, within the bound.
No kernel may reach another device: no remote copies, remote signals or barrier semaphores. Data moves between devices by JAX's collectives and lax.ppermute only.
A program may use at most 128 MiB of HBM per device.

v0:
```python
import jax
import jax.numpy as jnp
from jax import lax
from jax.sharding import PartitionSpec as P

TB = 64
PB = 8
AB = 2
MB = 2
NBC = 16
CAP = 2
NV = 2048
NOCC = 512


def shards(integral_tiles, tile_index, virtual_coeff, occupied_coeff):
    tensor_at = lax.axis_index("tensor")
    row_at = lax.axis_index("row")
    col_at = lax.axis_index("col")
    tensor_count = lax.axis_size("tensor")
    row_count = lax.axis_size("row")
    col_count = lax.axis_size("col")
    owners = tensor_count * row_count
    held = integral_tiles.shape[0]
    tile_size = integral_tiles.shape[2]
    owner = tile_index[:, 0] // AB * row_count + tile_index[:, 1] // MB
    earlier = jnp.arange(held)[:, None] > jnp.arange(held)[None, :]
    same_owner = owner[:, None] == owner[None, :]
    rank = jnp.sum(jnp.logical_and(earlier, same_owner), axis=1)
    position = owner * CAP + rank
    slots = owners * CAP
    send_tiles = jnp.zeros((slots, PB, tile_size), jnp.bfloat16).at[position].set(integral_tiles)
    send_index = jnp.full((slots, 3), -1, jnp.int32).at[position].set(tile_index)
    recv_tiles, recv_index = (
        lax.all_to_all(
            send_tiles.reshape(owners, CAP, PB, tile_size),
            ("tensor", "row"),
            split_axis=0,
            concat_axis=0,
            tiled=True,
        ),
        lax.all_to_all(
            send_index.reshape(owners, CAP, 3),
            ("tensor", "row"),
            split_axis=0,
            concat_axis=0,
            tiled=True,
        ),
    )
    recv_tiles = recv_tiles.reshape(slots, PB * tile_size)
    recv_index = recv_index.reshape(slots, 3)
    combos = AB * MB * NBC
    valid = recv_index[:, 0] >= 0
    local_aux = recv_index[:, 0] - tensor_at * AB
    local_mu = recv_index[:, 1] - row_at * MB
    local_nu = recv_index[:, 2] - col_at * NBC
    segment = jnp.where(valid, (local_aux * MB + local_mu) * NBC + local_nu, combos)
    selector = (jnp.arange(combos)[:, None] == segment[None, :]).astype(jnp.bfloat16)
    dense = jnp.dot(selector, recv_tiles, preferred_element_type=jnp.float32).astype(jnp.bfloat16)
    dense = dense.reshape(AB, MB, NBC, PB, TB, TB)
    virt_rows = virtual_coeff.shape[0]
    per_device = NV // (row_count * col_count)
    permuted = (
        virtual_coeff.reshape(virt_rows, row_count, col_count, per_device)
        .transpose(0, 2, 1, 3)
        .reshape(NBC, TB, NV)
    )
    half_rows = AB * MB * PB * TB
    product = jnp.einsum("knv,ajkpun->vajpu", permuted, dense, preferred_element_type=jnp.float32)
    half = lax.psum_scatter(
        product.reshape(NV // col_count * lax.axis_size("col"), half_rows).astype(jnp.bfloat16),
        "col",
        scatter_dimension=0,
        tiled=True,
    )
    occ_local = occupied_coeff.reshape(MB, TB, NOCC)
    picked = half.reshape(per_device * lax.axis_size("row"), AB, MB, PB, TB)
    product = jnp.einsum("vajpu,juo->vapo", picked, occ_local, preferred_element_type=jnp.float32)
    return lax.psum_scatter(
        product.reshape(per_device * lax.axis_size("row"), AB * PB, NOCC).astype(jnp.bfloat16),
        "row",
        scatter_dimension=0,
        tiled=True,
    )


def solution(mesh):
    in_specs = (
        P(("tensor", "row", "col"), None, None),
        P(("tensor", "row", "col"), None),
        P("col", None),
        P("row", None),
    )
    out_specs = P(("row", "col"), "tensor", None)
    return jax.shard_map(shards, mesh=mesh, in_specs=in_specs, out_specs=out_specs, check_vma=False)
```

profile of v0, /device:TPU:32, one launch (start us, length us, event | category | flops | bytes accessed | tf_op | source)
XLA Modules:
  0.0 326.9 jit_solution(9106468927834375563)
XLA Ops:
  6.5 0.0 copy-start
  6.5 0.0 copy-start.1
  6.5 0.9 fusion.18
  7.4 0.8 fusion.11
  8.2 0.8 copy.27
  8.9 0.2 convert_reduce_fusion
  9.1 0.8 fusion.10
  9.9 1.2 scatter_custom_fusion
  11.1 7.3 %all-to-all-start = ((s32[32,2,3]{2,1,0:T(2,128)}), s32[32,2,3]{2,1,0:T(2,128)S(1)}, u32[]{:S(2)}, u32[]{:S(2)}) async-start(s32[32,2,3]{2,1,0:T(2,128)} %bitcast.5), calls=%async_computation | async-start | bytes 65536 | tf_op jit(solution)/shard_map/all_to_all | solution.py:42
  18.5 2.4 broadcast_in_dim.10
  20.9 0.0 copy-done.1
  20.9 5.4 %scatter_fusion = bf16[64,8,4096]{2,1,0:T(8,128)(2,1)} fusion(bf16[64,8,4096]{2,1,0:T(8,128)(2,1)} %broadcast_in_dim.10, s32[32]{0:T(128)S(1)} %fusion.10, bf16[32,8,4096]{2,1,0:T(8,128)(2,1)S(1)} %copy-done.1), kind=kCustom, calls=%fused_computation.1 | custom fusion | bytes 6291584 | tf_op jit(solution)/shard_map/scatter | solution.py:32
  26.3 0.0 all-to-all-done
  26.3 7.5 %all-to-all-start.1 = ((bf16[32,2,8,4096]{3,2,1,0:T(8,128)(2,1)}), bf16[32,2,8,4096]{3,2,1,0:T(8,128)(2,1)}, u32[]{:S(2)}, u32[]{:S(2)}) async-start(bf16[32,2,8,4096]{3,2,1,0:T(8,128)(2,1)} %bitcast.74), calls=%async_computation.1 | async-start | bytes 8388608 | tf_op jit(solution)/shard_map/all_to_all | solution.py:35
  33.8 0.0 reduce-scatter.3.cloned.1.call-start
  33.9 6.4 %copy.31 = bf16[1024,2048]{0,1:T(8,128)(2,1)} copy(bf16[1024,2048]{1,0:T(8,128)(2,1)} %param.6) | data formatting | bytes 8388608 | tf_op args[2]
  40.3 5.0 %copy.32 = bf16[1024,8,16,16]{0,3,2,1:T(8,128)(2,1)} copy(bf16[1024,8,16,16]{0,3,1,2:T(8,128)(2,1)} %bitcast.76) | data formatting | bytes 8388608 | tf_op jit(solution)/shard_map/transpose | solution.py:65
  45.3 11.6 %reshape.133 = bf16[16,64,2048]{1,0,2:T(8,128)(2,1)} reshape(bf16[1024,8,16,16]{0,3,2,1:T(8,128)(2,1)} %copy.32) | data formatting | bytes 8388608 | tf_op jit(solution)/shard_map/reshape | solution.py:66
  56.9 0.1 fusion.13
  56.9 0.1 copy.45
  57.0 0.1 copy.44
  57.1 0.1 copy.46
  57.2 34.3 %all-to-all-done.1 = bf16[32,2,8,4096]{3,2,1,0:T(8,128)(2,1)} async-done(((bf16[32,2,8,4096]{3,2,1,0:T(8,128)(2,1)}), bf16[32,2,8,4096]{3,2,1,0:T(8,128)(2,1)}, u32[]{:S(2)}, u32[]{:S(2)}) %all-to-all-start.1) | async-done | bytes 4194336 | tf_op jit(solution)/shard_map/all_to_all | solution.py:35
  91.5 4.5 %copy.47 = bf16[8,8,8,4096]{3,1,2,0:T(8,128)(2,1)S(1)} copy(bf16[8,8,8,4096]{3,2,1,0:T(8,128)(2,1)} %bitcast.31) | data formatting | bytes 8388608
  96.0 3.2 convolution_convert_fusion
  99.2 11.4 %reshape.131 = bf16[2,2,16,8,64,64]{5,4,3,2,1,0:T(8,128)(2,1)} reshape(bf16[64,32768]{1,0:T(8,128)(2,1)} %convolution_convert_fusion) | data formatting | bytes 8388608 | tf_op jit(solution)/shard_map/reshape | solution.py:60
  110.6 23.9 %bitcast_convert_fusion = bf16[2,2,8,64,2048]{4,3,2,1,0:T(8,128)(2,1)} fusion(bf16[2,2,16,8,64,64]{5,4,3,2,1,0:T(8,128)(2,1)} %reshape.131, bf16[16,64,2048,1,1,1]{1,0,2,5,4,3:T(8,128)(2,1)} %bitcast.77), kind=kOutput, calls=%fused_computation.3 | convolution fusion | flops 8594128896 | bytes 16777216 | tf_op jit(solution)/shard_map/knv,ajkpun->vajpu/dot_general | solution.py:69
  134.5 0.0 reduce-scatter.3.cloned.1.call-update
  134.5 0.0 reduce-scatter.5.cloned.1.call-start
  134.6 95.8 %reduce-scatter.3.cloned.1.call-done = bf16[256,2048]{0,1:T(8,128)(2,1)} async-done(((bf16[2048,2048]{0,1:T(8,128)(2,1)}), bf16[256,2048]{0,1:T(8,128)(2,1)}) %reduce-scatter.3.cloned.1.call-update) | async-done | bytes 1048592 | tf_op jit(solution)/shard_map/reduce_scatter | solution.py:70
  230.4 1.3 copy.35
  231.7 0.0 copy-done
  231.7 3.2 bitcast_convert_fusion.1
  234.9 0.0 reduce-scatter.5.cloned.1.call-update
  235.0 83.2 %reduce-scatter.5.cloned.1.call-done = bf16[16,16,512]{2,0,1:T(8,128)(2,1)} async-done(((bf16[256,16,512]{2,0,1:T(8,128)(2,1)}), bf16[16,16,512]{2,0,1:T(8,128)(2,1)}) %reduce-scatter.5.cloned.1.call-update) | async-done | bytes 262160 | tf_op jit(solution)/shard_map/reduce_scatter | solution.py:79
  318.2 1.8 copy.36
  (1 shorter events, 0.0 us)
Async XLA Ops:
  6.5 225.2 %copy-start = (bf16[128,512]{1,0:T(8,128)(2,1)S(1)}, bf16[128,512]{1,0:T(8,128)(2,1)}, u32[]{:S(2)}) copy-start(bf16[128,512]{1,0:T(8,128)(2,1)} %param.7) | copy-start | bytes 393220
  6.5 14.4 %copy-start.1 = (bf16[32,8,4096]{2,1,0:T(8,128)(2,1)S(1)}, bf16[32,8,4096]{2,1,0:T(8,128)(2,1)}, u32[]{:S(2)}) copy-start(bf16[32,8,4096]{2,1,0:T(8,128)(2,1)} %param.4) | copy-start | bytes 6291460
  11.1 15.2 %all-to-all-start = ((s32[32,2,3]{2,1,0:T(2,128)}), s32[32,2,3]{2,1,0:T(2,128)S(1)}, u32[]{:S(2)}, u32[]{:S(2)}) async-start(s32[32,2,3]{2,1,0:T(2,128)} %bitcast.5), calls=%async_computation | async-start | bytes 65536 | tf_op jit(solution)/shard_map/all_to_all | solution.py:42
  26.3 65.1 %all-to-all-start.1 = ((bf16[32,2,8,4096]{3,2,1,0:T(8,128)(2,1)}), bf16[32,2,8,4096]{3,2,1,0:T(8,128)(2,1)}, u32[]{:S(2)}, u32[]{:S(2)}) async-start(bf16[32,2,8,4096]{3,2,1,0:T(8,128)(2,1)} %bitcast.74), calls=%async_computation.1 | async-start | bytes 8388608 | tf_op jit(solution)/shard_map/all_to_all | solution.py:35
  33.8 196.6 %reduce-scatter.3.cloned.1.call-start = ((), (), s32[]{:S(2)}) async-start(), calls=%async_computation.4 | async-start | bytes 9437184 | tf_op jit(solution)/shard_map/reduce_scatter | solution.py:70
  134.5 183.7 %reduce-scatter.5.cloned.1.call-start = ((), (), s32[]{:S(2)}) async-start(), calls=%async_computation.5 | async-start | bytes 4456448 | tf_op jit(solution)/shard_map/reduce_scatter | solution.py:79
Sparse Core Ops, SparseCore 0:
  134.7 95.7 reduce-scatter.2
  235.1 83.0 reduce-scatter.4
where the time goes:
time: 328 us; the launch traced here: 327 us
  waiting for transfers between devices  213 us (65%)
  local copies, waits for them, and re-layouts  52.2 us (16%)
  matrix products  30.3 us (9%)
  starting transfers between devices  14.9 us (5%)
  between operations  13.5 us (4%)
    reduce_scatter x1, waiting for transfers between devices, shards(): lax.psum_scatter(product.reshape(NV // col_count * lax.axis_size('col'),...  95.8 us
    reduce_scatter x1, waiting for transfers between devices, shards(): lax.psum_scatter(product.reshape(per_device * lax.axis_size('row'), AB *...  83.2 us
    all_to_all x1, waiting for transfers between devices, shards(): lax.all_to_all(send_tiles.reshape(owners, CAP, PB, tile_size), ('tensor',...  34.3 us
    dot_general x1, matrix products, shards(): jnp.einsum('knv,ajkpun->vajpu', permuted, dense, preferred_element_type=j...  23.9 us
    unnamed x10, local copies, waits for them, and re-layouts  11.9 us
    reshape x1, local copies, waits for them, and re-layouts, shards(): permuted = virtual_coeff.reshape(virt_rows, row_count, col_count, per_dev...  11.6 us
    reshape x1, local copies, waits for them, and re-layouts, shards(): dense = dense.reshape(AB, MB, NBC, PB, TB, TB)  11.4 us
    all_to_all x1, starting transfers between devices, shards(): lax.all_to_all(send_tiles.reshape(owners, CAP, PB, tile_size), ('tensor',...  7.49 us
  transfers between devices with their start and end apart: 4, of which 3 were waited for; matrix products, arithmetic and copies ran while one was open for 10% of the time, Pallas kernels for 0%

commit v1 on v0

v1 whole, which is shorter than its diff:
```python
import jax
import jax.numpy as jnp
from jax import lax
from jax.sharding import PartitionSpec as P

TB = 64
PB = 8
AB = 2
MB = 2
NBC = 16
CAP = 2
NV = 2048
NOCC = 512


def shards(integral_tiles, tile_index, virtual_coeff, occupied_coeff):
    tensor_at = lax.axis_index("tensor")
    row_at = lax.axis_index("row")
    col_at = lax.axis_index("col")
    tensor_count = lax.axis_size("tensor")
    row_count = lax.axis_size("row")
    col_count = lax.axis_size("col")
    held = integral_tiles.shape[0]
    aux_blocks = tensor_count * AB
    mu_blocks = row_count * MB
    quarters = tensor_count * 2
    qsize = TB // quarters
    assert row_count == 2 * PB and quarters * qsize == TB

    tiles = integral_tiles.reshape(held, PB, 2, tensor_count, qsize, TB)
    send = tiles.transpose(3, 1, 2, 0, 4, 5).reshape(tensor_count * row_count, held, qsize * TB)
    recv = lax.all_to_all(send, ("tensor", "row"), split_axis=0, concat_axis=0, tiled=True)
    recv = recv.reshape(tensor_count * row_count * held, qsize * TB)
    index = lax.all_gather(tile_index, ("tensor", "row"), axis=0, tiled=True)

    local_nu = index[:, 2] - col_at * NBC
    block = (index[:, 0] * NBC + local_nu) * mu_blocks + index[:, 1]
    blocks = aux_blocks * NBC * mu_blocks
    selector = (jnp.arange(blocks)[:, None] == block[None, :]).astype(jnp.bfloat16)
    dense = jnp.dot(selector, recv, preferred_element_type=jnp.float32).astype(jnp.bfloat16)
    dense = dense.reshape(aux_blocks, NBC, mu_blocks, qsize, TB)

    occ_all = lax.all_gather(occupied_coeff, "row", axis=0, tiled=True)
    quarter = 2 * (row_at % 2) + tensor_at
    occ_q = lax.dynamic_index_in_dim(
        occ_all.reshape(mu_blocks, quarters, qsize, NOCC), quarter, axis=1, keepdims=False
    )
    partial = jnp.einsum("anmuw,mui->anwi", dense, occ_q, preferred_element_type=jnp.float32)

    pair = lax.psum_scatter(partial.astype(jnp.bfloat16), "tensor", scatter_dimension=0, tiled=True)
    side = row_at % 2
    keep = lax.dynamic_index_in_dim(pair, side, axis=0, keepdims=False)
    give = lax.dynamic_index_in_dim(pair, 1 - side, axis=0, keepdims=False)
    got = lax.ppermute(give, "row", perm=[(i, i ^ 1) for i in range(row_count)])
    occ_done = (keep.astype(jnp.float32) + got.astype(jnp.float32)).astype(jnp.bfloat16)

    chunk = NV // (row_count * col_count)
    virt = virtual_coeff.reshape(NBC, TB, row_count, col_count, chunk)
    z = jnp.einsum("nwi,nwrcj->crji", occ_done, virt, preferred_element_type=jnp.float32)
    z = z.astype(jnp.bfloat16).reshape(col_count * row_count * chunk, NOCC)
    w = lax.psum_scatter(z, "col", scatter_dimension=0, tiled=True).reshape(row_count, chunk, NOCC)

    got_rows = lax.all_to_all(w, "row", split_axis=0, concat_axis=0, tiled=True)
    out = got_rows.reshape(PB, 2, chunk, NOCC).transpose(2, 1, 0, 3)
    return out.reshape(chunk, AB * PB, NOCC)


def solution(mesh):
    in_specs = (
        P(("tensor", "row", "col"), None, None),
        P(("tensor", "row", "col"), None),
        P("col", None),
        P("row", None),
    )
    out_specs = P(("row", "col"), "tensor", None)
    return jax.shard_map(shards, mesh=mesh, in_specs=in_specs, out_specs=out_specs, check_vma=False)
```

time: 328 us -> 266 us (0.81)
  waiting for transfers between devices: 213 us -> 66.4 us
  blocking collectives: 0 us -> 102 us
  matrix products: 30.3 us -> 21.8 us
  starting transfers between devices: 14.9 us -> 9.15 us
    reduce_scatter x2, waiting for transfers between devices: 179 us -> 59.9 us  [the longest x1 42.9 us: shards(): lax.psum_scatter(z, 'col', scatter_dimension=0, tiled=True)]
    all_gather x0 -> x1, blocking collectives: none -> 86.8 us  [shards(): index = lax.all_gather(tile_index, ('tensor', 'row'), axis=0, tiled=True)]
    all_to_all x2 -> x1, waiting for transfers between devices: 34.3 us -> 0.01 us  [shards(): lax.all_to_all(send, ('tensor', 'row'), split_axis=0, concat_axis=0, tile...]
    reshape x3 -> x5, local copies, waits for them, and re-layouts: 24.3 us -> 42.2 us  [the longest x2 12.3 us: shards(): tiles = integral_tiles.reshape(held, PB, 2, tensor_count, qsize, TB)]
    all_to_all x0 -> x1, blocking collectives: none -> 15.5 us  [shards(): got_rows = lax.all_to_all(w, 'row', split_axis=0, concat_axis=0, tiled=True)]
    dot_general x3, matrix products: 30.3 us -> 21.8 us  [the longest x1 7.97 us: shards(): jnp.einsum('nwi,nwrcj->crji', occ_done, virt, preferred_element_type=jnp....]
    all_to_all x2 -> x1, starting transfers between devices: 14.8 us -> 7.32 us  [shards(): lax.all_to_all(send, ('tensor', 'row'), split_axis=0, concat_axis=0, tile...]
    scatter x2 -> x0, local copies, waits for them, and re-layouts: 6.67 us -> none  [the longest x1 5.43 us: shards(): jnp.zeros((slots, PB, tile_size), jnp.bfloat16).at[position]]
  transfers between devices with their start and end apart: 4 -> 5, of which waited for: 3 -> 3; matrix products, arithmetic and copies ran while one was open for 10% -> 21% of each run, Pallas kernels for 0% -> 0%
where the time goes in v1:
time: 266 us; the launch traced here: 265 us
  blocking collectives  102 us (38%)
  waiting for transfers between devices  66.4 us (25%)
  local copies, waits for them, and re-layouts  52.3 us (20%)
  matrix products  21.8 us (8%)
  between operations  13.2 us (5%)
  starting transfers between devices  9.15 us (3%)
    all_gather x1, blocking collectives, shards(): index = lax.all_gather(tile_index, ('tensor', 'row'), axis=0, tiled=True)  86.8 us
    reduce_scatter x1, waiting for transfers between devices, shards(): lax.psum_scatter(z, 'col', scatter_dimension=0, tiled=True)  42.9 us
    reduce_scatter x1, waiting for transfers between devices, shards(): lax.psum_scatter(partial.astype(jnp.bfloat16), 'tensor', scatter_dimensio...  17 us
    all_to_all x1, blocking collectives, shards(): got_rows = lax.all_to_all(w, 'row', split_axis=0, concat_axis=0, tiled=True)  15.5 us
    reshape x2, local copies, waits for them, and re-layouts, shards(): tiles = integral_tiles.reshape(held, PB, 2, tensor_count, qsize, TB)  12.3 us
    reshape x1, local copies, waits for them, and re-layouts, shards(): virt = virtual_coeff.reshape(NBC, TB, row_count, col_count, chunk)  11.8 us
    reshape x1, local copies, waits for them, and re-layouts, shards(): dense = dense.reshape(aux_blocks, NBC, mu_blocks, qsize, TB)  11.6 us
    dot_general x1, matrix products, shards(): jnp.einsum('nwi,nwrcj->crji', occ_done, virt, preferred_element_type=jnp....  7.97 us
  transfers between devices with their start and end apart: 5, of which 3 were waited for; matrix products, arithmetic and copies ran while one was open for 21% of the time, Pallas kernels for 0%

profile of v1, /device:TPU:32, one launch (start us, length us, event | category | flops | bytes accessed | tf_op | source)
XLA Modules:
  0.0 265.2 jit_solution(8073186442823905420)
XLA Ops:
  6.5 0.0 all-gather.3.cloned.1.call-start
  6.5 0.7 all-gather.3.cloned.1.call-update
  7.3 6.9 %reshape.57 = bf16[32,8,2,2,16,64]{5,4,3,2,1,0:T(8,128)(2,1)} reshape(bf16[32,8,4096]{2,1,0:T(8,128)(2,1)} %param.4) | data formatting | bytes 4194304 | tf_op jit(solution)/shard_map/reshape | solution.py:30
  14.2 5.3 %copy.42 = bf16[32,8,2,2,16,64]{5,4,0,2,1,3:T(8,128)(2,1)} copy(bf16[32,8,2,2,16,64]{5,4,3,2,1,0:T(8,128)(2,1)} %reshape.57) | data formatting | bytes 4194304 | tf_op jit(solution)/shard_map/reshape | solution.py:30
  19.5 0.0 copy-start.1
  19.5 6.5 %reshape.58 = bf16[32,32,1024]{2,1,0:T(8,128)(2,1)} reshape(bf16[2,8,2,32,16,64]{5,4,3,2,1,0:T(8,128)(2,1)} %bitcast.55) | data formatting | bytes 4194304 | tf_op jit(solution)/shard_map/reshape | solution.py:31
  26.0 7.3 %all-to-all-start = ((bf16[32,32,1024]{2,1,0:T(8,128)(2,1)}), bf16[32,32,1024]{2,1,0:T(8,128)(2,1)S(1)}, u32[]{:S(2)}, u32[]{:S(2)}) async-start(bf16[32,32,1024]{2,1,0:T(8,128)(2,1)} %reshape.58), calls=%async_computation | async-start | bytes 4194304 | tf_op jit(solution)/shard_map/all_to_all | solution.py:32
  33.4 0.0 reduce-scatter.3.cloned.1.call-start
  33.4 0.0 copy-done.1
  33.5 86.8 %all-gather = s32[32,32,3]{1,2,0:T(4,128)S(1)} all-gather(s32[1,32,3]{1,2,0:T(4,128)S(1)} %bitcast.62), channel_id=1, replica_groups=mesh['tensor'=2,'row'=16,'col'=8] {'tensor','row'}, dimensions={0}, use_global_device_ids=true | all-gather | bytes 12672 | tf_op jit(solution)/shard_map/all_gather | solution.py:34
  120.3 0.1 reshape.69
  120.4 0.0 all-to-all-done
  120.4 6.0 %fusion.4 = bf16[2048,1024]{1,0:T(8,128)(2,1)} fusion(bf16[1024,1024]{1,0:T(8,128)(2,1)S(1)} %bitcast.57, s32[1024]{0:T(1024)S(1)} %bitcast.61), kind=kOutput, calls=%fused_computation.8 | convolution fusion | flops 4299161600 | bytes 6295552 | tf_op jit(solution)/shard_map/dot_general | solution.py:40
  126.4 11.6 %reshape.60 = bf16[4,16,32,16,64]{4,3,2,1,0:T(8,128)(2,1)} reshape(bf16[2048,1024]{1,0:T(8,128)(2,1)} %fusion.4) | data formatting | bytes 8388608 | tf_op jit(solution)/shard_map/reshape | solution.py:41
  138.0 0.0 all-gather.3.cloned.1.call-done
  138.0 7.8 %bitcast_convert_fusion = bf16[4,16,64,512]{3,2,1,0:T(8,128)(2,1)} fusion(bf16[4,16,32,16,64]{4,3,2,1,0:T(8,128)(2,1)} %reshape.60, bf16[32,4,16,512]{3,2,1,0:T(8,128)(2,1)} %bitcast.60, s32[]{:T(128)S(6)} %select_n.21), kind=kOutput, calls=%fused_computation | convolution fusion | flops 2149580800 | bytes 13107204 | tf_op jit(solution)/shard_map/anmuw,mui->anwi/dot_general | solution.py:48
  145.8 0.0 reduce-scatter.3.cloned.1.call-update
  145.8 0.0 reduce-scatter.5.cloned.1.call-start
  145.9 17.0 %reduce-scatter.3.cloned.1.call-done = bf16[2,16,64,512]{3,2,1,0:T(8,128)(2,1)} async-done(((bf16[4,16,64,512]{3,2,1,0:T(8,128)(2,1)}), bf16[2,16,64,512]{3,2,1,0:T(8,128)(2,1)}) %reduce-scatter.3.cloned.1.call-update) | async-done | bytes 2097168 | tf_op jit(solution)/shard_map/reduce_scatter | solution.py:50
  162.9 1.3 dynamic-slice_bitcast_fusion
  164.2 1.7 collective-permute-start
  165.9 6.4 %copy.25 = bf16[1024,2048]{0,1:T(8,128)(2,1)} copy(bf16[1024,2048]{1,0:T(8,128)(2,1)} %param.6) | data formatting | bytes 8388608 | tf_op args[2]
  172.3 0.0 copy-start
  172.3 11.8 %reshape.62 = bf16[16,64,16,8,16]{1,0,4,3,2:T(8,128)(2,1)} reshape(bf16[1024,2048]{0,1:T(8,128)(2,1)} %copy.25) | data formatting | bytes 8388608 | tf_op jit(solution)/shard_map/reshape | solution.py:58
  184.1 5.8 %collective-permute-done = bf16[16,64,512]{2,1,0:T(8,128)(2,1)} collective-permute-done((bf16[16,64,512]{2,1,0:T(8,128)(2,1)S(1)}, bf16[16,64,512]{2,1,0:T(8,128)(2,1)}, u32[]{:S(2)}, u32[]{:S(2)}) %collective-permute-start) | collective-permute-done | bytes 1048608 | tf_op jit(solution)/shard_map/ppermute | solution.py:54
  189.8 0.0 copy-done
  189.8 8.0 %fusion.8 = bf16[8,16,16,512]{3,2,0,1:T(8,128)(2,1)S(1)} fusion(bf16[16,64,16,8,16]{1,0,4,3,2:T(8,128)(2,1)} %reshape.62, bf16[16,64,512]{2,1,0:T(8,128)(2,1)} %collective-permute-done, bf16[2,16,64,512]{3,2,1,0:T(8,128)(2,1)S(1)} %copy-done, s32[]{:T(128)S(6)} %select_n.22), kind=kOutput, calls=%fused_computation.11 | convolution fusion | flops 2150629376 | bytes 8388612 | tf_op jit(solution)/shard_map/nwi,nwrcj->crji/dot_general | solution.py:59
  197.8 1.5 copy.27
  199.3 0.0 reduce-scatter.5.cloned.1.call-update
  199.4 42.9 %reduce-scatter.5.cloned.1.call-done = bf16[256,512]{1,0:T(8,128)(2,1)} async-done(((bf16[2048,512]{1,0:T(8,128)(2,1)}), bf16[256,512]{1,0:T(8,128)(2,1)}) %reduce-scatter.5.cloned.1.call-update) | async-done | bytes 262160 | tf_op jit(solution)/shard_map/reduce_scatter | solution.py:61
  242.3 15.5 %all_to_all.10 = bf16[16,16,512]{2,1,0:T(8,128)(2,1)S(1)} all-to-all(bf16[16,16,512]{2,1,0:T(8,128)(2,1)} %bitcast.59), channel_id=1, replica_groups=mesh['tensor'=2,'row'=16,'col'=8] {'row'}, dimensions={0} | all-to-all | bytes 524288 | tf_op jit(solution)/shard_map/all_to_all | solution.py:63
  257.8 0.9 copy.43
  (2 shorter events, 0.0 us)
Async XLA Ops:
  6.5 131.5 %all-gather.3.cloned.1.call-start = ((), (), s32[]{:S(2)}) async-start(), calls=%async_computation.4 | async-start | bytes 2228224 | tf_op jit(solution)/shard_map/all_gather | solution.py:43
  19.5 13.9 %copy-start.1 = (s32[32,3]{0,1:T(4,128)S(1)}, s32[32,3]{0,1:T(4,128)}, u32[]{:S(2)}) copy-start(s32[32,3]{0,1:T(4,128)} %param.5) | copy-start | bytes 1156
  26.0 94.3 %all-to-all-start = ((bf16[32,32,1024]{2,1,0:T(8,128)(2,1)}), bf16[32,32,1024]{2,1,0:T(8,128)(2,1)S(1)}, u32[]{:S(2)}, u32[]{:S(2)}) async-start(bf16[32,32,1024]{2,1,0:T(8,128)(2,1)} %reshape.58), calls=%async_computation | async-start | bytes 4194304 | tf_op jit(solution)/shard_map/all_to_all | solution.py:32
  33.4 129.5 %reduce-scatter.3.cloned.1.call-start = ((), (), s32[]{:S(2)}) async-start(), calls=%async_computation.5 | async-start | bytes 6291456 | tf_op jit(solution)/shard_map/reduce_scatter | solution.py:50
  145.8 96.5 %reduce-scatter.5.cloned.1.call-start = ((), (), s32[]{:S(2)}) async-start(), calls=%async_computation.6 | async-start | bytes 2359296 | tf_op jit(solution)/shard_map/reduce_scatter | solution.py:61
  164.2 25.6 %collective-permute-start = (bf16[16,64,512]{2,1,0:T(8,128)(2,1)S(1)}, bf16[16,64,512]{2,1,0:T(8,128)(2,1)}, u32[]{:S(2)}, u32[]{:S(2)}) collective-permute-start(bf16[16,64,512]{2,1,0:T(8,128)(2,1)S(1)} %dynamic-slice_bitcast_fusion), channel_id=1, source_target_pairs={{0,8},{8,0},{16,24},{24,16},{32,40},{40,32},{48,56},{56,48},{64,72... | collective-permute-start | bytes 3145736 | tf_op jit(solution)/shard_map/ppermute | solution.py:54
  172.3 17.5 %copy-start = (bf16[2,16,64,512]{3,2,1,0:T(8,128)(2,1)S(1)}, bf16[2,16,64,512]{3,2,1,0:T(8,128)(2,1)}, u32[]{:S(2)}) copy-start(bf16[2,16,64,512]{3,2,1,0:T(8,128)(2,1)} %reduce-scatter.3.cloned.1.call-done) | copy-start | bytes 6291460
Sparse Core Ops, SparseCore 0:
  9.8 63.4 all-gather.2
  145.9 16.8 reduce-scatter.2
  199.5 42.7 reduce-scatter.4

commit v2 on v1

--- a/solution.py
+++ b/solution.py
@@ -27,14 +27,15 @@
     qsize = TB // quarters
     assert row_count == 2 * PB and quarters * qsize == TB
 
-    tiles = integral_tiles.reshape(held, PB, 2, tensor_count, qsize, TB)
-    send = tiles.transpose(3, 1, 2, 0, 4, 5).reshape(tensor_count * row_count, held, qsize * TB)
-    recv = lax.all_to_all(send, ("tensor", "row"), split_axis=0, concat_axis=0, tiled=True)
+    owners = ("row", "tensor")
+    send = integral_tiles.reshape(held, row_count * tensor_count, qsize * TB).transpose(1, 0, 2)
+    recv = lax.all_to_all(send, owners, split_axis=0, concat_axis=0, tiled=True)
     recv = recv.reshape(tensor_count * row_count * held, qsize * TB)
-    index = lax.all_gather(tile_index, ("tensor", "row"), axis=0, tiled=True)
 
-    local_nu = index[:, 2] - col_at * NBC
-    block = (index[:, 0] * NBC + local_nu) * mu_blocks + index[:, 1]
+    local_nu = tile_index[:, 2] - col_at * NBC
+    own_block = (tile_index[:, 0] * NBC + local_nu) * mu_blocks + tile_index[:, 1]
+    send_block = jnp.broadcast_to(own_block[None, :], (row_count * tensor_count, held))
+    block = lax.all_to_all(send_block, owners, split_axis=0, concat_axis=0, tiled=True).reshape(-1)
     blocks = aux_blocks * NBC * mu_blocks
     selector = (jnp.arange(blocks)[:, None] == block[None, :]).astype(jnp.bfloat16)
     dense = jnp.dot(selector, recv, preferred_element_type=jnp.float32).astype(jnp.bfloat16)
@@ -55,9 +56,10 @@
     occ_done = (keep.astype(jnp.float32) + got.astype(jnp.float32)).astype(jnp.bfloat16)
 
     chunk = NV // (row_count * col_count)
-    virt = virtual_coeff.reshape(NBC, TB, row_count, col_count, chunk)
-    z = jnp.einsum("nwi,nwrcj->crji", occ_done, virt, preferred_element_type=jnp.float32)
-    z = z.astype(jnp.bfloat16).reshape(col_count * row_count * chunk, NOCC)
+    virt = virtual_coeff.reshape(NBC, TB, NV)
+    z = jnp.einsum("nwi,nwv->vi", occ_done, virt, preferred_element_type=jnp.float32).astype(jnp.bfloat16)
+    z = z.reshape(row_count, col_count, chunk, NOCC).transpose(1, 0, 2, 3)
+    z = z.reshape(col_count * row_count * chunk, NOCC)
     w = lax.psum_scatter(z, "col", scatter_dimension=0, tiled=True).reshape(row_count, chunk, NOCC)
 
     got_rows = lax.all_to_all(w, "row", split_axis=0, concat_axis=0, tiled=True)

time: 266 us -> 205 us (0.77)
  blocking collectives: 102 us -> 15.5 us
  waiting for transfers between devices: 66.4 us -> 114 us
  local copies, waits for them, and re-layouts: 52.3 us -> 25.2 us
  starting transfers between devices: 9.15 us -> 14.7 us
    all_gather x1 -> x0, blocking collectives: 86.8 us -> none  [shards(): index = lax.all_gather(tile_index, ('tensor', 'row'), axis=0, tiled=True)]
    all_to_all x1 -> x2, waiting for transfers between devices: 0.01 us -> 29.9 us  [the longest x1 28.3 us: shards(): recv = lax.all_to_all(send, owners, split_axis=0, concat_axis=0, tiled=True)]
    reshape x4 -> x1, local copies, waits for them, and re-layouts: 30.6 us -> 3.1 us  [shards(): integral_tiles.reshape(held, row_count * tensor_count, qsize * TB)]
    ppermute x1, waiting for transfers between devices: 5.76 us -> 23.9 us  [shards(): got = lax.ppermute(give, 'row', perm=[(i, i ^ 1) for i in range(row_count)])]
    unnamed x6 -> x2, local copies, waits for them, and re-layouts: 6.47 us -> 0.01 us
    all_to_all x1 -> x2, starting transfers between devices: 7.32 us -> 13 us  [the longest x1 7.32 us: shards(): lax.all_to_all(send_block, owners, split_axis=0, concat_axis=0, tiled=True)]
    transpose x0 -> x2, local copies, waits for them, and re-layouts: none -> 4.1 us  [the longest x1 2.51 us: shards(): integral_tiles.reshape(held, row_count * tensor_count, qsize * TB)]
  transfers between devices with their start and end apart: 5 -> 6, of which waited for: 3 -> 5; matrix products, arithmetic and copies ran while one was open for 21% -> 13% of each run, Pallas kernels for 0% -> 0%
where the time goes in v2:
time: 205 us; the launch traced here: 204 us
  waiting for transfers between devices  114 us (56%)
  local copies, waits for them, and re-layouts  25.2 us (12%)
  matrix products  20.1 us (10%)
  blocking collectives  15.5 us (8%)
  starting transfers between devices  14.7 us (7%)
  between operations  13.2 us (6%)
    reduce_scatter x1, waiting for transfers between devices, shards(): lax.psum_scatter(z, 'col', scatter_dimension=0, tiled=True)  43.1 us
    all_to_all x1, waiting for transfers between devices, shards(): recv = lax.all_to_all(send, owners, split_axis=0, concat_axis=0, tiled=True)  28.3 us
    ppermute x1, waiting for transfers between devices, shards(): got = lax.ppermute(give, 'row', perm=[(i, i ^ 1) for i in range(row_count)])  23.9 us
    reduce_scatter x1, waiting for transfers between devices, shards(): lax.psum_scatter(partial.astype(jnp.bfloat16), 'tensor', scatter_dimensio...  16.2 us
    all_to_all x1, blocking collectives, shards(): got_rows = lax.all_to_all(w, 'row', split_axis=0, concat_axis=0, tiled=True)  15.5 us
    reshape x1, local copies, waits for them, and re-layouts, shards(): dense = dense.reshape(aux_blocks, NBC, mu_blocks, qsize, TB)  11.7 us
    dot_general x1, matrix products, shards(): jnp.einsum('anmuw,mui->anwi', dense, occ_q, preferred_element_type=jnp.fl...  7.78 us
    all_to_all x1, starting transfers between devices, shards(): lax.all_to_all(send_block, owners, split_axis=0, concat_axis=0, tiled=True)  7.32 us
  transfers between devices with their start and end apart: 6, of which 5 were waited for; matrix products, arithmetic and copies ran while one was open for 13% of the time, Pallas kernels for 0%

profile of v2, /device:TPU:32, one launch (start us, length us, event | category | flops | bytes accessed | tf_op | source)
XLA Modules:
  0.0 203.9 jit_solution(8251943030286406106)
XLA Ops:
  6.5 0.0 all-gather.2.cloned.1.call-start
  6.5 0.7 all-gather.2.cloned.1.call-update
  7.3 0.8 add_bitcast_fusion
  8.1 0.6 broadcast_in_dim.2
  8.7 7.3 %all-to-all-start = ((s32[32,1,32]{2,1,0:T(1,128)}), s32[32,1,32]{2,1,0:T(1,128)S(1)}, u32[]{:S(2)}, u32[]{:S(2)}) async-start(s32[32,1,32]{2,1,0:T(1,128)} %broadcast_in_dim.2), calls=%async_computation | async-start | bytes 32768 | tf_op jit(solution)/shard_map/all_to_all | solution.py:38
  16.0 3.1 %reshape.65 = bf16[32,32,1024]{2,1,0:T(8,128)(2,1)S(1)} reshape(bf16[32,8,4096]{2,1,0:T(8,128)(2,1)} %param.4) | data formatting | bytes 4194304 | tf_op jit(solution)/shard_map/reshape | solution.py:31
  19.1 2.5 %copy.16 = bf16[32,32,1024]{2,1,0:T(8,128)(2,1)} copy(bf16[32,32,1024]{2,0,1:T(8,128)(2,1)S(1)} %bitcast.48) | data formatting | bytes 4194304 | tf_op jit(solution)/shard_map/transpose | solution.py:31
  21.6 1.7 all-to-all-done
  23.3 5.7 %all-to-all-start.1 = ((bf16[32,32,1024]{2,1,0:T(8,128)(2,1)}), bf16[32,32,1024]{2,1,0:T(8,128)(2,1)S(1)}, u32[]{:S(2)}, u32[]{:S(2)}) async-start(bf16[32,32,1024]{2,1,0:T(8,128)(2,1)} %copy.16), calls=%async_computation.1 | async-start | bytes 4194304 | tf_op jit(solution)/shard_map/all_to_all | solution.py:32
  29.0 0.0 reduce-scatter.3.cloned.1.call-start
  29.1 0.5 broadcast.26
  29.6 0.7 reduce.3
  30.3 0.1 eq.19
  30.4 28.3 %all-to-all-done.1 = bf16[32,32,1024]{2,1,0:T(8,128)(2,1)S(1)} async-done(((bf16[32,32,1024]{2,1,0:T(8,128)(2,1)}), bf16[32,32,1024]{2,1,0:T(8,128)(2,1)S(1)}, u32[]{:S(2)}, u32[]{:S(2)}) %all-to-all-start.1) | async-done | bytes 2097184 | tf_op jit(solution)/shard_map/all_to_all | solution.py:32
  58.6 6.0 %fusion.2 = bf16[2048,1024]{1,0:T(8,128)(2,1)} fusion(bf16[1024,1024]{1,0:T(8,128)(2,1)S(1)} %bitcast.49, s32[1024]{0:T(1024)S(1)} %eq.19), kind=kOutput, calls=%fused_computation.5 | convolution fusion | flops 4299161600 | bytes 6295552 | tf_op jit(solution)/shard_map/dot_general | solution.py:41
  64.7 11.7 %reshape.67 = bf16[4,16,32,16,64]{4,3,2,1,0:T(8,128)(2,1)} reshape(bf16[2048,1024]{1,0:T(8,128)(2,1)} %fusion.2) | data formatting | bytes 8388608 | tf_op jit(solution)/shard_map/reshape | solution.py:42
  76.3 0.0 all-gather.2.cloned.1.call-done
  76.3 7.8 %bitcast_convert_fusion = bf16[4,16,64,512]{3,2,1,0:T(8,128)(2,1)} fusion(bf16[4,16,32,16,64]{4,3,2,1,0:T(8,128)(2,1)} %reshape.67, bf16[32,4,16,512]{3,2,1,0:T(8,128)(2,1)} %bitcast.52, s32[]{:T(128)S(6)} %select_n.21), kind=kOutput, calls=%fused_computation | convolution fusion | flops 2149580800 | bytes 13107204 | tf_op jit(solution)/shard_map/anmuw,mui->anwi/dot_general | solution.py:49
  84.1 0.0 reduce-scatter.3.cloned.1.call-update
  84.1 0.0 reduce-scatter.5.cloned.1.call-start
  84.2 16.2 %reduce-scatter.3.cloned.1.call-done = bf16[2,16,64,512]{3,2,1,0:T(8,128)(2,1)} async-done(((bf16[4,16,64,512]{3,2,1,0:T(8,128)(2,1)}), bf16[2,16,64,512]{3,2,1,0:T(8,128)(2,1)}) %reduce-scatter.3.cloned.1.call-update) | async-done | bytes 2097168 | tf_op jit(solution)/shard_map/reduce_scatter | solution.py:51
  100.3 0.0 copy-start
  100.3 1.5 dynamic-slice_bitcast_fusion
  101.8 1.6 collective-permute-start
  103.4 23.9 %collective-permute-done = bf16[16,64,512]{2,1,0:T(8,128)(2,1)} collective-permute-done((bf16[16,64,512]{2,1,0:T(8,128)(2,1)S(1)}, bf16[16,64,512]{2,1,0:T(8,128)(2,1)}, u32[]{:S(2)}, u32[]{:S(2)}) %collective-permute-start) | collective-permute-done | bytes 1048608 | tf_op jit(solution)/shard_map/ppermute | solution.py:55
  127.3 0.0 copy-done
  127.3 6.3 %fusion.3 = bf16[2048,512]{0,1:T(8,128)(2,1)} fusion(bf16[16,64,2048]{2,1,0:T(8,128)(2,1)} %bitcast.53, bf16[16,64,512]{2,1,0:T(8,128)(2,1)} %collective-permute-done, bf16[2,16,64,512]{3,2,1,0:T(8,128)(2,1)S(1)} %copy-done, s32[]{:T(128)S(6)} %select_n.22), kind=kOutput, calls=%fused_computation.6 | convolution fusion | flops 2150629376 | bytes 8388612 | tf_op jit(solution)/shard_map/nwi,nwv->vi/dot_general | solution.py:60
  133.5 2.9 %copy.18 = bf16[2048,512]{1,0:T(8,128)(2,1)S(1)} copy(bf16[2048,512]{0,1:T(8,128)(2,1)} %fusion.3) | data formatting | bytes 4194304 | tf_op jit(solution)/shard_map/convert_element_type | solution.py:60
  136.4 1.6 copy.19
  138.0 0.0 reduce-scatter.5.cloned.1.call-update
  138.0 43.1 %reduce-scatter.5.cloned.1.call-done = bf16[256,512]{1,0:T(8,128)(2,1)} async-done(((bf16[2048,512]{1,0:T(8,128)(2,1)}), bf16[256,512]{1,0:T(8,128)(2,1)}) %reduce-scatter.5.cloned.1.call-update) | async-done | bytes 262160 | tf_op jit(solution)/shard_map/reduce_scatter | solution.py:63
  181.1 15.5 %all_to_all.16 = bf16[16,16,512]{2,1,0:T(8,128)(2,1)S(1)} all-to-all(bf16[16,16,512]{2,1,0:T(8,128)(2,1)} %bitcast.51), channel_id=1, replica_groups=mesh['tensor'=2,'row'=16,'col'=8] {'row'}, dimensions={0} | all-to-all | bytes 524288 | tf_op jit(solution)/shard_map/all_to_all | solution.py:65
  196.6 0.9 copy.25
Async XLA Ops:
  6.5 69.8 %all-gather.2.cloned.1.call-start = ((), (), s32[]{:S(2)}) async-start(), calls=%async_computation.5 | async-start | bytes 2228224 | tf_op jit(solution)/shard_map/all_gather | solution.py:44
  8.7 14.6 %all-to-all-start = ((s32[32,1,32]{2,1,0:T(1,128)}), s32[32,1,32]{2,1,0:T(1,128)S(1)}, u32[]{:S(2)}, u32[]{:S(2)}) async-start(s32[32,1,32]{2,1,0:T(1,128)} %broadcast_in_dim.2), calls=%async_computation | async-start | bytes 32768 | tf_op jit(solution)/shard_map/all_to_all | solution.py:38
  23.3 35.3 %all-to-all-start.1 = ((bf16[32,32,1024]{2,1,0:T(8,128)(2,1)}), bf16[32,32,1024]{2,1,0:T(8,128)(2,1)S(1)}, u32[]{:S(2)}, u32[]{:S(2)}) async-start(bf16[32,32,1024]{2,1,0:T(8,128)(2,1)} %copy.16), calls=%async_computation.1 | async-start | bytes 4194304 | tf_op jit(solution)/shard_map/all_to_all | solution.py:32
  29.0 71.3 %reduce-scatter.3.cloned.1.call-start = ((), (), s32[]{:S(2)}) async-start(), calls=%async_computation.6 | async-start | bytes 6291456 | tf_op jit(solution)/shard_map/reduce_scatter | solution.py:51
  84.1 97.0 %reduce-scatter.5.cloned.1.call-start = ((), (), s32[]{:S(2)}) async-start(), calls=%async_computation.7 | async-start | bytes 2359296 | tf_op jit(solution)/shard_map/reduce_scatter | solution.py:63
  100.3 26.9 %copy-start = (bf16[2,16,64,512]{3,2,1,0:T(8,128)(2,1)S(1)}, bf16[2,16,64,512]{3,2,1,0:T(8,128)(2,1)}, u32[]{:S(2)}) copy-start(bf16[2,16,64,512]{3,2,1,0:T(8,128)(2,1)} %reduce-scatter.3.cloned.1.call-done) | copy-start | bytes 6291460
  101.8 25.5 %collective-permute-start = (bf16[16,64,512]{2,1,0:T(8,128)(2,1)S(1)}, bf16[16,64,512]{2,1,0:T(8,128)(2,1)}, u32[]{:S(2)}, u32[]{:S(2)}) collective-permute-start(bf16[16,64,512]{2,1,0:T(8,128)(2,1)S(1)} %dynamic-slice_bitcast_fusion), channel_id=1, source_target_pairs={{0,8},{8,0},{16,24},{24,16},{32,40},{40,32},{48,56},{56,48},{64,72... | collective-permute-start | bytes 3145736 | tf_op jit(solution)/shard_map/ppermute | solution.py:55
Sparse Core Ops, SparseCore 0:
  9.8 63.4 all-gather.1
  84.2 16.0 reduce-scatter.2
  138.1 42.8 reduce-scatter.4

commit v3 on v2

--- a/solution.py
+++ b/solution.py
@@ -28,25 +28,32 @@
     assert row_count == 2 * PB and quarters * qsize == TB
 
     owners = ("row", "tensor")
-    send = integral_tiles.reshape(held, row_count * tensor_count, qsize * TB).transpose(1, 0, 2)
+    dests = row_count * tensor_count
+    lanes = qsize * TB
+    send = integral_tiles.reshape(held, dests, lanes).transpose(1, 0, 2)
+    local_index = jnp.stack(
+        [tile_index[:, 0], tile_index[:, 1], tile_index[:, 2] - col_at * NBC], axis=1
+    ).astype(jnp.bfloat16).reshape(1, 1, held * 3)
+    index_row = jnp.pad(local_index, ((0, 0), (0, 0), (0, lanes - held * 3)))
+    send = jnp.concatenate([send, jnp.broadcast_to(index_row, (dests, 1, lanes))], axis=1)
     recv = lax.all_to_all(send, owners, split_axis=0, concat_axis=0, tiled=True)
-    recv = recv.reshape(tensor_count * row_count * held, qsize * TB)
+    slices = recv[:, :held, :].reshape(dests * held, lanes)
+    index = recv[:, held, : held * 3].astype(jnp.int32).reshape(dests * held, 3)
 
-    local_nu = tile_index[:, 2] - col_at * NBC
-    own_block = (tile_index[:, 0] * NBC + local_nu) * mu_blocks + tile_index[:, 1]
-    send_block = jnp.broadcast_to(own_block[None, :], (row_count * tensor_count, held))
-    block = lax.all_to_all(send_block, owners, split_axis=0, concat_axis=0, tiled=True).reshape(-1)
+    block = (index[:, 0] * NBC + index[:, 2]) * mu_blocks + index[:, 1]
     blocks = aux_blocks * NBC * mu_blocks
     selector = (jnp.arange(blocks)[:, None] == block[None, :]).astype(jnp.bfloat16)
-    dense = jnp.dot(selector, recv, preferred_element_type=jnp.float32).astype(jnp.bfloat16)
-    dense = dense.reshape(aux_blocks, NBC, mu_blocks, qsize, TB)
+    dense = jnp.dot(selector, slices, preferred_element_type=jnp.float32).astype(jnp.bfloat16)
+    dense = dense.reshape(aux_blocks * NBC, mu_blocks, qsize, TB).transpose(0, 3, 1, 2)
+    dense = dense.reshape(aux_blocks * NBC, TB, mu_blocks * qsize)
 
-    occ_all = lax.all_gather(occupied_coeff, "row", axis=0, tiled=True)
-    quarter = 2 * (row_at % 2) + tensor_at
-    occ_q = lax.dynamic_index_in_dim(
-        occ_all.reshape(mu_blocks, quarters, qsize, NOCC), quarter, axis=1, keepdims=False
-    )
-    partial = jnp.einsum("anmuw,mui->anwi", dense, occ_q, preferred_element_type=jnp.float32)
+    occ_local = occupied_coeff.reshape(MB, 2, tensor_count, qsize, NOCC)
+    occ_local = lax.dynamic_index_in_dim(occ_local, tensor_at, axis=2, keepdims=False)
+    occ_half = lax.all_gather(occ_local, "row", axis=0, tiled=True)
+    occ_q = lax.dynamic_index_in_dim(occ_half, row_at % 2, axis=1, keepdims=False)
+    occ_q = occ_q.reshape(mu_blocks * qsize, NOCC)
+    partial = jnp.einsum("bwk,ki->bwi", dense, occ_q, preferred_element_type=jnp.float32)
+    partial = partial.reshape(aux_blocks, NBC, TB, NOCC)
 
     pair = lax.psum_scatter(partial.astype(jnp.bfloat16), "tensor", scatter_dimension=0, tiled=True)
     side = row_at % 2

time: 205 us -> 232 us (1.13)
  waiting for transfers between devices: 114 us -> 144 us
  starting transfers between devices: 14.7 us -> 9.19 us
  local copies, waits for them, and re-layouts: 25.2 us -> 27.6 us
    all_gather x1, waiting for transfers between devices: 0.01 us -> 60 us  [shards(): occ_half = lax.all_gather(occ_local, 'row', axis=0, tiled=True)]
    all_to_all x1, waiting for transfers between devices: 28.3 us -> 0.01 us  [shards(): recv = lax.all_to_all(send, owners, split_axis=0, concat_axis=0, tiled=True)]
    all_to_all x1 -> x0, starting transfers between devices: 7.32 us -> none  [shards(): lax.all_to_all(send_block, owners, split_axis=0, concat_axis=0, tiled=True)]
    concatenate x0 -> x1, local copies, waits for them, and re-layouts: none -> 2.74 us  [shards(): jnp.concatenate([send, jnp.broadcast_to(index_row, (dests, 1, lanes))], a...]
    transpose x1 -> x0, local copies, waits for them, and re-layouts: 2.51 us -> none  [shards(): integral_tiles.reshape(held, row_count * tensor_count, qsize * TB)]
  transfers between devices with their start and end apart: 6 -> 5, of which waited for: 5 -> 4; matrix products, arithmetic and copies ran while one was open for 13% -> 1% of each run, Pallas kernels for 0% -> 0%
where the time goes in v3:
time: 232 us; the launch traced here: 231 us
  waiting for transfers between devices  144 us (62%)
  local copies, waits for them, and re-layouts  27.6 us (12%)
  matrix products  20 us (9%)
  blocking collectives  15.3 us (7%)
  between operations  13.2 us (6%)
  starting transfers between devices  9.19 us (4%)
    all_gather x1, waiting for transfers between devices, shards(): occ_half = lax.all_gather(occ_local, 'row', axis=0, tiled=True)  60 us
    reduce_scatter x1, waiting for transfers between devices, shards(): lax.psum_scatter(z, 'col', scatter_dimension=0, tiled=True)  43.1 us
    ppermute x1, waiting for transfers between devices, shards(): got = lax.ppermute(give, 'row', perm=[(i, i ^ 1) for i in range(row_count)])  23.8 us
    reduce_scatter x1, waiting for transfers between devices, shards(): lax.psum_scatter(partial.astype(jnp.bfloat16), 'tensor', scatter_dimensio...  16.9 us
    all_to_all x1, blocking collectives, shards(): got_rows = lax.all_to_all(w, 'row', split_axis=0, concat_axis=0, tiled=True)  15.3 us
    reshape x1, local copies, waits for them, and re-layouts, shards(): dense.reshape(aux_blocks * NBC, mu_blocks, qsize, TB).transpose(0, 3, 1, 2)  11.6 us
    dot_general x1, matrix products, shards(): jnp.einsum('bwk,ki->bwi', dense, occ_q, preferred_element_type=jnp.float32)  7.74 us
    all_to_all x1, starting transfers between devices, shards(): recv = lax.all_to_all(send, owners, split_axis=0, concat_axis=0, tiled=True)  7.32 us
  transfers between devices with their start and end apart: 5, of which 4 were waited for; matrix products, arithmetic and copies ran while one was open for 1% of the time, Pallas kernels for 0%

profile of v3, /device:TPU:32, one launch (start us, length us, event | category | flops | bytes accessed | tf_op | source)
XLA Modules:
  0.0 231.4 jit_solution(16851518065777410352)
XLA Ops:
  6.5 0.0 copy-start
  6.5 0.7 convert.9
  7.3 0.7 subtract_convert_fusion
  8.0 0.1 copy.20
  8.1 0.1 convert_element_type.45
  8.2 3.1 %reshape.80 = bf16[32,32,1024]{2,1,0:T(8,128)(2,1)S(1)} reshape(bf16[32,8,4096]{2,1,0:T(8,128)(2,1)} %param.4) | data formatting | bytes 4194304 | tf_op jit(solution)/shard_map/reshape | solution.py:33
  11.3 0.2 pad_maximum_fusion
  11.5 2.7 %copy.21 = bf16[32,33,1024]{2,1,0:T(8,128)(2,1)} copy(bf16[32,33,1024]{2,0,1:T(8,128)(2,1)S(1)} %pad_maximum_fusion) | data formatting | bytes 4325376 | tf_op jit(solution)/shard_map/concatenate | solution.py:38
  14.3 7.3 %all-to-all-start = ((bf16[32,33,1024]{2,1,0:T(8,128)(2,1)}), bf16[32,33,1024]{2,1,0:T(8,128)(2,1)S(1)}, u32[]{:S(2)}, u32[]{:S(2)}) async-start(bf16[32,33,1024]{2,1,0:T(8,128)(2,1)} %copy.21), calls=%async_computation | async-start | bytes 5242880 | tf_op jit(solution)/shard_map/all_to_all | solution.py:39
  21.6 0.0 all-gather.3.cloned.1.call-start
  21.7 0.0 copy-done
  21.7 0.6 copy.29
  22.3 0.0 all-gather.3.cloned.1.call-update
  22.3 0.0 reduce-scatter.3.cloned.1.call-start
  22.4 60.0 %all-gather.3.cloned.1.call-done = bf16[32,2,1,16,512]{4,3,0,2,1:T(8,128)(2,1)} async-done(((bf16[2,2,1,16,512]{4,3,0,2,1:T(8,128)(2,1)}), bf16[32,2,1,16,512]{4,3,0,2,1:T(8,128)(2,1)}) %all-gather.3.cloned.1.call-update) | async-done | bytes 1048592 | tf_op jit(solution)/shard_map/all_gather | solution.py:52
  82.4 1.9 constant_dynamic-slice_fusion
  84.3 0.0 all-to-all-done
  84.3 0.1 fusion.10
  84.4 0.5 reshape.91
  84.9 0.5 fusion.8
  85.4 0.2 slice.35
  85.6 6.0 %fusion.2 = bf16[2048,1024]{1,0:T(8,128)(2,1)} fusion(bf16[1024,1024]{1,0:T(8,128)(2,1)S(1)} %bitcast.47, s32[1024]{0:T(1024)S(1)} %fusion.8), kind=kOutput, calls=%fused_computation.4 | convolution fusion | flops 4299161600 | bytes 6295552 | tf_op jit(solution)/shard_map/dot_general | solution.py:46
  91.6 0.0 copy-start.1
  91.6 11.6 %reshape.82 = bf16[64,32,16,64]{3,2,1,0:T(8,128)(2,1)} reshape(bf16[2048,1024]{1,0:T(8,128)(2,1)} %fusion.2) | data formatting | bytes 8388608 | tf_op jit(solution)/shard_map/reshape | solution.py:47
  103.3 0.0 copy-done.1
  103.3 7.7 %convolution_convert_fusion = bf16[4,16,64,512]{3,2,1,0:T(8,128)(2,1)} fusion(bf16[4,16,64,512]{2,3,1,0:T(8,128)(2,1)} %bitcast.42, bf16[512,512,1,1]{1,0,3,2:T(8,128)(2,1)S(1)} %bitcast.46), kind=kOutput, calls=%fused_computation.6 | convolution fusion | flops 2149580800 | bytes 8912896 | tf_op jit(solution)/shard_map/bwk,ki->bwi/dot_general | solution.py:55
  111.0 0.0 reduce-scatter.3.cloned.1.call-update
  111.0 0.0 reduce-scatter.5.cloned.1.call-start
  111.1 16.9 %reduce-scatter.3.cloned.1.call-done = bf16[2,16,64,512]{3,2,1,0:T(8,128)(2,1)} async-done(((bf16[4,16,64,512]{3,2,1,0:T(8,128)(2,1)}), bf16[2,16,64,512]{3,2,1,0:T(8,128)(2,1)}) %reduce-scatter.3.cloned.1.call-update) | async-done | bytes 2097168 | tf_op jit(solution)/shard_map/reduce_scatter | solution.py:58
  128.0 1.3 dynamic-slice_bitcast_fusion
  129.3 1.7 collective-permute-start
  131.0 23.8 %collective-permute-done = bf16[16,64,512]{2,1,0:T(8,128)(2,1)S(1)} collective-permute-done((bf16[16,64,512]{2,1,0:T(8,128)(2,1)S(1)}, bf16[16,64,512]{2,1,0:T(8,128)(2,1)S(1)}, u32[]{:S(2)}, u32[]{:S(2)}) %collective-permute-start) | collective-permute-done | bytes 1048608 | tf_op jit(solution)/shard_map/ppermute | solution.py:62
  154.8 6.2 %fusion.3 = bf16[2048,512]{0,1:T(8,128)(2,1)} fusion(bf16[16,64,2048]{2,1,0:T(8,128)(2,1)} %bitcast.50, bf16[16,64,512]{2,1,0:T(8,128)(2,1)S(1)} %collective-permute-done, bf16[2,16,64,512]{3,2,1,0:T(8,128)(2,1)} %reduce-scatter.3.cloned.1.call-done, s32[]{:T(128)S(6)} %select_n.24), kind=kOutput, calls=%fused_computation.5 | convolution fusion | flops 2150629376 | bytes 8388612 | tf_op jit(solution)/shard_map/nwi,nwv->vi/dot_general | solution.py:67
  161.0 2.9 %copy.24 = bf16[2048,512]{1,0:T(8,128)(2,1)S(1)} copy(bf16[2048,512]{0,1:T(8,128)(2,1)} %fusion.3) | data formatting | bytes 4194304 | tf_op jit(solution)/shard_map/convert_element_type | solution.py:67
  163.9 1.6 copy.25
  165.5 0.0 reduce-scatter.5.cloned.1.call-update
  165.5 43.1 %reduce-scatter.5.cloned.1.call-done = bf16[256,512]{1,0:T(8,128)(2,1)} async-done(((bf16[2048,512]{1,0:T(8,128)(2,1)}), bf16[256,512]{1,0:T(8,128)(2,1)}) %reduce-scatter.5.cloned.1.call-update) | async-done | bytes 262160 | tf_op jit(solution)/shard_map/reduce_scatter | solution.py:70
  208.6 15.3 %all_to_all.10 = bf16[16,16,512]{2,1,0:T(8,128)(2,1)S(1)} all-to-all(bf16[16,16,512]{2,1,0:T(8,128)(2,1)} %bitcast.49), channel_id=1, replica_groups=mesh['tensor'=2,'row'=16,'col'=8] {'row'}, dimensions={0} | all-to-all | bytes 524288 | tf_op jit(solution)/shard_map/all_to_all | solution.py:72
  224.0 0.9 copy.31
  (5 shorter events, 0.1 us)
Async XLA Ops:
  6.5 15.1 %copy-start = (bf16[128,512]{1,0:T(8,128)(2,1)S(1)}, bf16[128,512]{1,0:T(8,128)(2,1)}, u32[]{:S(2)}) copy-start(bf16[128,512]{1,0:T(8,128)(2,1)} %param.7) | copy-start | bytes 393220
  14.3 70.0 %all-to-all-start = ((bf16[32,33,1024]{2,1,0:T(8,128)(2,1)}), bf16[32,33,1024]{2,1,0:T(8,128)(2,1)S(1)}, u32[]{:S(2)}, u32[]{:S(2)}) async-start(bf16[32,33,1024]{2,1,0:T(8,128)(2,1)} %copy.21), calls=%async_computation | async-start | bytes 5242880 | tf_op jit(solution)/shard_map/all_to_all | solution.py:39
  21.6 60.8 %all-gather.3.cloned.1.call-start = ((), (), s32[]{:S(2)}) async-start(), calls=%async_computation.6 | async-start | bytes 1114112 | tf_op jit(solution)/shard_map/all_gather | solution.py:52
  22.3 105.6 %reduce-scatter.3.cloned.1.call-start = ((), (), s32[]{:S(2)}) async-start(), calls=%async_computation.4 | async-start | bytes 6291456 | tf_op jit(solution)/shard_map/reduce_scatter | solution.py:58
  91.6 11.6 %copy-start.1 = (bf16[32,1,1,16,512]{4,3,0,2,1:T(8,128)(2,1)S(1)}, bf16[32,1,1,16,512]{4,3,0,2,1:T(8,128)(2,1)}, u32[]{:S(2)}) copy-start(bf16[32,1,1,16,512]{4,3,0,2,1:T(8,128)(2,1)} %constant_dynamic-slice_fusion) | copy-start | bytes 1572868
  111.0 97.6 %reduce-scatter.5.cloned.1.call-start = ((), (), s32[]{:S(2)}) async-start(), calls=%async_computation.5 | async-start | bytes 2359296 | tf_op jit(solution)/shard_map/reduce_scatter | solution.py:70
  129.3 25.5 %collective-permute-start = (bf16[16,64,512]{2,1,0:T(8,128)(2,1)S(1)}, bf16[16,64,512]{2,1,0:T(8,128)(2,1)S(1)}, u32[]{:S(2)}, u32[]{:S(2)}) collective-permute-start(bf16[16,64,512]{2,1,0:T(8,128)(2,1)S(1)} %dynamic-slice_bitcast_fusion), channel_id=1, source_target_pairs={{0,8},{8,0},{16,24},{24,16},{32,40},{40,32},{48,56},{56,48},{64,72... | collective-permute-start | bytes 3145736 | tf_op jit(solution)/shard_map/ppermute | solution.py:62
Sparse Core Ops, SparseCore 0:
  24.9 57.4 all-gather.2
  111.1 16.7 reduce-scatter.2
  165.6 42.9 reduce-scatter.4

commit v4 on v3

--- a/solution.py
+++ b/solution.py
@@ -25,7 +25,7 @@
     mu_blocks = row_count * MB
     quarters = tensor_count * 2
     qsize = TB // quarters
-    assert row_count == 2 * PB and quarters * qsize == TB
+    assert row_count == 2 * PB and quarters * qsize == TB and row_count * tensor_count == mu_blocks
 
     owners = ("row", "tensor")
     dests = row_count * tensor_count
@@ -35,10 +35,16 @@
         [tile_index[:, 0], tile_index[:, 1], tile_index[:, 2] - col_at * NBC], axis=1
     ).astype(jnp.bfloat16).reshape(1, 1, held * 3)
     index_row = jnp.pad(local_index, ((0, 0), (0, 0), (0, lanes - held * 3)))
-    send = jnp.concatenate([send, jnp.broadcast_to(index_row, (dests, 1, lanes))], axis=1)
+    occ_rows = qsize * NOCC // lanes
+    occ_block = lax.dynamic_index_in_dim(occupied_coeff.reshape(MB, TB, NOCC), tensor_at, 0, keepdims=False)
+    occ_send = jnp.broadcast_to(occ_block.reshape(1, quarters, occ_rows, lanes), (PB, quarters, occ_rows, lanes))
+    send = jnp.concatenate(
+        [send, jnp.broadcast_to(index_row, (dests, 1, lanes)), occ_send.reshape(dests, occ_rows, lanes)], axis=1
+    )
     recv = lax.all_to_all(send, owners, split_axis=0, concat_axis=0, tiled=True)
     slices = recv[:, :held, :].reshape(dests * held, lanes)
     index = recv[:, held, : held * 3].astype(jnp.int32).reshape(dests * held, 3)
+    occ_q = recv[:, held + 1 :, :].reshape(mu_blocks * qsize, NOCC)
 
     block = (index[:, 0] * NBC + index[:, 2]) * mu_blocks + index[:, 1]
     blocks = aux_blocks * NBC * mu_blocks
@@ -47,11 +53,6 @@
     dense = dense.reshape(aux_blocks * NBC, mu_blocks, qsize, TB).transpose(0, 3, 1, 2)
     dense = dense.reshape(aux_blocks * NBC, TB, mu_blocks * qsize)
 
-    occ_local = occupied_coeff.reshape(MB, 2, tensor_count, qsize, NOCC)
-    occ_local = lax.dynamic_index_in_dim(occ_local, tensor_at, axis=2, keepdims=False)
-    occ_half = lax.all_gather(occ_local, "row", axis=0, tiled=True)
-    occ_q = lax.dynamic_index_in_dim(occ_half, row_at % 2, axis=1, keepdims=False)
-    occ_q = occ_q.reshape(mu_blocks * qsize, NOCC)
     partial = jnp.einsum("bwk,ki->bwi", dense, occ_q, preferred_element_type=jnp.float32)
     partial = partial.reshape(aux_blocks, NBC, TB, NOCC)
 

time: 232 us -> 213 us (0.918)
  waiting for transfers between devices: 144 us -> 83.9 us
  blocking collectives: 15.3 us -> 61.7 us
  starting transfers between devices: 9.19 us -> 1.79 us
    all_gather x1 -> x0, waiting for transfers between devices: 60 us -> none  [shards(): occ_half = lax.all_gather(occ_local, 'row', axis=0, tiled=True)]
    all_to_all x0 -> x1, blocking collectives: none -> 46.4 us  [shards(): recv = lax.all_to_all(send, owners, split_axis=0, concat_axis=0, tiled=True)]
    all_to_all x1 -> x0, starting transfers between devices: 7.32 us -> none  [shards(): recv = lax.all_to_all(send, owners, split_axis=0, concat_axis=0, tiled=True)]
  transfers between devices with their start and end apart: 5 -> 3, of which waited for: 4 -> 3; matrix products, arithmetic and copies ran while one was open for 1% -> 0% of each run, Pallas kernels for 0% -> 0%
where the time goes in v4:
time: 213 us
  waiting for transfers between devices  83.9 us (39%)
  blocking collectives  61.7 us (29%)
  local copies, waits for them, and re-layouts  28 us (13%)
  matrix products  19.9 us (9%)
  between operations  13.5 us (6%)
  other arithmetic  3.68 us (2%)
    all_to_all x1, blocking collectives, shards(): recv = lax.all_to_all(send, owners, split_axis=0, concat_axis=0, tiled=True)  46.4 us
    reduce_scatter x1, waiting for transfers between devices, shards(): lax.psum_scatter(z, 'col', scatter_dimension=0, tiled=True)  43.1 us
    ppermute x1, waiting for transfers between devices, shards(): got = lax.ppermute(give, 'row', perm=[(i, i ^ 1) for i in range(row_count)])  23.8 us
    reduce_scatter x1, waiting for transfers between devices, shards(): lax.psum_scatter(partial.astype(jnp.bfloat16), 'tensor', scatter_dimensio...  16.9 us
    all_to_all x1, blocking collectives, shards(): got_rows = lax.all_to_all(w, 'row', split_axis=0, concat_axis=0, tiled=True)  15.3 us
    reshape x1, local copies, waits for them, and re-layouts, shards(): dense.reshape(aux_blocks * NBC, mu_blocks, qsize, TB).transpose(0, 3, 1, 2)  11.6 us
    dot_general x1, matrix products, shards(): jnp.einsum('bwk,ki->bwi', dense, occ_q, preferred_element_type=jnp.float32)  7.74 us
    dot_general x1, matrix products, shards(): jnp.einsum('nwi,nwv->vi', occ_done, virt, preferred_element_type=jnp.floa...  6.19 us
  transfers between devices with their start and end apart: 3, of which 3 were waited for; matrix products, arithmetic and copies ran while one was open for 0% of the time, Pallas kernels for 0%

profile of v4, /device:TPU:32, one launch (start us, length us, event | category | flops | bytes accessed | tf_op | source)
XLA Modules:
  0.0 212.5 jit_solution(9407285849809376303)
XLA Ops:
  6.5 0.0 copy-start
  6.5 0.0 reduce-scatter.3.cloned.1.call-start
  6.5 0.7 convert.9
  7.3 0.7 subtract_convert_fusion
  8.0 0.1 copy.26
  8.1 0.1 convert_element_type.45
  8.2 0.0 copy-done
  8.3 0.1 copy.27
  8.3 0.2 broadcast_in_dim.19
  8.5 0.1 reshape.87
  8.6 3.1 %reshape.85 = bf16[32,32,1024]{2,1,0:T(8,128)(2,1)S(1)} reshape(bf16[32,8,4096]{2,1,0:T(8,128)(2,1)} %param.4) | data formatting | bytes 4194304 | tf_op jit(solution)/shard_map/reshape | solution.py:33
  11.8 0.3 pad_maximum_fusion
  12.1 1.5 copy.28
  13.6 46.4 %all_to_all.10 = bf16[32,41,1024]{2,1,0:T(8,128)(2,1)S(1)} all-to-all(bf16[32,41,1024]{2,1,0:T(8,128)(2,1)S(1)} %copy.28), channel_id=1, replica_groups=mesh['tensor'=2,'row'=16,'col'=8] {'row','tensor'}, dimensions={0} | all-to-all | bytes 5373952 | tf_op jit(solution)/shard_map/all_to_all | solution.py:44
  60.0 0.1 fusion.11
  60.1 1.3 reshape.97
  61.4 1.9 fusion.8
  63.3 1.0 slice.40
  64.3 2.0 reshape.99
  66.3 0.2 slice.39
  66.5 6.0 %fusion.2 = bf16[2048,1024]{1,0:T(8,128)(2,1)} fusion(bf16[1024,1024]{1,0:T(8,128)(2,1)S(1)} %bitcast.45, s32[1024]{0:T(1024)S(1)} %fusion.8), kind=kOutput, calls=%fused_computation.4 | convolution fusion | flops 4299161600 | bytes 6295552 | tf_op jit(solution)/shard_map/dot_general | solution.py:52
  72.5 0.0 copy-start.1
  72.5 11.6 %reshape.89 = bf16[64,32,16,64]{3,2,1,0:T(8,128)(2,1)} reshape(bf16[2048,1024]{1,0:T(8,128)(2,1)} %fusion.2) | data formatting | bytes 8388608 | tf_op jit(solution)/shard_map/reshape | solution.py:53
  84.1 0.0 copy-done.1
  84.1 7.7 %convolution_convert_fusion = bf16[4,16,64,512]{3,2,1,0:T(8,128)(2,1)} fusion(bf16[4,16,64,512]{2,3,1,0:T(8,128)(2,1)} %bitcast.41, bf16[512,512,1,1]{1,0,2,3:T(8,128)(2,1)S(1)} %copy-done.1), kind=kOutput, calls=%fused_computation.7 | convolution fusion | flops 2149580800 | bytes 8912896 | tf_op jit(solution)/shard_map/bwk,ki->bwi/dot_general | solution.py:56
  91.9 0.0 reduce-scatter.3.cloned.1.call-update
  91.9 0.0 reduce-scatter.5.cloned.1.call-start
  92.0 16.9 %reduce-scatter.3.cloned.1.call-done = bf16[2,16,64,512]{3,2,1,0:T(8,128)(2,1)} async-done(((bf16[4,16,64,512]{3,2,1,0:T(8,128)(2,1)}), bf16[2,16,64,512]{3,2,1,0:T(8,128)(2,1)}) %reduce-scatter.3.cloned.1.call-update) | async-done | bytes 2097168 | tf_op jit(solution)/shard_map/reduce_scatter | solution.py:59
  108.9 1.3 dynamic-slice_bitcast_fusion
  110.2 1.7 collective-permute-start
  112.0 23.8 %collective-permute-done = bf16[16,64,512]{2,1,0:T(8,128)(2,1)S(1)} collective-permute-done((bf16[16,64,512]{2,1,0:T(8,128)(2,1)S(1)}, bf16[16,64,512]{2,1,0:T(8,128)(2,1)S(1)}, u32[]{:S(2)}, u32[]{:S(2)}) %collective-permute-start) | collective-permute-done | bytes 1048608 | tf_op jit(solution)/shard_map/ppermute | solution.py:63
  135.8 6.2 %fusion.3 = bf16[2048,512]{0,1:T(8,128)(2,1)} fusion(bf16[16,64,2048]{2,1,0:T(8,128)(2,1)} %bitcast.48, bf16[16,64,512]{2,1,0:T(8,128)(2,1)S(1)} %collective-permute-done, bf16[2,16,64,512]{3,2,1,0:T(8,128)(2,1)} %reduce-scatter.3.cloned.1.call-done, s32[]{:T(128)S(6)} %select_n.20), kind=kOutput, calls=%fused_computation.5 | convolution fusion | flops 2150629376 | bytes 8388612 | tf_op jit(solution)/shard_map/nwi,nwv->vi/dot_general | solution.py:68
  141.9 2.9 %copy.30 = bf16[2048,512]{1,0:T(8,128)(2,1)S(1)} copy(bf16[2048,512]{0,1:T(8,128)(2,1)} %fusion.3) | data formatting | bytes 4194304 | tf_op jit(solution)/shard_map/convert_element_type | solution.py:68
  144.8 1.6 copy.31
  146.4 0.0 reduce-scatter.5.cloned.1.call-update
  146.4 43.1 %reduce-scatter.5.cloned.1.call-done = bf16[256,512]{1,0:T(8,128)(2,1)} async-done(((bf16[2048,512]{1,0:T(8,128)(2,1)}), bf16[256,512]{1,0:T(8,128)(2,1)}) %reduce-scatter.5.cloned.1.call-update) | async-done | bytes 262160 | tf_op jit(solution)/shard_map/reduce_scatter | solution.py:71
  189.6 15.3 %all_to_all.11 = bf16[16,16,512]{2,1,0:T(8,128)(2,1)S(1)} all-to-all(bf16[16,16,512]{2,1,0:T(8,128)(2,1)} %bitcast.47), channel_id=1, replica_groups=mesh['tensor'=2,'row'=16,'col'=8] {'row'}, dimensions={0} | all-to-all | bytes 524288 | tf_op jit(solution)/shard_map/all_to_all | solution.py:73
  204.8 0.9 copy.36
  (6 shorter events, 0.1 us)
Async XLA Ops:
  6.5 1.7 copy-start
  6.5 102.4 %reduce-scatter.3.cloned.1.call-start = ((), (), s32[]{:S(2)}) async-start(), calls=%async_computation.4 | async-start | bytes 6291456 | tf_op jit(solution)/shard_map/reduce_scatter | solution.py:59
  72.5 11.6 %copy-start.1 = (bf16[512,512,1,1]{1,0,2,3:T(8,128)(2,1)S(1)}, bf16[512,512,1,1]{1,0,2,3:T(8,128)(2,1)}, u32[]{:S(2)}) copy-start(bf16[512,512,1,1]{1,0,2,3:T(8,128)(2,1)} %reshape.99) | copy-start | bytes 1572868
  91.9 97.7 %reduce-scatter.5.cloned.1.call-start = ((), (), s32[]{:S(2)}) async-start(), calls=%async_computation.5 | async-start | bytes 2359296 | tf_op jit(solution)/shard_map/reduce_scatter | solution.py:71
  110.2 25.5 %collective-permute-start = (bf16[16,64,512]{2,1,0:T(8,128)(2,1)S(1)}, bf16[16,64,512]{2,1,0:T(8,128)(2,1)S(1)}, u32[]{:S(2)}, u32[]{:S(2)}) collective-permute-start(bf16[16,64,512]{2,1,0:T(8,128)(2,1)S(1)} %dynamic-slice_bitcast_fusion), channel_id=1, source_target_pairs={{0,8},{8,0},{16,24},{24,16},{32,40},{40,32},{48,56},{56,48},{64,72... | collective-permute-start | bytes 3145736 | tf_op jit(solution)/shard_map/ppermute | solution.py:63
Sparse Core Ops, SparseCore 0:
  92.0 16.8 reduce-scatter.2
  146.5 42.9 reduce-scatter.4

commit v5 on v3

--- a/solution.py
+++ b/solution.py
@@ -25,7 +25,7 @@
     mu_blocks = row_count * MB
     quarters = tensor_count * 2
     qsize = TB // quarters
-    assert row_count == 2 * PB and quarters * qsize == TB
+    assert row_count == 2 * PB and tensor_count == 2 and quarters * qsize == TB
 
     owners = ("row", "tensor")
     dests = row_count * tensor_count
@@ -40,6 +40,12 @@
     slices = recv[:, :held, :].reshape(dests * held, lanes)
     index = recv[:, held, : held * 3].astype(jnp.int32).reshape(dests * held, 3)
 
+    occ_all = lax.all_gather(occupied_coeff, "row", axis=0, tiled=True)
+    quarter = 2 * (row_at % 2) + tensor_at
+    occ_q = lax.dynamic_index_in_dim(
+        occ_all.reshape(mu_blocks, quarters, qsize, NOCC), quarter, axis=1, keepdims=False
+    ).reshape(mu_blocks * qsize, NOCC)
+
     block = (index[:, 0] * NBC + index[:, 2]) * mu_blocks + index[:, 1]
     blocks = aux_blocks * NBC * mu_blocks
     selector = (jnp.arange(blocks)[:, None] == block[None, :]).astype(jnp.bfloat16)
@@ -47,20 +53,22 @@
     dense = dense.reshape(aux_blocks * NBC, mu_blocks, qsize, TB).transpose(0, 3, 1, 2)
     dense = dense.reshape(aux_blocks * NBC, TB, mu_blocks * qsize)
 
-    occ_local = occupied_coeff.reshape(MB, 2, tensor_count, qsize, NOCC)
-    occ_local = lax.dynamic_index_in_dim(occ_local, tensor_at, axis=2, keepdims=False)
-    occ_half = lax.all_gather(occ_local, "row", axis=0, tiled=True)
-    occ_q = lax.dynamic_index_in_dim(occ_half, row_at % 2, axis=1, keepdims=False)
-    occ_q = occ_q.reshape(mu_blocks * qsize, NOCC)
     partial = jnp.einsum("bwk,ki->bwi", dense, occ_q, preferred_element_type=jnp.float32)
     partial = partial.reshape(aux_blocks, NBC, TB, NOCC)
 
-    pair = lax.psum_scatter(partial.astype(jnp.bfloat16), "tensor", scatter_dimension=0, tiled=True)
     side = row_at % 2
-    keep = lax.dynamic_index_in_dim(pair, side, axis=0, keepdims=False)
-    give = lax.dynamic_index_in_dim(pair, 1 - side, axis=0, keepdims=False)
-    got = lax.ppermute(give, "row", perm=[(i, i ^ 1) for i in range(row_count)])
-    occ_done = (keep.astype(jnp.float32) + got.astype(jnp.float32)).astype(jnp.bfloat16)
+    halves = []
+    for half in jnp.split(partial.astype(jnp.bfloat16), 2, axis=3):
+        pairs = half.reshape(tensor_count, AB, NBC, TB, NOCC // 2)
+        mine = lax.dynamic_index_in_dim(pairs, tensor_at, axis=0, keepdims=False)
+        other = lax.dynamic_index_in_dim(pairs, 1 - tensor_at, axis=0, keepdims=False)
+        got_t = lax.ppermute(other, "tensor", perm=[(0, 1), (1, 0)])
+        pair = (mine.astype(jnp.float32) + got_t.astype(jnp.float32)).astype(jnp.bfloat16)
+        keep = lax.dynamic_index_in_dim(pair, side, axis=0, keepdims=False)
+        give = lax.dynamic_index_in_dim(pair, 1 - side, axis=0, keepdims=False)
+        got_r = lax.ppermute(give, "row", perm=[(i, i ^ 1) for i in range(row_count)])
+        halves.append(keep.astype(jnp.float32) + got_r.astype(jnp.float32))
+    occ_done = jnp.concatenate(halves, axis=2).astype(jnp.bfloat16)
 
     chunk = NV // (row_count * col_count)
     virt = virtual_coeff.reshape(NBC, TB, NV)

time: 232 us -> 196 us (0.84)
  waiting for transfers between devices: 144 us -> 103 us
  other arithmetic: 2.17 us -> 8 us
    all_gather x1, waiting for transfers between devices: 60 us -> 3.29 us  [shards(): occ_all = lax.all_gather(occupied_coeff, 'row', axis=0, tiled=True)]
    all_to_all x1, waiting for transfers between devices: 0.01 us -> 36.7 us  [shards(): recv = lax.all_to_all(send, owners, split_axis=0, concat_axis=0, tiled=True)]
    reduce_scatter x1 -> x0, waiting for transfers between devices: 16.9 us -> none  [shards(): lax.psum_scatter(partial.astype(jnp.bfloat16), 'tensor', scatter_dimensio...]
    convert_element_type x0 -> x2, other arithmetic: none -> 3.49 us  [shards(): (mine.astype(jnp.float32) + got_t.astype(jnp.float32)).astype(jnp.bfloat16)]
    ppermute x1 -> x4, waiting for transfers between devices: 23.8 us -> 20.7 us  [the longest x2 19.5 us: shards(): lax.ppermute(give, 'row', perm=[(i, i ^ 1) for i in range(row_count)])]
    another operation x2 -> x4, other arithmetic: 1.41 us -> 3.75 us
  transfers between devices with their start and end apart: 5 -> 7, of which waited for: 4 -> 6; matrix products, arithmetic and copies ran while one was open for 1% -> 17% of each run, Pallas kernels for 0% -> 0%
where the time goes in v5:
time: 196 us
  waiting for transfers between devices  103 us (53%)
  local copies, waits for them, and re-layouts  28.6 us (15%)
  matrix products  17.7 us (9%)
  blocking collectives  15.3 us (8%)
  between operations  13.6 us (7%)
  starting transfers between devices  9.68 us (5%)
  other arithmetic  8 us (4%)
    reduce_scatter x1, waiting for transfers between devices, shards(): lax.psum_scatter(z, 'col', scatter_dimension=0, tiled=True)  41.3 us
    all_to_all x1, waiting for transfers between devices, shards(): recv = lax.all_to_all(send, owners, split_axis=0, concat_axis=0, tiled=True)  36.7 us
    ppermute x2, waiting for transfers between devices, shards(): lax.ppermute(give, 'row', perm=[(i, i ^ 1) for i in range(row_count)])  19.5 us
    all_to_all x1, blocking collectives, shards(): got_rows = lax.all_to_all(w, 'row', split_axis=0, concat_axis=0, tiled=True)  15.3 us
    reshape x1, local copies, waits for them, and re-layouts, shards(): dense.reshape(aux_blocks * NBC, mu_blocks, qsize, TB).transpose(0, 3, 1, 2)  11.6 us
    all_to_all x1, starting transfers between devices, shards(): recv = lax.all_to_all(send, owners, split_axis=0, concat_axis=0, tiled=True)  7.32 us
    dot_general x1, matrix products, shards(): jnp.dot(selector, slices, preferred_element_type=jnp.float32)  6.03 us
    dot_general x1, matrix products, shards(): jnp.einsum('nwi,nwv->vi', occ_done, virt, preferred_element_type=jnp.floa...  5.9 us
  transfers between devices with their start and end apart: 7, of which 6 were waited for; matrix products, arithmetic and copies ran while one was open for 17% of the time, Pallas kernels for 0%

profile of v5, /device:TPU:32, one launch (start us, length us, event | category | flops | bytes accessed | tf_op | source)
XLA Modules:
  0.0 195.5 jit_solution(14515395971492727885)
XLA Ops:
  6.5 0.0 all-gather.2.cloned.1.call-start
  6.5 0.7 all-gather.2.cloned.1.call-update
  7.3 0.7 convert.18
  8.0 0.7 subtract_convert_fusion
  8.7 0.1 copy.20
  8.8 0.1 convert_element_type.76
  8.9 3.1 %reshape.92 = bf16[32,32,1024]{2,1,0:T(8,128)(2,1)S(1)} reshape(bf16[32,8,4096]{2,1,0:T(8,128)(2,1)} %param.4) | data formatting | bytes 4194304 | tf_op jit(solution)/shard_map/reshape | solution.py:33
  12.0 0.2 pad_maximum_fusion
  12.2 2.7 %copy.21 = bf16[32,33,1024]{2,1,0:T(8,128)(2,1)} copy(bf16[32,33,1024]{2,0,1:T(8,128)(2,1)S(1)} %pad_maximum_fusion) | data formatting | bytes 4325376 | tf_op jit(solution)/shard_map/concatenate | solution.py:38
  15.0 7.3 %all-to-all-start = ((bf16[32,33,1024]{2,1,0:T(8,128)(2,1)}), bf16[32,33,1024]{2,1,0:T(8,128)(2,1)S(1)}, u32[]{:S(2)}, u32[]{:S(2)}) async-start(bf16[32,33,1024]{2,1,0:T(8,128)(2,1)} %copy.21), calls=%async_computation | async-start | bytes 5242880 | tf_op jit(solution)/shard_map/all_to_all | solution.py:39
  22.3 0.0 reduce-scatter.2.cloned.1.call-start
  22.4 36.7 %all-to-all-done = bf16[32,33,1024]{2,1,0:T(8,128)(2,1)S(1)} async-done(((bf16[32,33,1024]{2,1,0:T(8,128)(2,1)}), bf16[32,33,1024]{2,1,0:T(8,128)(2,1)S(1)}, u32[]{:S(2)}, u32[]{:S(2)}) %all-to-all-start) | async-done | bytes 2162720 | tf_op jit(solution)/shard_map/all_to_all | solution.py:39
  59.0 0.1 fusion.13
  59.1 0.5 reshape.105
  59.6 0.2 slice.35
  59.9 0.5 fusion.11
  60.4 6.0 %fusion.2 = bf16[2048,1024]{1,0:T(8,128)(2,1)} fusion(bf16[1024,1024]{1,0:T(8,128)(2,1)S(1)} %bitcast.66, s32[1024]{0:T(1024)S(1)} %fusion.11), kind=kOutput, calls=%fused_computation.4 | convolution fusion | flops 4299161600 | bytes 6295552 | tf_op jit(solution)/shard_map/dot_general | solution.py:52
  66.4 11.6 %reshape.94 = bf16[64,32,16,64]{3,2,1,0:T(8,128)(2,1)} reshape(bf16[2048,1024]{1,0:T(8,128)(2,1)} %fusion.2) | data formatting | bytes 8388608 | tf_op jit(solution)/shard_map/reshape | solution.py:53
  78.0 3.3 %all-gather.2.cloned.1.call-done = bf16[2048,512]{1,0:T(8,128)(2,1)} async-done(((bf16[128,512]{1,0:T(8,128)(2,1)}), bf16[2048,512]{1,0:T(8,128)(2,1)}) %all-gather.2.cloned.1.call-update) | async-done | bytes 2097168 | tf_op jit(solution)/shard_map/all_gather | solution.py:43
  81.3 1.1 constant_dynamic-slice_fusion
  82.4 5.8 %convolution_convert_fusion = bf16[4,16,64,512]{3,2,1,0:T(8,128)(2,1)S(1)} fusion(bf16[4,16,64,512]{2,3,1,0:T(8,128)(2,1)} %bitcast.57, bf16[512,512,1,1]{1,0,3,2:T(8,128)(2,1)S(1)} %bitcast.65), kind=kOutput, calls=%fused_computation.6 | convolution fusion | flops 2149580800 | bytes 8912896 | tf_op jit(solution)/shard_map/bwk,ki->bwi/dot_general | solution.py:56
  88.1 0.4 fusion.15
  88.5 0.0 copy-start
  88.5 0.1 dynamic-slice_bitcast_fusion.1
  88.6 0.1 collective-permute-start
  88.7 1.3 dynamic-slice_bitcast_fusion
  90.0 0.2 copy-done
  90.2 0.1 collective-permute-start.2
  90.3 1.2 collective-permute-done
  91.5 1.9 fusion.5
  93.4 0.9 dynamic-slice_bitcast_fusion.3
  94.3 1.2 collective-permute-start.1
  95.4 0.0 collective-permute-done.2
  95.4 1.6 fusion.4
  97.0 0.0 copy-start.1
  97.0 1.0 copy-done.1
  98.0 1.0 collective-permute-start.3
  99.0 10.4 %collective-permute-done.1 = bf16[16,64,256]{2,1,0:T(8,128)(2,1)} collective-permute-done((bf16[16,64,256]{2,1,0:T(8,128)(2,1)}, bf16[16,64,256]{2,1,0:T(8,128)(2,1)}, u32[]{:S(2)}, u32[]{:S(2)}) %collective-permute-start.1) | collective-permute-done | bytes 524320 | tf_op jit(solution)/shard_map/ppermute | solution.py:69
  109.4 1.2 fusion.10
  110.6 9.1 %collective-permute-done.3 = bf16[16,64,256]{2,1,0:T(8,128)(2,1)S(1)} collective-permute-done((bf16[16,64,256]{2,1,0:T(8,128)(2,1)S(1)}, bf16[16,64,256]{2,1,0:T(8,128)(2,1)S(1)}, u32[]{:S(2)}, u32[]{:S(2)}) %collective-permute-start.3) | collective-permute-done | bytes 524320 | tf_op jit(solution)/shard_map/ppermute | solution.py:69
  119.7 1.2 fusion.9
  120.9 5.9 %fusion.3 = bf16[2048,512]{0,1:T(8,128)(2,1)} fusion(bf16[16,64,2048]{2,1,0:T(8,128)(2,1)} %bitcast.70, bf16[16,64,256]{2,1,0:T(8,128)(2,1)S(1)} %fusion.9, bf16[16,64,256]{2,1,0:T(8,128)(2,1)S(1)} %fusion.10), kind=kOutput, calls=%fused_computation.5 | convolution fusion | flops 2150629376 | bytes 7340032 | tf_op jit(solution)/shard_map/nwi,nwv->vi/dot_general | solution.py:75
  126.8 2.9 %copy.24 = bf16[2048,512]{1,0:T(8,128)(2,1)S(1)} copy(bf16[2048,512]{0,1:T(8,128)(2,1)} %fusion.3) | data formatting | bytes 4194304 | tf_op jit(solution)/shard_map/convert_element_type | solution.py:75
  129.6 1.6 copy.25
  131.2 0.0 reduce-scatter.2.cloned.1.call-update
  131.2 41.3 %reduce-scatter.2.cloned.1.call-done = bf16[256,512]{1,0:T(8,128)(2,1)} async-done(((bf16[2048,512]{1,0:T(8,128)(2,1)}), bf16[256,512]{1,0:T(8,128)(2,1)}) %reduce-scatter.2.cloned.1.call-update) | async-done | bytes 262160 | tf_op jit(solution)/shard_map/reduce_scatter | solution.py:78
  172.6 15.3 %all_to_all.10 = bf16[16,16,512]{2,1,0:T(8,128)(2,1)S(1)} all-to-all(bf16[16,16,512]{2,1,0:T(8,128)(2,1)} %bitcast.68), channel_id=1, replica_groups=mesh['tensor'=2,'row'=16,'col'=8] {'row'}, dimensions={0} | all-to-all | bytes 524288 | tf_op jit(solution)/shard_map/all_to_all | solution.py:80
  187.8 0.9 copy.31
  (5 shorter events, 0.1 us)
Async XLA Ops:
  6.5 74.7 %all-gather.2.cloned.1.call-start = ((), (), s32[]{:S(2)}) async-start(), calls=%async_computation.3 | async-start | bytes 2228224 | tf_op jit(solution)/shard_map/all_gather | solution.py:43
  15.0 44.1 %all-to-all-start = ((bf16[32,33,1024]{2,1,0:T(8,128)(2,1)}), bf16[32,33,1024]{2,1,0:T(8,128)(2,1)S(1)}, u32[]{:S(2)}, u32[]{:S(2)}) async-start(bf16[32,33,1024]{2,1,0:T(8,128)(2,1)} %copy.21), calls=%async_computation | async-start | bytes 5242880 | tf_op jit(solution)/shard_map/all_to_all | solution.py:39
  22.3 150.3 %reduce-scatter.2.cloned.1.call-start = ((), (), s32[]{:S(2)}) async-start(), calls=%async_computation.4 | async-start | bytes 2359296 | tf_op jit(solution)/shard_map/reduce_scatter | solution.py:78
  88.5 1.7 copy-start
  88.6 2.9 %collective-permute-start = (bf16[2,16,64,256]{3,2,1,0:T(8,128)(2,1)S(1)}, bf16[2,16,64,256]{3,2,1,0:T(8,128)(2,1)}, u32[]{:S(2)}, u32[]{:S(2)}) collective-permute-start(bf16[2,16,64,256]{3,2,1,0:T(8,128)(2,1)S(1)} %dynamic-slice_bitcast_fusion.1), channel_id=1, source_target_pairs={{0,128},{128,0},{1,129},{129,1},{2,130},{130,2},{3,131},{131,3},{4... | collective-permute-start | bytes 3145736 | tf_op jit(solution)/shard_map/ppermute | solution.py:65
  90.2 5.3 %collective-permute-start.2 = (bf16[2,16,64,256]{3,2,1,0:T(8,128)(2,1)}, bf16[2,16,64,256]{3,2,1,0:T(8,128)(2,1)}, u32[]{:S(2)}, u32[]{:S(2)}) collective-permute-start(bf16[2,16,64,256]{3,2,1,0:T(8,128)(2,1)} %dynamic-slice_bitcast_fusion), channel_id=1, source_target_pairs={{0,128},{128,0},{1,129},{129,1},{2,130},{130,2},{3,131},{131,3},{4... | collective-permute-start | bytes 3145736 | tf_op jit(solution)/shard_map/ppermute | solution.py:65
  94.3 15.1 %collective-permute-start.1 = (bf16[16,64,256]{2,1,0:T(8,128)(2,1)}, bf16[16,64,256]{2,1,0:T(8,128)(2,1)}, u32[]{:S(2)}, u32[]{:S(2)}) collective-permute-start(bf16[16,64,256]{2,1,0:T(8,128)(2,1)} %dynamic-slice_bitcast_fusion.3), channel_id=1, source_target_pairs={{0,8},{8,0},{16,24},{24,16},{32,40},{40,32},{48,56},{56,48},{64,72... | collective-permute-start | bytes 1572872 | tf_op jit(solution)/shard_map/ppermute | solution.py:69
  97.0 1.0 copy-start.1
  98.0 21.6 %collective-permute-start.3 = (bf16[16,64,256]{2,1,0:T(8,128)(2,1)S(1)}, bf16[16,64,256]{2,1,0:T(8,128)(2,1)S(1)}, u32[]{:S(2)}, u32[]{:S(2)}) collective-permute-start(bf16[16,64,256]{2,1,0:T(8,128)(2,1)S(1)} %dynamic-slice_bitcast_fusion.2), channel_id=1, source_target_pairs={{0,8},{8,0},{16,24},{24,16},{32,40},{40,32},{48,56},{56,48},{64,72... | collective-permute-start | bytes 1572872 | tf_op jit(solution)/shard_map/ppermute | solution.py:69
Sparse Core Ops, SparseCore 0:
  9.8 71.4 all-gather.1
  131.4 41.1 reduce-scatter.1

commit v6 on v5

--- a/solution.py
+++ b/solution.py
@@ -74,8 +74,22 @@
     virt = virtual_coeff.reshape(NBC, TB, NV)
     z = jnp.einsum("nwi,nwv->vi", occ_done, virt, preferred_element_type=jnp.float32).astype(jnp.bfloat16)
     z = z.reshape(row_count, col_count, chunk, NOCC).transpose(1, 0, 2, 3)
-    z = z.reshape(col_count * row_count * chunk, NOCC)
-    w = lax.psum_scatter(z, "col", scatter_dimension=0, tiled=True).reshape(row_count, chunk, NOCC)
+    z = z.reshape(col_count, row_count * chunk, NOCC)
+    lanes_half = NOCC // 2
+    ring = (z[:, :, :lanes_half], z[:, :, lanes_half:])
+    steps = (1, -1)
+    accs = [
+        lax.dynamic_index_in_dim(part, (col_at - step) % col_count, axis=0, keepdims=False)
+        for part, step in zip(ring, steps)
+    ]
+    for hop in range(col_count - 1):
+        for which in range(2):
+            step = steps[which]
+            perm = [(i, (i + step) % col_count) for i in range(col_count)]
+            got = lax.ppermute(accs[which], "col", perm=perm)
+            own = lax.dynamic_index_in_dim(ring[which], (col_at - step * (hop + 2)) % col_count, axis=0, keepdims=False)
+            accs[which] = (got.astype(jnp.float32) + own.astype(jnp.float32)).astype(jnp.bfloat16)
+    w = jnp.concatenate(accs, axis=-1).reshape(row_count, chunk, NOCC)
 
     got_rows = lax.all_to_all(w, "row", split_axis=0, concat_axis=0, tiled=True)
     out = got_rows.reshape(PB, 2, chunk, NOCC).transpose(2, 1, 0, 3)

time: 196 us -> 201 us (1.026); the launches traced: 196 us -> 197 us
  starting transfers between devices: 9.68 us -> 26.5 us
  waiting for transfers between devices: 103 us -> 88.8 us
  blocking collectives: 15.3 us -> 13.2 us
    reduce_scatter x1 -> x0, waiting for transfers between devices: 41.3 us -> none  [shards(): lax.psum_scatter(z, 'col', scatter_dimension=0, tiled=True)]
    ppermute x0 -> x14, waiting for transfers between devices: none -> 28.5 us  [shards(): got = lax.ppermute(accs[which], 'col', perm=perm)]
    ppermute x0 -> x14, starting transfers between devices: none -> 16.9 us  [shards(): got = lax.ppermute(accs[which], 'col', perm=perm)]
    all_to_all x1, blocking collectives: 15.3 us -> 13.2 us  [shards(): got_rows = lax.all_to_all(w, 'row', split_axis=0, concat_axis=0, tiled=True)]
  transfers between devices with their start and end apart: 7 -> 20, of which waited for: 6 -> 18; matrix products, arithmetic and copies ran while one was open for 17% -> 18% of each run, Pallas kernels for 0% -> 0%
where the time goes in v6:
time: 201 us; the launch traced here: 197 us
  waiting for transfers between devices  88.8 us (44%)
  local copies, waits for them, and re-layouts  27.6 us (14%)
  starting transfers between devices  26.5 us (13%)
  matrix products  17.7 us (9%)
  between operations  13.7 us (7%)
  blocking collectives  13.2 us (7%)
  other arithmetic  9.64 us (5%)
    all_to_all x1, waiting for transfers between devices, shards(): recv = lax.all_to_all(send, owners, split_axis=0, concat_axis=0, tiled=True)  36.7 us
    ppermute x14, waiting for transfers between devices, shards(): got = lax.ppermute(accs[which], 'col', perm=perm)  28.5 us
    ppermute x2, waiting for transfers between devices, shards(): lax.ppermute(give, 'row', perm=[(i, i ^ 1) for i in range(row_count)])  18.4 us
    ppermute x14, starting transfers between devices, shards(): got = lax.ppermute(accs[which], 'col', perm=perm)  16.9 us
    all_to_all x1, blocking collectives, shards(): got_rows = lax.all_to_all(w, 'row', split_axis=0, concat_axis=0, tiled=True)  13.2 us
    reshape x1, local copies, waits for them, and re-layouts, shards(): dense.reshape(aux_blocks * NBC, mu_blocks, qsize, TB).transpose(0, 3, 1, 2)  11.6 us
    all_to_all x1, starting transfers between devices, shards(): recv = lax.all_to_all(send, owners, split_axis=0, concat_axis=0, tiled=True)  7.32 us
    dot_general x1, matrix products, shards(): jnp.dot(selector, slices, preferred_element_type=jnp.float32)  6.05 us
  transfers between devices with their start and end apart: 20, of which 18 were waited for; matrix products, arithmetic and copies ran while one was open for 18% of the time, Pallas kernels for 0%

profile of v6, /device:TPU:32, one launch (start us, length us, event | category | flops | bytes accessed | tf_op | source)
XLA Modules:
  0.0 197.1 jit_solution(6345098890101870038)
XLA Ops:
  6.5 0.7 all-gather.2.cloned.1.call-update
  7.3 0.7 convert.32
  8.9 3.1 %reshape.120 = bf16[32,32,1024]{2,1,0:T(8,128)(2,1)S(1)} reshape(bf16[32,8,4096]{2,1,0:T(8,128)(2,1)} %param.4) | data formatting | bytes 4194304 | tf_op jit(solution)/shard_map/reshape | solution.py:33
  12.2 2.7 %copy.21 = bf16[32,33,1024]{2,1,0:T(8,128)(2,1)} copy(bf16[32,33,1024]{2,0,1:T(8,128)(2,1)S(1)} %pad_maximum_fusion) | data formatting | bytes 4325376 | tf_op jit(solution)/shard_map/concatenate | solution.py:38
  15.0 7.3 %all-to-all-start = ((bf16[32,33,1024]{2,1,0:T(8,128)(2,1)}), bf16[32,33,1024]{2,1,0:T(8,128)(2,1)S(1)}, u32[]{:S(2)}, u32[]{:S(2)}) async-start(bf16[32,33,1024]{2,1,0:T(8,128)(2,1)} %copy.21), calls=%async_computation | async-start | bytes 5242880 | tf_op jit(solution)/shard_map/all_to_all | solution.py:39
  22.3 36.7 %all-to-all-done = bf16[32,33,1024]{2,1,0:T(8,128)(2,1)S(1)} async-done(((bf16[32,33,1024]{2,1,0:T(8,128)(2,1)}), bf16[32,33,1024]{2,1,0:T(8,128)(2,1)S(1)}, u32[]{:S(2)}, u32[]{:S(2)}) %all-to-all-start) | async-done | bytes 2162720 | tf_op jit(solution)/shard_map/all_to_all | solution.py:39
  60.3 6.0 %fusion.2 = bf16[2048,1024]{1,0:T(8,128)(2,1)} fusion(bf16[1024,1024]{1,0:T(8,128)(2,1)S(1)} %bitcast.112, s32[1024]{0:T(1024)S(1)} %fusion.11), kind=kOutput, calls=%fused_computation.4 | convolution fusion | flops 4299161600 | bytes 6295552 | tf_op jit(solution)/shard_map/dot_general | solution.py:52
  66.4 11.6 %reshape.122 = bf16[64,32,16,64]{3,2,1,0:T(8,128)(2,1)} reshape(bf16[2048,1024]{1,0:T(8,128)(2,1)} %fusion.2) | data formatting | bytes 8388608 | tf_op jit(solution)/shard_map/reshape | solution.py:53
  78.0 3.2 %all-gather.2.cloned.1.call-done = bf16[2048,512]{1,0:T(8,128)(2,1)} async-done(((bf16[128,512]{1,0:T(8,128)(2,1)}), bf16[2048,512]{1,0:T(8,128)(2,1)}) %all-gather.2.cloned.1.call-update) | async-done | bytes 2097168 | tf_op jit(solution)/shard_map/all_gather | solution.py:43
  81.3 1.1 constant_dynamic-slice_fusion
  82.4 5.8 %convolution_convert_fusion = bf16[4,16,64,512]{3,2,1,0:T(8,128)(2,1)S(1)} fusion(bf16[4,16,64,512]{2,3,1,0:T(8,128)(2,1)} %bitcast.103, bf16[512,512,1,1]{1,0,3,2:T(8,128)(2,1)S(1)} %bitcast.111), kind=kOutput, calls=%fused_computation.6 | convolution fusion | flops 2149580800 | bytes 8912896 | tf_op jit(solution)/shard_map/bwk,ki->bwi/dot_general | solution.py:56
  88.7 1.3 dynamic-slice_bitcast_fusion
  90.3 1.2 collective-permute-done
  91.5 1.9 fusion.5
  93.4 0.9 dynamic-slice_bitcast_fusion.3
  94.3 1.2 collective-permute-start.1
  95.4 2.6 %fusion.4 = bf16[2,16,64,256]{3,2,1,0:T(8,128)(2,1)} fusion(bf16[2,16,64,256]{3,2,1,0:T(8,128)(2,1)} %collective-permute-done.2, bf16[2,2,16,64,256]{4,3,2,1,0:T(8,128)(2,1)S(1)} %bitcast.108, s32[]{:T(128)S(6)} %select_n.146), kind=kLoop, calls=%fused_computation.9 | loop fusion | flops 2097152 | bytes 3145732 | tf_op jit(solution)/shard_map/convert_element_type | solution.py:66
  98.0 1.1 dynamic-slice_bitcast_fusion.2
  99.1 1.0 collective-permute-start.3
  100.0 9.3 %collective-permute-done.1 = bf16[16,64,256]{2,1,0:T(8,128)(2,1)} collective-permute-done((bf16[16,64,256]{2,1,0:T(8,128)(2,1)}, bf16[16,64,256]{2,1,0:T(8,128)(2,1)}, u32[]{:S(2)}, u32[]{:S(2)}) %collective-permute-start.1) | collective-permute-done | bytes 524320 | tf_op jit(solution)/shard_map/ppermute | solution.py:69
  109.4 1.2 fusion.10
  110.6 9.1 %collective-permute-done.3 = bf16[16,64,256]{2,1,0:T(8,128)(2,1)S(1)} collective-permute-done((bf16[16,64,256]{2,1,0:T(8,128)(2,1)S(1)}, bf16[16,64,256]{2,1,0:T(8,128)(2,1)S(1)}, u32[]{:S(2)}, u32[]{:S(2)}) %collective-permute-start.3) | collective-permute-done | bytes 524320 | tf_op jit(solution)/shard_map/ppermute | solution.py:69
  119.7 1.2 fusion.9
  120.9 5.9 %fusion.3 = bf16[2048,512]{0,1:T(8,128)(2,1)} fusion(bf16[16,64,2048]{2,1,0:T(8,128)(2,1)} %bitcast.116, bf16[16,64,256]{2,1,0:T(8,128)(2,1)S(1)} %fusion.9, bf16[16,64,256]{2,1,0:T(8,128)(2,1)S(1)} %fusion.10), kind=kOutput, calls=%fused_computation.5 | convolution fusion | flops 2150629376 | bytes 7340032 | tf_op jit(solution)/shard_map/nwi,nwv->vi/dot_general | solution.py:75
  126.8 2.9 %copy.24 = bf16[2048,512]{1,0:T(8,128)(2,1)S(1)} copy(bf16[2048,512]{0,1:T(8,128)(2,1)} %fusion.3) | data formatting | bytes 4194304 | tf_op jit(solution)/shard_map/convert_element_type | solution.py:75
  130.1 1.6 collective-permute-start.4
  132.3 2.9 %collective-permute-done.4 = bf16[256,256]{1,0:T(8,128)(2,1)S(1)} collective-permute-done((bf16[256,256]{1,0:T(8,128)(2,1)S(1)}, bf16[256,256]{1,0:T(8,128)(2,1)S(1)}, u32[]{:S(2)}, u32[]{:S(2)}) %collective-permute-start.4) | collective-permute-done | bytes 131104 | tf_op jit(solution)/shard_map/ppermute | solution.py:89
  135.2 1.6 collective-permute-start.5
  137.4 2.8 %collective-permute-done.5 = bf16[256,256]{1,0:T(8,128)(2,1)S(1)} collective-permute-done((bf16[256,256]{1,0:T(8,128)(2,1)S(1)}, bf16[256,256]{1,0:T(8,128)(2,1)S(1)}, u32[]{:S(2)}, u32[]{:S(2)}) %collective-permute-start.5) | collective-permute-done | bytes 131104 | tf_op jit(solution)/shard_map/ppermute | solution.py:89
  140.3 1.6 collective-permute-start.6
  142.2 1.3 collective-permute-start.13
  143.5 2.8 %collective-permute-done.6 = bf16[256,256]{1,0:T(8,128)(2,1)S(1)} collective-permute-done((bf16[256,256]{1,0:T(8,128)(2,1)S(1)}, bf16[256,256]{1,0:T(8,128)(2,1)S(1)}, u32[]{:S(2)}, u32[]{:S(2)}) %collective-permute-start.6) | collective-permute-done | bytes 131104 | tf_op jit(solution)/shard_map/ppermute | solution.py:89
  146.4 1.3 collective-permute-start.7
  147.7 0.9 collective-permute-done.13
  148.6 1.3 collective-permute-start.14
  149.8 3.7 %collective-permute-done.7 = bf16[256,256]{1,0:T(8,128)(2,1)S(1)} collective-permute-done((bf16[256,256]{1,0:T(8,128)(2,1)S(1)}, bf16[256,256]{1,0:T(8,128)(2,1)S(1)}, u32[]{:S(2)}, u32[]{:S(2)}) %collective-permute-start.7) | collective-permute-done | bytes 131104 | tf_op jit(solution)/shard_map/ppermute | solution.py:89
  153.6 1.6 collective-permute-start.8
  155.6 1.9 collective-permute-start.15
  157.5 3.4 %collective-permute-done.8 = bf16[256,256]{1,0:T(8,128)(2,1)S(1)} collective-permute-done((bf16[256,256]{1,0:T(8,128)(2,1)S(1)}, bf16[256,256]{1,0:T(8,128)(2,1)S(1)}, u32[]{:S(2)}, u32[]{:S(2)}) %collective-permute-start.8) | collective-permute-done | bytes 131104 | tf_op jit(solution)/shard_map/ppermute | solution.py:89
  160.9 1.5 collective-permute-start.9
  162.4 1.5 collective-permute-done.15
  164.1 2.8 %collective-permute-done.9 = bf16[256,256]{1,0:T(8,128)(2,1)S(1)} collective-permute-done((bf16[256,256]{1,0:T(8,128)(2,1)S(1)}, bf16[256,256]{1,0:T(8,128)(2,1)S(1)}, u32[]{:S(2)}, u32[]{:S(2)}) %collective-permute-start.9) | collective-permute-done | bytes 131104 | tf_op jit(solution)/shard_map/ppermute | solution.py:89
  167.0 1.6 collective-permute-start.10
  168.6 1.5 collective-permute-done.16
  170.4 2.8 %collective-permute-done.10 = bf16[256,256]{1,0:T(8,128)(2,1)S(1)} collective-permute-done((bf16[256,256]{1,0:T(8,128)(2,1)S(1)}, bf16[256,256]{1,0:T(8,128)(2,1)S(1)}, u32[]{:S(2)}, u32[]{:S(2)}) %collective-permute-start.10) | collective-permute-done | bytes 131104 | tf_op jit(solution)/shard_map/ppermute | solution.py:89
  173.3 2.9 %collective-permute-done.17 = bf16[256,256]{1,0:T(8,128)(2,1)S(1)} collective-permute-done((bf16[256,256]{1,0:T(8,128)(2,1)S(1)}, bf16[256,256]{1,0:T(8,128)(2,1)S(1)}, u32[]{:S(2)}, u32[]{:S(2)}) %collective-permute-start.17) | collective-permute-done | bytes 131104 | tf_op jit(solution)/shard_map/ppermute | solution.py:89
  176.2 13.2 %all_to_all.10 = bf16[16,16,512]{2,1,0:T(8,128)(2,1)S(1)} all-to-all(bf16[16,16,512]{2,1,0:T(8,128)(2,1)S(1)} %bitcast.113), channel_id=1, replica_groups=mesh['tensor'=2,'row'=16,'col'=8] {'row'}, dimensions={0} | all-to-all | bytes 524288 | tf_op jit(solution)/shard_map/all_to_all | solution.py:94
  189.4 0.9 copy.31
  (46 shorter events, 6.5 us)
Async XLA Ops:
  6.5 74.7 %all-gather.2.cloned.1.call-start = ((), (), s32[]{:S(2)}) async-start(), calls=%async_computation.2 | async-start | bytes 2228224 | tf_op jit(solution)/shard_map/all_gather | solution.py:43
  15.0 44.1 %all-to-all-start = ((bf16[32,33,1024]{2,1,0:T(8,128)(2,1)}), bf16[32,33,1024]{2,1,0:T(8,128)(2,1)S(1)}, u32[]{:S(2)}, u32[]{:S(2)}) async-start(bf16[32,33,1024]{2,1,0:T(8,128)(2,1)} %copy.21), calls=%async_computation | async-start | bytes 5242880 | tf_op jit(solution)/shard_map/all_to_all | solution.py:39
  88.5 1.7 copy-start
  88.6 2.9 %collective-permute-start = (bf16[2,16,64,256]{3,2,1,0:T(8,128)(2,1)S(1)}, bf16[2,16,64,256]{3,2,1,0:T(8,128)(2,1)}, u32[]{:S(2)}, u32[]{:S(2)}) collective-permute-start(bf16[2,16,64,256]{3,2,1,0:T(8,128)(2,1)S(1)} %dynamic-slice_bitcast_fusion.1), channel_id=1, source_target_pairs={{0,128},{128,0},{1,129},{129,1},{2,130},{130,2},{3,131},{131,3},{4... | collective-permute-start | bytes 3145736 | tf_op jit(solution)/shard_map/ppermute | solution.py:65
  90.2 5.3 %collective-permute-start.2 = (bf16[2,16,64,256]{3,2,1,0:T(8,128)(2,1)}, bf16[2,16,64,256]{3,2,1,0:T(8,128)(2,1)}, u32[]{:S(2)}, u32[]{:S(2)}) collective-permute-start(bf16[2,16,64,256]{3,2,1,0:T(8,128)(2,1)} %dynamic-slice_bitcast_fusion), channel_id=1, source_target_pairs={{0,128},{128,0},{1,129},{129,1},{2,130},{130,2},{3,131},{131,3},{4... | collective-permute-start | bytes 3145736 | tf_op jit(solution)/shard_map/ppermute | solution.py:65
  94.3 15.1 %collective-permute-start.1 = (bf16[16,64,256]{2,1,0:T(8,128)(2,1)}, bf16[16,64,256]{2,1,0:T(8,128)(2,1)}, u32[]{:S(2)}, u32[]{:S(2)}) collective-permute-start(bf16[16,64,256]{2,1,0:T(8,128)(2,1)} %dynamic-slice_bitcast_fusion.3), channel_id=1, source_target_pairs={{0,8},{8,0},{16,24},{24,16},{32,40},{40,32},{48,56},{56,48},{64,72... | collective-permute-start | bytes 1572872 | tf_op jit(solution)/shard_map/ppermute | solution.py:69
  99.1 20.6 %collective-permute-start.3 = (bf16[16,64,256]{2,1,0:T(8,128)(2,1)S(1)}, bf16[16,64,256]{2,1,0:T(8,128)(2,1)S(1)}, u32[]{:S(2)}, u32[]{:S(2)}) collective-permute-start(bf16[16,64,256]{2,1,0:T(8,128)(2,1)S(1)} %dynamic-slice_bitcast_fusion.2), channel_id=1, source_target_pairs={{0,8},{8,0},{16,24},{24,16},{32,40},{40,32},{48,56},{56,48},{64,72... | collective-permute-start | bytes 1572872 | tf_op jit(solution)/shard_map/ppermute | solution.py:69
  130.1 5.0 %collective-permute-start.4 = (bf16[256,256]{1,0:T(8,128)(2,1)S(1)}, bf16[256,256]{1,0:T(8,128)(2,1)S(1)}, u32[]{:S(2)}, u32[]{:S(2)}) collective-permute-start(bf16[256,256]{1,0:T(8,128)(2,1)S(1)} %dynamic-slice_bitcast_fusion.5), channel_id=1, source_target_pairs={{0,1},{1,2},{2,3},{3,4},{4,5},{5,6},{6,7},{7,0},{8,9},{9,10},{10,1... | collective-permute-start | bytes 393224 | tf_op jit(solution)/shard_map/ppermute | solution.py:89
  131.8 5.1 %collective-permute-start.11 = (bf16[256,256]{1,0:T(8,128)(2,1)S(1)}, bf16[256,256]{1,0:T(8,128)(2,1)S(1)}, u32[]{:S(2)}, u32[]{:S(2)}) collective-permute-start(bf16[256,256]{1,0:T(8,128)(2,1)S(1)} %dynamic-slice_bitcast_fusion.4), channel_id=1, source_target_pairs={{0,7},{1,0},{2,1},{3,2},{4,3},{5,4},{6,5},{7,6},{8,15},{9,8},{10,9... | collective-permute-start | bytes 393224 | tf_op jit(solution)/shard_map/ppermute | solution.py:89
  135.2 5.0 %collective-permute-start.5 = (bf16[256,256]{1,0:T(8,128)(2,1)S(1)}, bf16[256,256]{1,0:T(8,128)(2,1)S(1)}, u32[]{:S(2)}, u32[]{:S(2)}) collective-permute-start(bf16[256,256]{1,0:T(8,128)(2,1)S(1)} %fusion.26), channel_id=1, source_target_pairs={{0,1},{1,2},{2,3},{3,4},{4,5},{5,6},{6,7},{7,0},{8,9},{9,10},{10,1... | collective-permute-start | bytes 393224 | tf_op jit(solution)/shard_map/ppermute | solution.py:89
  136.9 5.3 %collective-permute-start.12 = (bf16[256,256]{1,0:T(8,128)(2,1)S(1)}, bf16[256,256]{1,0:T(8,128)(2,1)S(1)}, u32[]{:S(2)}, u32[]{:S(2)}) collective-permute-start(bf16[256,256]{1,0:T(8,128)(2,1)S(1)} %fusion.19), channel_id=1, source_target_pairs={{0,7},{1,0},{2,1},{3,2},{4,3},{5,4},{6,5},{7,6},{8,15},{9,8},{10,9... | collective-permute-start | bytes 393224 | tf_op jit(solution)/shard_map/ppermute | solution.py:89
  140.3 6.0 %collective-permute-start.6 = (bf16[256,256]{1,0:T(8,128)(2,1)S(1)}, bf16[256,256]{1,0:T(8,128)(2,1)S(1)}, u32[]{:S(2)}, u32[]{:S(2)}) collective-permute-start(bf16[256,256]{1,0:T(8,128)(2,1)S(1)} %fusion.25), channel_id=1, source_target_pairs={{0,1},{1,2},{2,3},{3,4},{4,5},{5,6},{6,7},{7,0},{8,9},{9,10},{10,1... | collective-permute-start | bytes 393224 | tf_op jit(solution)/shard_map/ppermute | solution.py:89
  142.2 6.3 %collective-permute-start.13 = (bf16[256,256]{1,0:T(8,128)(2,1)S(1)}, bf16[256,256]{1,0:T(8,128)(2,1)S(1)}, u32[]{:S(2)}, u32[]{:S(2)}) collective-permute-start(bf16[256,256]{1,0:T(8,128)(2,1)S(1)} %fusion.18), channel_id=1, source_target_pairs={{0,7},{1,0},{2,1},{3,2},{4,3},{5,4},{6,5},{7,6},{8,15},{9,8},{10,9... | collective-permute-start | bytes 393224 | tf_op jit(solution)/shard_map/ppermute | solution.py:89
  146.4 7.1 %collective-permute-start.7 = (bf16[256,256]{1,0:T(8,128)(2,1)S(1)}, bf16[256,256]{1,0:T(8,128)(2,1)S(1)}, u32[]{:S(2)}, u32[]{:S(2)}) collective-permute-start(bf16[256,256]{1,0:T(8,128)(2,1)S(1)} %fusion.24), channel_id=1, source_target_pairs={{0,1},{1,2},{2,3},{3,4},{4,5},{5,6},{6,7},{7,0},{8,9},{9,10},{10,1... | collective-permute-start | bytes 393224 | tf_op jit(solution)/shard_map/ppermute | solution.py:89
  148.6 7.0 %collective-permute-start.14 = (bf16[256,256]{1,0:T(8,128)(2,1)S(1)}, bf16[256,256]{1,0:T(8,128)(2,1)S(1)}, u32[]{:S(2)}, u32[]{:S(2)}) collective-permute-start(bf16[256,256]{1,0:T(8,128)(2,1)S(1)} %fusion.17), channel_id=1, source_target_pairs={{0,7},{1,0},{2,1},{3,2},{4,3},{5,4},{6,5},{7,6},{8,15},{9,8},{10,9... | collective-permute-start | bytes 393224 | tf_op jit(solution)/shard_map/ppermute | solution.py:89
  153.6 7.3 %collective-permute-start.8 = (bf16[256,256]{1,0:T(8,128)(2,1)S(1)}, bf16[256,256]{1,0:T(8,128)(2,1)S(1)}, u32[]{:S(2)}, u32[]{:S(2)}) collective-permute-start(bf16[256,256]{1,0:T(8,128)(2,1)S(1)} %fusion.23), channel_id=1, source_target_pairs={{0,1},{1,2},{2,3},{3,4},{4,5},{5,6},{6,7},{7,0},{8,9},{9,10},{10,1... | collective-permute-start | bytes 393224 | tf_op jit(solution)/shard_map/ppermute | solution.py:89
  155.6 8.3 %collective-permute-start.15 = (bf16[256,256]{1,0:T(8,128)(2,1)S(1)}, bf16[256,256]{1,0:T(8,128)(2,1)S(1)}, u32[]{:S(2)}, u32[]{:S(2)}) collective-permute-start(bf16[256,256]{1,0:T(8,128)(2,1)S(1)} %fusion.16), channel_id=1, source_target_pairs={{0,7},{1,0},{2,1},{3,2},{4,3},{5,4},{6,5},{7,6},{8,15},{9,8},{10,9... | collective-permute-start | bytes 393224 | tf_op jit(solution)/shard_map/ppermute | solution.py:89
  160.9 6.0 %collective-permute-start.9 = (bf16[256,256]{1,0:T(8,128)(2,1)S(1)}, bf16[256,256]{1,0:T(8,128)(2,1)S(1)}, u32[]{:S(2)}, u32[]{:S(2)}) collective-permute-start(bf16[256,256]{1,0:T(8,128)(2,1)S(1)} %fusion.22), channel_id=1, source_target_pairs={{0,1},{1,2},{2,3},{3,4},{4,5},{5,6},{6,7},{7,0},{8,9},{9,10},{10,1... | collective-permute-start | bytes 393224 | tf_op jit(solution)/shard_map/ppermute | solution.py:89
  163.9 6.2 %collective-permute-start.16 = (bf16[256,256]{1,0:T(8,128)(2,1)S(1)}, bf16[256,256]{1,0:T(8,128)(2,1)S(1)}, u32[]{:S(2)}, u32[]{:S(2)}) collective-permute-start(bf16[256,256]{1,0:T(8,128)(2,1)S(1)} %fusion.15), channel_id=1, source_target_pairs={{0,7},{1,0},{2,1},{3,2},{4,3},{5,4},{6,5},{7,6},{8,15},{9,8},{10,9... | collective-permute-start | bytes 393224 | tf_op jit(solution)/shard_map/ppermute | solution.py:89
  167.0 6.2 %collective-permute-start.10 = (bf16[256,256]{1,0:T(8,128)(2,1)S(1)}, bf16[256,256]{1,0:T(8,128)(2,1)S(1)}, u32[]{:S(2)}, u32[]{:S(2)}) collective-permute-start(bf16[256,256]{1,0:T(8,128)(2,1)S(1)} %fusion.21), channel_id=1, source_target_pairs={{0,1},{1,2},{2,3},{3,4},{4,5},{5,6},{6,7},{7,0},{8,9},{9,10},{10,1... | collective-permute-start | bytes 393224 | tf_op jit(solution)/shard_map/ppermute | solution.py:89
  170.2 5.9 %collective-permute-start.17 = (bf16[256,256]{1,0:T(8,128)(2,1)S(1)}, bf16[256,256]{1,0:T(8,128)(2,1)S(1)}, u32[]{:S(2)}, u32[]{:S(2)}) collective-permute-start(bf16[256,256]{1,0:T(8,128)(2,1)S(1)} %fusion.14), channel_id=1, source_target_pairs={{0,7},{1,0},{2,1},{3,2},{4,3},{5,4},{6,5},{7,6},{8,15},{9,8},{10,9... | collective-permute-start | bytes 393224 | tf_op jit(solution)/shard_map/ppermute | solution.py:89
Sparse Core Ops, SparseCore 0:
  9.8 71.4 all-gather.1

commit v7 on v5

--- a/solution.py
+++ b/solution.py
@@ -74,8 +74,20 @@
     virt = virtual_coeff.reshape(NBC, TB, NV)
     z = jnp.einsum("nwi,nwv->vi", occ_done, virt, preferred_element_type=jnp.float32).astype(jnp.bfloat16)
     z = z.reshape(row_count, col_count, chunk, NOCC).transpose(1, 0, 2, 3)
-    z = z.reshape(col_count * row_count * chunk, NOCC)
-    w = lax.psum_scatter(z, "col", scatter_dimension=0, tiled=True).reshape(row_count, chunk, NOCC)
+    z = z.reshape(col_count, row_count * chunk, NOCC)
+    lanes_half = NOCC // 2
+    native = lax.psum_scatter(
+        z[:, :, :lanes_half].reshape(col_count * row_count * chunk, lanes_half), "col",
+        scatter_dimension=0, tiled=True,
+    )
+    ring = z[:, :, lanes_half:]
+    acc = lax.dynamic_index_in_dim(ring, (col_at + 1) % col_count, axis=0, keepdims=False)
+    perm = [(i, (i - 1) % col_count) for i in range(col_count)]
+    for hop in range(col_count - 1):
+        got = lax.ppermute(acc, "col", perm=perm)
+        own = lax.dynamic_index_in_dim(ring, (col_at + hop + 2) % col_count, axis=0, keepdims=False)
+        acc = (got.astype(jnp.float32) + own.astype(jnp.float32)).astype(jnp.bfloat16)
+    w = jnp.concatenate([native, acc], axis=-1).reshape(row_count, chunk, NOCC)
 
     got_rows = lax.all_to_all(w, "row", split_axis=0, concat_axis=0, tiled=True)
     out = got_rows.reshape(PB, 2, chunk, NOCC).transpose(2, 1, 0, 3)

time: 196 us -> 204 us (1.041); the launches traced: 196 us -> 201 us
  starting transfers between devices: 9.68 us -> 30.7 us
  waiting for transfers between devices: 103 us -> 87.7 us
    reduce_scatter x1, waiting for transfers between devices: 41.3 us -> 0.02 us  [shards(): lax.psum_scatter(z[:, :, :lanes_half].reshape(col_count * row_count * chu...]
    ppermute x0 -> x7, waiting for transfers between devices: none -> 26.4 us  [shards(): got = lax.ppermute(acc, 'col', perm=perm)]
    ppermute x0 -> x7, starting transfers between devices: none -> 21 us  [shards(): got = lax.ppermute(acc, 'col', perm=perm)]
  transfers between devices with their start and end apart: 7 -> 14, of which waited for: 6 -> 12; matrix products, arithmetic and copies ran while one was open for 17% -> 17% of each run, Pallas kernels for 0% -> 0%
where the time goes in v7:
time: 204 us; the launch traced here: 201 us
  waiting for transfers between devices  87.7 us (43%)
  starting transfers between devices  30.7 us (15%)
  local copies, waits for them, and re-layouts  28.4 us (14%)
  matrix products  17.7 us (9%)
  blocking collectives  14.1 us (7%)
  between operations  13.7 us (7%)
  other arithmetic  9.24 us (5%)
    all_to_all x1, waiting for transfers between devices, shards(): recv = lax.all_to_all(send, owners, split_axis=0, concat_axis=0, tiled=True)  36.7 us
    ppermute x7, waiting for transfers between devices, shards(): got = lax.ppermute(acc, 'col', perm=perm)  26.4 us
    ppermute x7, starting transfers between devices, shards(): got = lax.ppermute(acc, 'col', perm=perm)  21 us
    ppermute x2, waiting for transfers between devices, shards(): lax.ppermute(give, 'row', perm=[(i, i ^ 1) for i in range(row_count)])  19.5 us
    all_to_all x1, blocking collectives, shards(): got_rows = lax.all_to_all(w, 'row', split_axis=0, concat_axis=0, tiled=True)  14.1 us
    reshape x1, local copies, waits for them, and re-layouts, shards(): dense.reshape(aux_blocks * NBC, mu_blocks, qsize, TB).transpose(0, 3, 1, 2)  11.6 us
    all_to_all x1, starting transfers between devices, shards(): recv = lax.all_to_all(send, owners, split_axis=0, concat_axis=0, tiled=True)  7.32 us
    dot_general x1, matrix products, shards(): jnp.dot(selector, slices, preferred_element_type=jnp.float32)  6.04 us
  transfers between devices with their start and end apart: 14, of which 12 were waited for; matrix products, arithmetic and copies ran while one was open for 17% of the time, Pallas kernels for 0%

profile of v7, /device:TPU:32, one launch (start us, length us, event | category | flops | bytes accessed | tf_op | source)
XLA Modules:
  0.0 201.5 jit_solution(5100941275238449032)
XLA Ops:
  6.5 0.7 all-gather.2.cloned.1.call-update
  7.3 0.7 convert.25
  8.0 0.7 subtract_convert_fusion
  8.9 3.1 %reshape.109 = bf16[32,32,1024]{2,1,0:T(8,128)(2,1)S(1)} reshape(bf16[32,8,4096]{2,1,0:T(8,128)(2,1)} %param.4) | data formatting | bytes 4194304 | tf_op jit(solution)/shard_map/reshape | solution.py:33
  12.2 2.8 %copy.21 = bf16[32,33,1024]{2,1,0:T(8,128)(2,1)} copy(bf16[32,33,1024]{2,0,1:T(8,128)(2,1)S(1)} %pad_maximum_fusion) | data formatting | bytes 4325376 | tf_op jit(solution)/shard_map/concatenate | solution.py:38
  15.0 7.3 %all-to-all-start = ((bf16[32,33,1024]{2,1,0:T(8,128)(2,1)}), bf16[32,33,1024]{2,1,0:T(8,128)(2,1)S(1)}, u32[]{:S(2)}, u32[]{:S(2)}) async-start(bf16[32,33,1024]{2,1,0:T(8,128)(2,1)} %copy.21), calls=%async_computation | async-start | bytes 5242880 | tf_op jit(solution)/shard_map/all_to_all | solution.py:39
  22.4 36.7 %all-to-all-done = bf16[32,33,1024]{2,1,0:T(8,128)(2,1)S(1)} async-done(((bf16[32,33,1024]{2,1,0:T(8,128)(2,1)}), bf16[32,33,1024]{2,1,0:T(8,128)(2,1)S(1)}, u32[]{:S(2)}, u32[]{:S(2)}) %all-to-all-start) | async-done | bytes 2162720 | tf_op jit(solution)/shard_map/all_to_all | solution.py:39
  59.1 0.5 reshape.123
  59.6 0.2 slice.43
  59.9 0.5 fusion.11
  60.4 6.0 %fusion.2 = bf16[2048,1024]{1,0:T(8,128)(2,1)} fusion(bf16[1024,1024]{1,0:T(8,128)(2,1)S(1)} %bitcast.91, s32[1024]{0:T(1024)S(1)} %fusion.11), kind=kOutput, calls=%fused_computation.4 | convolution fusion | flops 4299161600 | bytes 6295552 | tf_op jit(solution)/shard_map/dot_general | solution.py:52
  66.4 11.6 %reshape.111 = bf16[64,32,16,64]{3,2,1,0:T(8,128)(2,1)} reshape(bf16[2048,1024]{1,0:T(8,128)(2,1)} %fusion.2) | data formatting | bytes 8388608 | tf_op jit(solution)/shard_map/reshape | solution.py:53
  78.0 3.2 %all-gather.2.cloned.1.call-done = bf16[2048,512]{1,0:T(8,128)(2,1)} async-done(((bf16[128,512]{1,0:T(8,128)(2,1)}), bf16[2048,512]{1,0:T(8,128)(2,1)}) %all-gather.2.cloned.1.call-update) | async-done | bytes 2097168 | tf_op jit(solution)/shard_map/all_gather | solution.py:43
  81.2 1.1 constant_dynamic-slice_fusion
  82.3 5.8 %convolution_convert_fusion = bf16[4,16,64,512]{3,2,1,0:T(8,128)(2,1)S(1)} fusion(bf16[4,16,64,512]{2,3,1,0:T(8,128)(2,1)} %bitcast.81, bf16[512,512,1,1]{1,0,3,2:T(8,128)(2,1)S(1)} %bitcast.90), kind=kOutput, calls=%fused_computation.6 | convolution fusion | flops 2149580800 | bytes 8912896 | tf_op jit(solution)/shard_map/bwk,ki->bwi/dot_general | solution.py:56
  88.1 0.4 fusion.22
  88.6 1.3 dynamic-slice_bitcast_fusion
  90.2 1.2 collective-permute-done
  91.4 1.9 fusion.5
  93.3 0.9 dynamic-slice_bitcast_fusion.3
  94.2 1.2 collective-permute-start.1
  95.4 1.6 fusion.4
  97.0 1.0 copy-done.1
  98.0 1.0 collective-permute-start.3
  98.9 10.4 %collective-permute-done.1 = bf16[16,64,256]{2,1,0:T(8,128)(2,1)} collective-permute-done((bf16[16,64,256]{2,1,0:T(8,128)(2,1)}, bf16[16,64,256]{2,1,0:T(8,128)(2,1)}, u32[]{:S(2)}, u32[]{:S(2)}) %collective-permute-start.1) | collective-permute-done | bytes 524320 | tf_op jit(solution)/shard_map/ppermute | solution.py:69
  109.3 1.2 fusion.10
  110.5 9.1 %collective-permute-done.3 = bf16[16,64,256]{2,1,0:T(8,128)(2,1)S(1)} collective-permute-done((bf16[16,64,256]{2,1,0:T(8,128)(2,1)S(1)}, bf16[16,64,256]{2,1,0:T(8,128)(2,1)S(1)}, u32[]{:S(2)}, u32[]{:S(2)}) %collective-permute-start.3) | collective-permute-done | bytes 524320 | tf_op jit(solution)/shard_map/ppermute | solution.py:69
  119.6 1.2 fusion.9
  120.8 5.9 %fusion.3 = bf16[2048,512]{0,1:T(8,128)(2,1)} fusion(bf16[16,64,2048]{2,1,0:T(8,128)(2,1)} %bitcast.95, bf16[16,64,256]{2,1,0:T(8,128)(2,1)S(1)} %fusion.9, bf16[16,64,256]{2,1,0:T(8,128)(2,1)S(1)} %fusion.10), kind=kOutput, calls=%fused_computation.5 | convolution fusion | flops 2150629376 | bytes 7340032 | tf_op jit(solution)/shard_map/nwi,nwv->vi/dot_general | solution.py:75
  126.7 2.9 %copy.24 = bf16[2048,512]{1,0:T(8,128)(2,1)S(1)} copy(bf16[2048,512]{0,1:T(8,128)(2,1)} %fusion.3) | data formatting | bytes 4194304 | tf_op jit(solution)/shard_map/convert_element_type | solution.py:75
  129.8 1.2 fusion.23
  131.0 0.5 collective-permute-start.4
  131.5 4.5 %collective-permute-done.4 = bf16[256,256]{1,0:T(8,128)(2,1)S(1)} collective-permute-done((bf16[256,256]{1,0:T(8,128)(2,1)S(1)}, bf16[256,256]{1,0:T(8,128)(2,1)S(1)}, u32[]{:S(2)}, u32[]{:S(2)}) %collective-permute-start.4) | collective-permute-done | bytes 131104 | tf_op jit(solution)/shard_map/ppermute | solution.py:87
  136.1 1.4 collective-permute-start.5
  137.5 3.6 %collective-permute-done.5 = bf16[256,256]{1,0:T(8,128)(2,1)S(1)} collective-permute-done((bf16[256,256]{1,0:T(8,128)(2,1)S(1)}, bf16[256,256]{1,0:T(8,128)(2,1)S(1)}, u32[]{:S(2)}, u32[]{:S(2)}) %collective-permute-start.5) | collective-permute-done | bytes 131104 | tf_op jit(solution)/shard_map/ppermute | solution.py:87
  141.2 2.6 %collective-permute-start.6 = (bf16[256,256]{1,0:T(8,128)(2,1)S(1)}, bf16[256,256]{1,0:T(8,128)(2,1)S(1)}, u32[]{:S(2)}, u32[]{:S(2)}) collective-permute-start(bf16[256,256]{1,0:T(8,128)(2,1)S(1)} %fusion.18), channel_id=1, source_target_pairs={{0,7},{1,0},{2,1},{3,2},{4,3},{5,4},{6,5},{7,6},{8,15},{9,8},{10,9... | collective-permute-start | bytes 393224 | tf_op jit(solution)/shard_map/ppermute | solution.py:87
  143.8 2.7 %collective-permute-done.6 = bf16[256,256]{1,0:T(8,128)(2,1)S(1)} collective-permute-done((bf16[256,256]{1,0:T(8,128)(2,1)S(1)}, bf16[256,256]{1,0:T(8,128)(2,1)S(1)}, u32[]{:S(2)}, u32[]{:S(2)}) %collective-permute-start.6) | collective-permute-done | bytes 131104 | tf_op jit(solution)/shard_map/ppermute | solution.py:87
  146.5 5.7 %collective-permute-start.7 = (bf16[256,256]{1,0:T(8,128)(2,1)S(1)}, bf16[256,256]{1,0:T(8,128)(2,1)S(1)}, u32[]{:S(2)}, u32[]{:S(2)}) collective-permute-start(bf16[256,256]{1,0:T(8,128)(2,1)S(1)} %fusion.17), channel_id=1, source_target_pairs={{0,7},{1,0},{2,1},{3,2},{4,3},{5,4},{6,5},{7,6},{8,15},{9,8},{10,9... | collective-permute-start | bytes 393224 | tf_op jit(solution)/shard_map/ppermute | solution.py:87
  152.3 5.0 %collective-permute-done.7 = bf16[256,256]{1,0:T(8,128)(2,1)S(1)} collective-permute-done((bf16[256,256]{1,0:T(8,128)(2,1)S(1)}, bf16[256,256]{1,0:T(8,128)(2,1)S(1)}, u32[]{:S(2)}, u32[]{:S(2)}) %collective-permute-start.7) | collective-permute-done | bytes 131104 | tf_op jit(solution)/shard_map/ppermute | solution.py:87
  157.4 3.8 %collective-permute-start.8 = (bf16[256,256]{1,0:T(8,128)(2,1)S(1)}, bf16[256,256]{1,0:T(8,128)(2,1)S(1)}, u32[]{:S(2)}, u32[]{:S(2)}) collective-permute-start(bf16[256,256]{1,0:T(8,128)(2,1)S(1)} %fusion.16), channel_id=1, source_target_pairs={{0,7},{1,0},{2,1},{3,2},{4,3},{5,4},{6,5},{7,6},{8,15},{9,8},{10,9... | collective-permute-start | bytes 393224 | tf_op jit(solution)/shard_map/ppermute | solution.py:87
  161.2 5.0 %collective-permute-done.8 = bf16[256,256]{1,0:T(8,128)(2,1)S(1)} collective-permute-done((bf16[256,256]{1,0:T(8,128)(2,1)S(1)}, bf16[256,256]{1,0:T(8,128)(2,1)S(1)}, u32[]{:S(2)}, u32[]{:S(2)}) %collective-permute-start.8) | collective-permute-done | bytes 131104 | tf_op jit(solution)/shard_map/ppermute | solution.py:87
  166.2 3.3 %collective-permute-start.9 = (bf16[256,256]{1,0:T(8,128)(2,1)S(1)}, bf16[256,256]{1,0:T(8,128)(2,1)S(1)}, u32[]{:S(2)}, u32[]{:S(2)}) collective-permute-start(bf16[256,256]{1,0:T(8,128)(2,1)S(1)} %fusion.15), channel_id=1, source_target_pairs={{0,7},{1,0},{2,1},{3,2},{4,3},{5,4},{6,5},{7,6},{8,15},{9,8},{10,9... | collective-permute-start | bytes 393224 | tf_op jit(solution)/shard_map/ppermute | solution.py:87
  169.5 3.1 %collective-permute-done.9 = bf16[256,256]{1,0:T(8,128)(2,1)S(1)} collective-permute-done((bf16[256,256]{1,0:T(8,128)(2,1)S(1)}, bf16[256,256]{1,0:T(8,128)(2,1)S(1)}, u32[]{:S(2)}, u32[]{:S(2)}) %collective-permute-start.9) | collective-permute-done | bytes 131104 | tf_op jit(solution)/shard_map/ppermute | solution.py:87
  172.7 3.5 %collective-permute-start.10 = (bf16[256,256]{1,0:T(8,128)(2,1)S(1)}, bf16[256,256]{1,0:T(8,128)(2,1)S(1)}, u32[]{:S(2)}, u32[]{:S(2)}) collective-permute-start(bf16[256,256]{1,0:T(8,128)(2,1)S(1)} %fusion.14), channel_id=1, source_target_pairs={{0,7},{1,0},{2,1},{3,2},{4,3},{5,4},{6,5},{7,6},{8,15},{9,8},{10,9... | collective-permute-start | bytes 393224 | tf_op jit(solution)/shard_map/ppermute | solution.py:87
  176.2 2.5 %collective-permute-done.10 = bf16[256,256]{1,0:T(8,128)(2,1)S(1)} collective-permute-done((bf16[256,256]{1,0:T(8,128)(2,1)S(1)}, bf16[256,256]{1,0:T(8,128)(2,1)S(1)}, u32[]{:S(2)}, u32[]{:S(2)}) %collective-permute-start.10) | collective-permute-done | bytes 131104 | tf_op jit(solution)/shard_map/ppermute | solution.py:87
  178.8 0.9 pad_maximum_fusion.1
  179.7 14.1 %all_to_all.10 = bf16[16,16,512]{2,1,0:T(8,128)(2,1)S(1)} all-to-all(bf16[16,16,512]{2,1,0:T(8,128)(2,1)S(1)} %bitcast.92), channel_id=1, replica_groups=mesh['tensor'=2,'row'=16,'col'=8] {'row'}, dimensions={0} | all-to-all | bytes 524288 | tf_op jit(solution)/shard_map/all_to_all | solution.py:92
  193.8 0.9 copy.31
  (29 shorter events, 1.6 us)
Async XLA Ops:
  6.5 74.7 %all-gather.2.cloned.1.call-start = ((), (), s32[]{:S(2)}) async-start(), calls=%async_computation.3 | async-start | bytes 2228224 | tf_op jit(solution)/shard_map/all_gather | solution.py:43
  15.0 44.1 %all-to-all-start = ((bf16[32,33,1024]{2,1,0:T(8,128)(2,1)}), bf16[32,33,1024]{2,1,0:T(8,128)(2,1)S(1)}, u32[]{:S(2)}, u32[]{:S(2)}) async-start(bf16[32,33,1024]{2,1,0:T(8,128)(2,1)} %copy.21), calls=%async_computation | async-start | bytes 5242880 | tf_op jit(solution)/shard_map/all_to_all | solution.py:39
  22.3 156.5 %reduce-scatter.2.cloned.1.call-start = ((), (), s32[]{:S(2)}) async-start(), calls=%async_computation.4 | async-start | bytes 1179648 | tf_op jit(solution)/shard_map/reduce_scatter | solution.py:79
  88.4 1.6 copy-start
  88.5 2.9 %collective-permute-start = (bf16[2,16,64,256]{3,2,1,0:T(8,128)(2,1)S(1)}, bf16[2,16,64,256]{3,2,1,0:T(8,128)(2,1)}, u32[]{:S(2)}, u32[]{:S(2)}) collective-permute-start(bf16[2,16,64,256]{3,2,1,0:T(8,128)(2,1)S(1)} %dynamic-slice_bitcast_fusion.1), channel_id=1, source_target_pairs={{0,128},{128,0},{1,129},{129,1},{2,130},{130,2},{3,131},{131,3},{4... | collective-permute-start | bytes 3145736 | tf_op jit(solution)/shard_map/ppermute | solution.py:65
  90.1 5.3 %collective-permute-start.2 = (bf16[2,16,64,256]{3,2,1,0:T(8,128)(2,1)}, bf16[2,16,64,256]{3,2,1,0:T(8,128)(2,1)}, u32[]{:S(2)}, u32[]{:S(2)}) collective-permute-start(bf16[2,16,64,256]{3,2,1,0:T(8,128)(2,1)} %dynamic-slice_bitcast_fusion), channel_id=1, source_target_pairs={{0,128},{128,0},{1,129},{129,1},{2,130},{130,2},{3,131},{131,3},{4... | collective-permute-start | bytes 3145736 | tf_op jit(solution)/shard_map/ppermute | solution.py:65
  94.2 15.1 %collective-permute-start.1 = (bf16[16,64,256]{2,1,0:T(8,128)(2,1)}, bf16[16,64,256]{2,1,0:T(8,128)(2,1)}, u32[]{:S(2)}, u32[]{:S(2)}) collective-permute-start(bf16[16,64,256]{2,1,0:T(8,128)(2,1)} %dynamic-slice_bitcast_fusion.3), channel_id=1, source_target_pairs={{0,8},{8,0},{16,24},{24,16},{32,40},{40,32},{48,56},{56,48},{64,72... | collective-permute-start | bytes 1572872 | tf_op jit(solution)/shard_map/ppermute | solution.py:69
  97.0 1.0 copy-start.1
  98.0 21.6 %collective-permute-start.3 = (bf16[16,64,256]{2,1,0:T(8,128)(2,1)S(1)}, bf16[16,64,256]{2,1,0:T(8,128)(2,1)S(1)}, u32[]{:S(2)}, u32[]{:S(2)}) collective-permute-start(bf16[16,64,256]{2,1,0:T(8,128)(2,1)S(1)} %dynamic-slice_bitcast_fusion.2), channel_id=1, source_target_pairs={{0,8},{8,0},{16,24},{24,16},{32,40},{40,32},{48,56},{56,48},{64,72... | collective-permute-start | bytes 1572872 | tf_op jit(solution)/shard_map/ppermute | solution.py:69
  131.0 5.0 %collective-permute-start.4 = (bf16[256,256]{1,0:T(8,128)(2,1)S(1)}, bf16[256,256]{1,0:T(8,128)(2,1)S(1)}, u32[]{:S(2)}, u32[]{:S(2)}) collective-permute-start(bf16[256,256]{1,0:T(8,128)(2,1)S(1)} %dynamic-slice_bitcast_fusion.4), channel_id=1, source_target_pairs={{0,7},{1,0},{2,1},{3,2},{4,3},{5,4},{6,5},{7,6},{8,15},{9,8},{10,9... | collective-permute-start | bytes 393224 | tf_op jit(solution)/shard_map/ppermute | solution.py:87
  136.1 5.0 %collective-permute-start.5 = (bf16[256,256]{1,0:T(8,128)(2,1)S(1)}, bf16[256,256]{1,0:T(8,128)(2,1)S(1)}, u32[]{:S(2)}, u32[]{:S(2)}) collective-permute-start(bf16[256,256]{1,0:T(8,128)(2,1)S(1)} %fusion.19), channel_id=1, source_target_pairs={{0,7},{1,0},{2,1},{3,2},{4,3},{5,4},{6,5},{7,6},{8,15},{9,8},{10,9... | collective-permute-start | bytes 393224 | tf_op jit(solution)/shard_map/ppermute | solution.py:87
  141.2 5.3 %collective-permute-start.6 = (bf16[256,256]{1,0:T(8,128)(2,1)S(1)}, bf16[256,256]{1,0:T(8,128)(2,1)S(1)}, u32[]{:S(2)}, u32[]{:S(2)}) collective-permute-start(bf16[256,256]{1,0:T(8,128)(2,1)S(1)} %fusion.18), channel_id=1, source_target_pairs={{0,7},{1,0},{2,1},{3,2},{4,3},{5,4},{6,5},{7,6},{8,15},{9,8},{10,9... | collective-permute-start | bytes 393224 | tf_op jit(solution)/shard_map/ppermute | solution.py:87
  146.5 10.8 %collective-permute-start.7 = (bf16[256,256]{1,0:T(8,128)(2,1)S(1)}, bf16[256,256]{1,0:T(8,128)(2,1)S(1)}, u32[]{:S(2)}, u32[]{:S(2)}) collective-permute-start(bf16[256,256]{1,0:T(8,128)(2,1)S(1)} %fusion.17), channel_id=1, source_target_pairs={{0,7},{1,0},{2,1},{3,2},{4,3},{5,4},{6,5},{7,6},{8,15},{9,8},{10,9... | collective-permute-start | bytes 393224 | tf_op jit(solution)/shard_map/ppermute | solution.py:87
  157.4 8.8 %collective-permute-start.8 = (bf16[256,256]{1,0:T(8,128)(2,1)S(1)}, bf16[256,256]{1,0:T(8,128)(2,1)S(1)}, u32[]{:S(2)}, u32[]{:S(2)}) collective-permute-start(bf16[256,256]{1,0:T(8,128)(2,1)S(1)} %fusion.16), channel_id=1, source_target_pairs={{0,7},{1,0},{2,1},{3,2},{4,3},{5,4},{6,5},{7,6},{8,15},{9,8},{10,9... | collective-permute-start | bytes 393224 | tf_op jit(solution)/shard_map/ppermute | solution.py:87
  166.2 6.4 %collective-permute-start.9 = (bf16[256,256]{1,0:T(8,128)(2,1)S(1)}, bf16[256,256]{1,0:T(8,128)(2,1)S(1)}, u32[]{:S(2)}, u32[]{:S(2)}) collective-permute-start(bf16[256,256]{1,0:T(8,128)(2,1)S(1)} %fusion.15), channel_id=1, source_target_pairs={{0,7},{1,0},{2,1},{3,2},{4,3},{5,4},{6,5},{7,6},{8,15},{9,8},{10,9... | collective-permute-start | bytes 393224 | tf_op jit(solution)/shard_map/ppermute | solution.py:87
  172.7 6.0 %collective-permute-start.10 = (bf16[256,256]{1,0:T(8,128)(2,1)S(1)}, bf16[256,256]{1,0:T(8,128)(2,1)S(1)}, u32[]{:S(2)}, u32[]{:S(2)}) collective-permute-start(bf16[256,256]{1,0:T(8,128)(2,1)S(1)} %fusion.14), channel_id=1, source_target_pairs={{0,7},{1,0},{2,1},{3,2},{4,3},{5,4},{6,5},{7,6},{8,15},{9,8},{10,9... | collective-permute-start | bytes 393224 | tf_op jit(solution)/shard_map/ppermute | solution.py:87
Sparse Core Ops, SparseCore 0:
  9.8 71.3 all-gather.1
  137.6 39.2 reduce-scatter.1

commit v8 on v5

--- a/solution.py
+++ b/solution.py
@@ -30,7 +30,7 @@
     owners = ("row", "tensor")
     dests = row_count * tensor_count
     lanes = qsize * TB
-    send = integral_tiles.reshape(held, dests, lanes).transpose(1, 0, 2)
+    send = integral_tiles.reshape(held, PB, quarters, lanes).transpose(1, 2, 0, 3).reshape(dests, held, lanes)
     local_index = jnp.stack(
         [tile_index[:, 0], tile_index[:, 1], tile_index[:, 2] - col_at * NBC], axis=1
     ).astype(jnp.bfloat16).reshape(1, 1, held * 3)
@@ -67,12 +67,14 @@
         keep = lax.dynamic_index_in_dim(pair, side, axis=0, keepdims=False)
         give = lax.dynamic_index_in_dim(pair, 1 - side, axis=0, keepdims=False)
         got_r = lax.ppermute(give, "row", perm=[(i, i ^ 1) for i in range(row_count)])
-        halves.append(keep.astype(jnp.float32) + got_r.astype(jnp.float32))
-    occ_done = jnp.concatenate(halves, axis=2).astype(jnp.bfloat16)
+        halves.append((keep.astype(jnp.float32) + got_r.astype(jnp.float32)).astype(jnp.bfloat16))
 
     chunk = NV // (row_count * col_count)
     virt = virtual_coeff.reshape(NBC, TB, NV)
-    z = jnp.einsum("nwi,nwv->vi", occ_done, virt, preferred_element_type=jnp.float32).astype(jnp.bfloat16)
+    z = jnp.concatenate(
+        [jnp.einsum("nwi,nwv->vi", h, virt, preferred_element_type=jnp.float32).astype(jnp.bfloat16) for h in halves],
+        axis=1,
+    )
     z = z.reshape(row_count, col_count, chunk, NOCC).transpose(1, 0, 2, 3)
     z = z.reshape(col_count * row_count * chunk, NOCC)
     w = lax.psum_scatter(z, "col", scatter_dimension=0, tiled=True).reshape(row_count, chunk, NOCC)

time: 196 us -> 192 us (0.980)
  matrix products: 17.7 us -> 15.4 us
    convert_element_type x1 -> x0, local copies, waits for them, and re-layouts: 2.86 us -> none  [shards(): jnp.einsum('nwi,nwv->vi', occ_done, virt, preferred_element_type=jnp.floa...]
    another operation x4 -> x2, other arithmetic: 3.75 us -> 1.37 us
    dot_general x1 -> x2, matrix products: 5.9 us -> 3.63 us  [shards(): jnp.einsum('nwi,nwv->vi', h, virt, preferred_element_type=jnp.float32)]
  transfers between devices with their start and end apart: 7 -> 7, of which waited for: 6 -> 6; matrix products, arithmetic and copies ran while one was open for 17% -> 18% of each run, Pallas kernels for 0% -> 0%
where the time goes in v8:
time: 192 us; the launch traced here: 191 us
  waiting for transfers between devices  102 us (53%)
  local copies, waits for them, and re-layouts  27.6 us (14%)
  matrix products  15.4 us (8%)
  blocking collectives  15.4 us (8%)
  between operations  13.6 us (7%)
  starting transfers between devices  9.68 us (5%)
  other arithmetic  7.57 us (4%)
    reduce_scatter x1, waiting for transfers between devices, shards(): lax.psum_scatter(z, 'col', scatter_dimension=0, tiled=True)  41.2 us
    all_to_all x1, waiting for transfers between devices, shards(): recv = lax.all_to_all(send, owners, split_axis=0, concat_axis=0, tiled=True)  36.7 us
    ppermute x2, waiting for transfers between devices, shards(): lax.ppermute(give, 'row', perm=[(i, i ^ 1) for i in range(row_count)])  19.1 us
    all_to_all x1, blocking collectives, shards(): got_rows = lax.all_to_all(w, 'row', split_axis=0, concat_axis=0, tiled=True)  15.4 us
    reshape x1, local copies, waits for them, and re-layouts, shards(): dense.reshape(aux_blocks * NBC, mu_blocks, qsize, TB).transpose(0, 3, 1, 2)  11.6 us
    all_to_all x1, starting transfers between devices, shards(): recv = lax.all_to_all(send, owners, split_axis=0, concat_axis=0, tiled=True)  7.32 us
    dot_general x1, matrix products, shards(): jnp.dot(selector, slices, preferred_element_type=jnp.float32)  6.02 us
    dot_general x1, matrix products, shards(): jnp.einsum('bwk,ki->bwi', dense, occ_q, preferred_element_type=jnp.float32)  5.77 us
  transfers between devices with their start and end apart: 7, of which 6 were waited for; matrix products, arithmetic and copies ran while one was open for 18% of the time, Pallas kernels for 0%

profile of v8, /device:TPU:32, one launch (start us, length us, event | category | flops | bytes accessed | tf_op | source)
XLA Modules:
  0.0 191.2 jit_solution(6300204169569031849)
XLA Ops:
  6.5 0.0 all-gather.2.cloned.1.call-start
  6.5 0.7 all-gather.2.cloned.1.call-update
  7.3 0.7 convert.12
  8.0 0.7 subtract_convert_fusion
  8.7 0.1 copy.14
  8.8 0.1 convert_element_type.87
  8.9 3.3 %reshape.95 = bf16[32,8,4,1024]{3,2,1,0:T(4,128)(2,1)S(1)} reshape(bf16[32,8,4096]{2,1,0:T(8,128)(2,1)} %param.4) | data formatting | bytes 4194304 | tf_op jit(solution)/shard_map/reshape | solution.py:33
  12.2 1.2 copy.13
  13.4 0.1 broadcast_in_dim.10
  13.5 1.8 pad_maximum_fusion
  15.3 7.3 %all-to-all-start = ((bf16[32,33,1024]{2,1,0:T(8,128)(2,1)}), bf16[32,33,1024]{2,1,0:T(8,128)(2,1)S(1)}, u32[]{:S(2)}, u32[]{:S(2)}) async-start(bf16[32,33,1024]{2,1,0:T(8,128)(2,1)} %pad_maximum_fusion), calls=%async_computation | async-start | bytes 5242880 | tf_op jit(solution)/shard_map/all_to_all | solution.py:39
  22.6 0.0 reduce-scatter.2.cloned.1.call-start
  22.7 36.7 %all-to-all-done = bf16[32,33,1024]{2,1,0:T(8,128)(2,1)S(1)} async-done(((bf16[32,33,1024]{2,1,0:T(8,128)(2,1)}), bf16[32,33,1024]{2,1,0:T(8,128)(2,1)S(1)}, u32[]{:S(2)}, u32[]{:S(2)}) %all-to-all-start) | async-done | bytes 2162720 | tf_op jit(solution)/shard_map/all_to_all | solution.py:39
  59.4 0.1 fusion.19
  59.4 0.5 reshape.109
  60.0 0.2 slice.35
  60.2 0.5 fusion.13
  60.7 6.0 %fusion.2 = bf16[2048,1024]{1,0:T(8,128)(2,1)} fusion(bf16[1024,1024]{1,0:T(8,128)(2,1)S(1)} %bitcast.85, s32[1024]{0:T(1024)S(1)} %fusion.13), kind=kOutput, calls=%fused_computation.3 | convolution fusion | flops 4299161600 | bytes 6295552 | tf_op jit(solution)/shard_map/dot_general | solution.py:52
  66.7 11.6 %reshape.98 = bf16[64,32,16,64]{3,2,1,0:T(8,128)(2,1)} reshape(bf16[2048,1024]{1,0:T(8,128)(2,1)} %fusion.2) | data formatting | bytes 8388608 | tf_op jit(solution)/shard_map/reshape | solution.py:53
  78.4 3.1 %all-gather.2.cloned.1.call-done = bf16[2048,512]{1,0:T(8,128)(2,1)} async-done(((bf16[128,512]{1,0:T(8,128)(2,1)}), bf16[2048,512]{1,0:T(8,128)(2,1)}) %all-gather.2.cloned.1.call-update) | async-done | bytes 2097168 | tf_op jit(solution)/shard_map/all_gather | solution.py:43
  81.4 1.1 constant_dynamic-slice_fusion
  82.5 5.8 %convolution_convert_fusion = bf16[4,16,64,512]{3,2,1,0:T(8,128)(2,1)S(1)} fusion(bf16[4,16,64,512]{2,3,1,0:T(8,128)(2,1)} %bitcast.75, bf16[512,512,1,1]{1,0,3,2:T(8,128)(2,1)S(1)} %bitcast.84), kind=kOutput, calls=%fused_computation.6 | convolution fusion | flops 2149580800 | bytes 8912896 | tf_op jit(solution)/shard_map/bwk,ki->bwi/dot_general | solution.py:56
  88.3 0.4 fusion.22
  88.7 0.0 copy-start
  88.7 0.1 dynamic-slice_bitcast_fusion.1
  88.8 0.1 collective-permute-start
  88.9 1.3 dynamic-slice_bitcast_fusion
  90.2 0.2 copy-done
  90.3 0.1 collective-permute-start.2
  90.4 1.2 collective-permute-done
  91.6 1.9 %fusion.8 = bf16[2,16,64,256]{3,2,1,0:T(8,128)(2,1)S(1)} fusion(bf16[2,16,64,256]{3,2,1,0:T(8,128)(2,1)} %collective-permute-done, bf16[2,2,16,64,256]{4,3,2,1,0:T(8,128)(2,1)} %bitcast.83, s32[]{:T(128)S(6)} %select_n.33), kind=kLoop, calls=%fused_computation.16 | loop fusion | flops 2097152 | bytes 3145732 | tf_op jit(solution)/shard_map/convert_element_type | solution.py:66
  93.6 0.8 dynamic-slice_bitcast_fusion.3
  94.4 1.2 collective-permute-start.1
  95.6 0.0 collective-permute-done.2
  95.6 1.7 fusion.7
  97.4 1.0 collective-permute-start.3
  98.3 11.2 %collective-permute-done.1 = bf16[16,64,256]{2,1,0:T(8,128)(2,1)} collective-permute-done((bf16[16,64,256]{2,1,0:T(8,128)(2,1)}, bf16[16,64,256]{2,1,0:T(8,128)(2,1)}, u32[]{:S(2)}, u32[]{:S(2)}) %collective-permute-start.1) | collective-permute-done | bytes 524320 | tf_op jit(solution)/shard_map/ppermute | solution.py:69
  109.5 0.0 copy-done.1
  109.5 2.3 %fusion.6 = bf16[2048,256]{0,1:T(8,128)(2,1)S(1)} fusion(bf16[16,64,2048]{2,1,0:T(8,128)(2,1)S(1)} %bitcast.89, bf16[16,64,256]{2,1,0:T(8,128)(2,1)} %collective-permute-done.1, bf16[2,16,64,256]{3,2,1,0:T(8,128)(2,1)S(1)} %fusion.8, s32[]{:T(128)S(6)} %select_n.35), kind=kOutput, calls=%fused_computation.11 | convolution fusion | flops 1075314688 | bytes 6291460 | tf_op jit(solution)/shard_map/nwi,nwv->vi/dot_general | solution.py:75
  111.8 8.0 %collective-permute-done.3 = bf16[16,64,256]{2,1,0:T(8,128)(2,1)S(1)} collective-permute-done((bf16[16,64,256]{2,1,0:T(8,128)(2,1)S(1)}, bf16[16,64,256]{2,1,0:T(8,128)(2,1)S(1)}, u32[]{:S(2)}, u32[]{:S(2)}) %collective-permute-start.3) | collective-permute-done | bytes 524320 | tf_op jit(solution)/shard_map/ppermute | solution.py:69
  119.8 1.3 fusion.5
  121.1 0.1 pad_maximum_fusion.1
  121.3 2.5 %copy.17 = bf16[2048,512]{1,0:T(8,128)(2,1)} copy(bf16[2048,512]{0,1:T(8,128)(2,1)S(1)} %pad_maximum_fusion.1) | data formatting | bytes 4194304 | tf_op jit(solution)/shard_map/concatenate | solution.py:74
  123.8 3.2 %copy.18 = bf16[8,16,16,512]{3,2,1,0:T(8,128)(2,1)} copy(bf16[8,16,16,512]{3,2,0,1:T(8,128)(2,1)} %bitcast.78) | data formatting | bytes 4194304 | tf_op jit(solution)/shard_map/transpose | solution.py:78
  126.9 0.0 reduce-scatter.2.cloned.1.call-update
  127.0 41.2 %reduce-scatter.2.cloned.1.call-done = bf16[256,512]{1,0:T(8,128)(2,1)} async-done(((bf16[2048,512]{1,0:T(8,128)(2,1)}), bf16[256,512]{1,0:T(8,128)(2,1)}) %reduce-scatter.2.cloned.1.call-update) | async-done | bytes 262160 | tf_op jit(solution)/shard_map/reduce_scatter | solution.py:80
  168.2 15.4 %all_to_all.10 = bf16[16,16,512]{2,1,0:T(8,128)(2,1)S(1)} all-to-all(bf16[16,16,512]{2,1,0:T(8,128)(2,1)} %bitcast.87), channel_id=1, replica_groups=mesh['tensor'=2,'row'=16,'col'=8] {'row'}, dimensions={0} | all-to-all | bytes 524288 | tf_op jit(solution)/shard_map/all_to_all | solution.py:82
  183.6 0.9 copy.24
  (5 shorter events, 0.1 us)
Async XLA Ops:
  6.5 74.9 %all-gather.2.cloned.1.call-start = ((), (), s32[]{:S(2)}) async-start(), calls=%async_computation.3 | async-start | bytes 2228224 | tf_op jit(solution)/shard_map/all_gather | solution.py:43
  15.3 44.1 %all-to-all-start = ((bf16[32,33,1024]{2,1,0:T(8,128)(2,1)}), bf16[32,33,1024]{2,1,0:T(8,128)(2,1)S(1)}, u32[]{:S(2)}, u32[]{:S(2)}) async-start(bf16[32,33,1024]{2,1,0:T(8,128)(2,1)} %pad_maximum_fusion), calls=%async_computation | async-start | bytes 5242880 | tf_op jit(solution)/shard_map/all_to_all | solution.py:39
  22.6 145.6 %reduce-scatter.2.cloned.1.call-start = ((), (), s32[]{:S(2)}) async-start(), calls=%async_computation.4 | async-start | bytes 2359296 | tf_op jit(solution)/shard_map/reduce_scatter | solution.py:80
  88.7 1.7 copy-start
  88.8 2.9 %collective-permute-start = (bf16[2,16,64,256]{3,2,1,0:T(8,128)(2,1)S(1)}, bf16[2,16,64,256]{3,2,1,0:T(8,128)(2,1)}, u32[]{:S(2)}, u32[]{:S(2)}) collective-permute-start(bf16[2,16,64,256]{3,2,1,0:T(8,128)(2,1)S(1)} %dynamic-slice_bitcast_fusion.1), channel_id=1, source_target_pairs={{0,128},{128,0},{1,129},{129,1},{2,130},{130,2},{3,131},{131,3},{4... | collective-permute-start | bytes 3145736 | tf_op jit(solution)/shard_map/ppermute | solution.py:65
  90.3 5.2 %collective-permute-start.2 = (bf16[2,16,64,256]{3,2,1,0:T(8,128)(2,1)}, bf16[2,16,64,256]{3,2,1,0:T(8,128)(2,1)}, u32[]{:S(2)}, u32[]{:S(2)}) collective-permute-start(bf16[2,16,64,256]{3,2,1,0:T(8,128)(2,1)} %dynamic-slice_bitcast_fusion), channel_id=1, source_target_pairs={{0,128},{128,0},{1,129},{129,1},{2,130},{130,2},{3,131},{131,3},{4... | collective-permute-start | bytes 3145736 | tf_op jit(solution)/shard_map/ppermute | solution.py:65
  94.4 15.1 %collective-permute-start.1 = (bf16[16,64,256]{2,1,0:T(8,128)(2,1)}, bf16[16,64,256]{2,1,0:T(8,128)(2,1)}, u32[]{:S(2)}, u32[]{:S(2)}) collective-permute-start(bf16[16,64,256]{2,1,0:T(8,128)(2,1)} %dynamic-slice_bitcast_fusion.3), channel_id=1, source_target_pairs={{0,8},{8,0},{16,24},{24,16},{32,40},{40,32},{48,56},{56,48},{64,72... | collective-permute-start | bytes 1572872 | tf_op jit(solution)/shard_map/ppermute | solution.py:69
  95.6 13.9 %copy-start.1 = (bf16[1024,2048]{1,0:T(8,128)(2,1)S(1)}, bf16[1024,2048]{1,0:T(8,128)(2,1)}, u32[]{:S(2)}) copy-start(bf16[1024,2048]{1,0:T(8,128)(2,1)} %param.6) | copy-start | bytes 12582916
  97.4 22.4 %collective-permute-start.3 = (bf16[16,64,256]{2,1,0:T(8,128)(2,1)S(1)}, bf16[16,64,256]{2,1,0:T(8,128)(2,1)S(1)}, u32[]{:S(2)}, u32[]{:S(2)}) collective-permute-start(bf16[16,64,256]{2,1,0:T(8,128)(2,1)S(1)} %dynamic-slice_bitcast_fusion.2), channel_id=1, source_target_pairs={{0,8},{8,0},{16,24},{24,16},{32,40},{40,32},{48,56},{56,48},{64,72... | collective-permute-start | bytes 1572872 | tf_op jit(solution)/shard_map/ppermute | solution.py:69
Sparse Core Ops, SparseCore 0:
  9.8 71.5 all-gather.1
  127.1 41.0 reduce-scatter.1

commit v9 on v8

--- a/solution.py
+++ b/solution.py
@@ -79,7 +79,13 @@
     z = z.reshape(col_count * row_count * chunk, NOCC)
     w = lax.psum_scatter(z, "col", scatter_dimension=0, tiled=True).reshape(row_count, chunk, NOCC)
 
-    got_rows = lax.all_to_all(w, "row", split_axis=0, concat_axis=0, tiled=True)
+    side_count = 4
+    by_x = [[g * side_count + k for k in range(side_count)] for g in range(row_count // side_count)]
+    by_y = [[k * side_count + g for k in range(row_count // side_count)] for g in range(side_count)]
+    w = w.reshape(row_count // side_count, side_count, chunk, NOCC)
+    w = lax.all_to_all(w, "row", split_axis=1, concat_axis=1, axis_index_groups=by_x, tiled=True)
+    w = lax.all_to_all(w, "row", split_axis=0, concat_axis=0, axis_index_groups=by_y, tiled=True)
+    got_rows = w.reshape(row_count, chunk, NOCC)
     out = got_rows.reshape(PB, 2, chunk, NOCC).transpose(2, 1, 0, 3)
     return out.reshape(chunk, AB * PB, NOCC)
 

time: 192 us -> 199 us (1.036)
  blocking collectives: 15.4 us -> 21.6 us
    all_to_all x1 -> x2, blocking collectives: 15.4 us -> 21.6 us  [the longest x1 10.8 us: shards(): lax.all_to_all(w, 'row', split_axis=1, concat_axis=1, axis_index_groups=b...]
where the time goes in v9:
time: 199 us; the launch traced here: 198 us
  waiting for transfers between devices  102 us (51%)
  local copies, waits for them, and re-layouts  28.6 us (14%)
  blocking collectives  21.6 us (11%)
  matrix products  15.4 us (8%)
  between operations  13.6 us (7%)
  starting transfers between devices  9.68 us (5%)
  other arithmetic  7.57 us (4%)
    reduce_scatter x1, waiting for transfers between devices, shards(): lax.psum_scatter(z, 'col', scatter_dimension=0, tiled=True)  41.2 us
    all_to_all x1, waiting for transfers between devices, shards(): recv = lax.all_to_all(send, owners, split_axis=0, concat_axis=0, tiled=True)  36.7 us
    ppermute x2, waiting for transfers between devices, shards(): lax.ppermute(give, 'row', perm=[(i, i ^ 1) for i in range(row_count)])  19.1 us
    reshape x1, local copies, waits for them, and re-layouts, shards(): dense.reshape(aux_blocks * NBC, mu_blocks, qsize, TB).transpose(0, 3, 1, 2)  11.6 us
    all_to_all x1, blocking collectives, shards(): lax.all_to_all(w, 'row', split_axis=1, concat_axis=1, axis_index_groups=b...  10.8 us
    all_to_all x1, blocking collectives, shards(): lax.all_to_all(w, 'row', split_axis=0, concat_axis=0, axis_index_groups=b...  10.8 us
    all_to_all x1, starting transfers between devices, shards(): recv = lax.all_to_all(send, owners, split_axis=0, concat_axis=0, tiled=True)  7.32 us
    dot_general x1, matrix products, shards(): jnp.dot(selector, slices, preferred_element_type=jnp.float32)  6.02 us
  transfers between devices with their start and end apart: 7, of which 6 were waited for; matrix products, arithmetic and copies ran while one was open for 18% of the time, Pallas kernels for 0%

profile of v9, /device:TPU:32, one launch (start us, length us, event | category | flops | bytes accessed | tf_op | source)
XLA Modules:
  0.0 198.4 jit_solution(12896733734906822349)
XLA Ops:
  6.5 0.0 all-gather.2.cloned.1.call-start
  6.5 0.7 all-gather.2.cloned.1.call-update
  7.3 0.7 convert.12
  8.0 0.7 subtract_convert_fusion
  8.7 0.1 copy.21
  8.8 0.1 convert_element_type.87
  8.9 3.3 %reshape.89 = bf16[32,8,4,1024]{3,2,1,0:T(4,128)(2,1)S(1)} reshape(bf16[32,8,4096]{2,1,0:T(8,128)(2,1)} %param.4) | data formatting | bytes 4194304 | tf_op jit(solution)/shard_map/reshape | solution.py:33
  12.2 1.2 copy.20
  13.4 0.1 broadcast_in_dim.10
  13.5 1.8 pad_maximum_fusion
  15.3 7.3 %all-to-all-start = ((bf16[32,33,1024]{2,1,0:T(8,128)(2,1)}), bf16[32,33,1024]{2,1,0:T(8,128)(2,1)S(1)}, u32[]{:S(2)}, u32[]{:S(2)}) async-start(bf16[32,33,1024]{2,1,0:T(8,128)(2,1)} %pad_maximum_fusion), calls=%async_computation | async-start | bytes 5242880 | tf_op jit(solution)/shard_map/all_to_all | solution.py:39
  22.6 0.0 reduce-scatter.2.cloned.1.call-start
  22.7 36.7 %all-to-all-done = bf16[32,33,1024]{2,1,0:T(8,128)(2,1)S(1)} async-done(((bf16[32,33,1024]{2,1,0:T(8,128)(2,1)}), bf16[32,33,1024]{2,1,0:T(8,128)(2,1)S(1)}, u32[]{:S(2)}, u32[]{:S(2)}) %all-to-all-start) | async-done | bytes 2162720 | tf_op jit(solution)/shard_map/all_to_all | solution.py:39
  59.4 0.1 fusion.19
  59.4 0.5 reshape.101
  60.0 0.2 slice.35
  60.2 0.5 fusion.13
  60.7 6.0 %fusion.2 = bf16[2048,1024]{1,0:T(8,128)(2,1)} fusion(bf16[1024,1024]{1,0:T(8,128)(2,1)S(1)} %bitcast.85, s32[1024]{0:T(1024)S(1)} %fusion.13), kind=kOutput, calls=%fused_computation.3 | convolution fusion | flops 4299161600 | bytes 6295552 | tf_op jit(solution)/shard_map/dot_general | solution.py:52
  66.7 11.6 %reshape.92 = bf16[64,32,16,64]{3,2,1,0:T(8,128)(2,1)} reshape(bf16[2048,1024]{1,0:T(8,128)(2,1)} %fusion.2) | data formatting | bytes 8388608 | tf_op jit(solution)/shard_map/reshape | solution.py:53
  78.4 3.1 %all-gather.2.cloned.1.call-done = bf16[2048,512]{1,0:T(8,128)(2,1)} async-done(((bf16[128,512]{1,0:T(8,128)(2,1)}), bf16[2048,512]{1,0:T(8,128)(2,1)}) %all-gather.2.cloned.1.call-update) | async-done | bytes 2097168 | tf_op jit(solution)/shard_map/all_gather | solution.py:43
  81.4 1.1 constant_dynamic-slice_fusion
  82.5 5.8 %convolution_convert_fusion = bf16[4,16,64,512]{3,2,1,0:T(8,128)(2,1)S(1)} fusion(bf16[4,16,64,512]{2,3,1,0:T(8,128)(2,1)} %bitcast.75, bf16[512,512,1,1]{1,0,3,2:T(8,128)(2,1)S(1)} %bitcast.84), kind=kOutput, calls=%fused_computation.6 | convolution fusion | flops 2149580800 | bytes 8912896 | tf_op jit(solution)/shard_map/bwk,ki->bwi/dot_general | solution.py:56
  88.3 0.4 fusion.22
  88.7 0.1 dynamic-slice_bitcast_fusion.1
  88.8 0.1 collective-permute-start
  88.9 1.3 dynamic-slice_bitcast_fusion
  90.2 0.2 copy-done
  90.3 0.1 collective-permute-start.2
  90.4 1.2 collective-permute-done
  91.6 1.9 fusion.8
  93.6 0.8 dynamic-slice_bitcast_fusion.3
  94.4 1.2 collective-permute-start.1
  95.6 0.0 collective-permute-done.2
  95.6 1.7 fusion.7
  97.4 1.0 collective-permute-start.3
  98.3 11.2 %collective-permute-done.1 = bf16[16,64,256]{2,1,0:T(8,128)(2,1)} collective-permute-done((bf16[16,64,256]{2,1,0:T(8,128)(2,1)}, bf16[16,64,256]{2,1,0:T(8,128)(2,1)}, u32[]{:S(2)}, u32[]{:S(2)}) %collective-permute-start.1) | collective-permute-done | bytes 524320 | tf_op jit(solution)/shard_map/ppermute | solution.py:69
  109.5 2.3 %fusion.6 = bf16[2048,256]{0,1:T(8,128)(2,1)S(1)} fusion(bf16[16,64,2048]{2,1,0:T(8,128)(2,1)S(1)} %bitcast.89, bf16[16,64,256]{2,1,0:T(8,128)(2,1)} %collective-permute-done.1, bf16[2,16,64,256]{3,2,1,0:T(8,128)(2,1)S(1)} %fusion.8, s32[]{:T(128)S(6)} %select_n.35), kind=kOutput, calls=%fused_computation.11 | convolution fusion | flops 1075314688 | bytes 6291460 | tf_op jit(solution)/shard_map/nwi,nwv->vi/dot_general | solution.py:75
  111.8 8.0 %collective-permute-done.3 = bf16[16,64,256]{2,1,0:T(8,128)(2,1)S(1)} collective-permute-done((bf16[16,64,256]{2,1,0:T(8,128)(2,1)S(1)}, bf16[16,64,256]{2,1,0:T(8,128)(2,1)S(1)}, u32[]{:S(2)}, u32[]{:S(2)}) %collective-permute-start.3) | collective-permute-done | bytes 524320 | tf_op jit(solution)/shard_map/ppermute | solution.py:69
  119.8 1.3 fusion.5
  121.1 0.1 pad_maximum_fusion.1
  121.3 2.5 %copy.24 = bf16[2048,512]{1,0:T(8,128)(2,1)} copy(bf16[2048,512]{0,1:T(8,128)(2,1)S(1)} %pad_maximum_fusion.1) | data formatting | bytes 4194304 | tf_op jit(solution)/shard_map/concatenate | solution.py:74
  123.8 3.2 %copy.25 = bf16[8,16,16,512]{3,2,1,0:T(8,128)(2,1)} copy(bf16[8,16,16,512]{3,2,0,1:T(8,128)(2,1)} %bitcast.78) | data formatting | bytes 4194304 | tf_op jit(solution)/shard_map/transpose | solution.py:78
  126.9 0.0 reduce-scatter.2.cloned.1.call-update
  127.0 41.2 %reduce-scatter.2.cloned.1.call-done = bf16[256,512]{1,0:T(8,128)(2,1)} async-done(((bf16[2048,512]{1,0:T(8,128)(2,1)}), bf16[256,512]{1,0:T(8,128)(2,1)}) %reduce-scatter.2.cloned.1.call-update) | async-done | bytes 262160 | tf_op jit(solution)/shard_map/reduce_scatter | solution.py:80
  168.2 1.0 copy.26
  169.2 10.8 %all_to_all.15 = bf16[4,4,16,512]{3,2,0,1:T(8,128)(2,1)S(1)} all-to-all(bf16[4,4,16,512]{3,2,0,1:T(8,128)(2,1)S(1)} %copy.26), channel_id=1, replica_groups={{0,8,16,24},{32,40,48,56},{64,72,80,88},{96,104,112,120},{1,9,17,25},{3..., dimensions={1} | all-to-all | bytes 524288 | tf_op jit(solution)/shard_map/all_to_all | solution.py:86
  180.0 10.8 %all_to_all.16 = bf16[4,4,16,512]{3,2,1,0:T(8,128)(2,1)S(1)} all-to-all(bf16[4,4,16,512]{3,2,1,0:T(8,128)(2,1)S(1)} %copy.27), channel_id=1, replica_groups={{0,32,64,96},{8,40,72,104},{16,48,80,112},{24,56,88,120},{1,33,65,97},{..., dimensions={0} | all-to-all | bytes 524288 | tf_op jit(solution)/shard_map/all_to_all | solution.py:87
  190.8 0.9 copy.33
  (8 shorter events, 0.1 us)
Async XLA Ops:
  6.5 74.9 %all-gather.2.cloned.1.call-start = ((), (), s32[]{:S(2)}) async-start(), calls=%async_computation.4 | async-start | bytes 2228224 | tf_op jit(solution)/shard_map/all_gather | solution.py:43
  15.3 44.1 %all-to-all-start = ((bf16[32,33,1024]{2,1,0:T(8,128)(2,1)}), bf16[32,33,1024]{2,1,0:T(8,128)(2,1)S(1)}, u32[]{:S(2)}, u32[]{:S(2)}) async-start(bf16[32,33,1024]{2,1,0:T(8,128)(2,1)} %pad_maximum_fusion), calls=%async_computation | async-start | bytes 5242880 | tf_op jit(solution)/shard_map/all_to_all | solution.py:39
  22.6 145.6 %reduce-scatter.2.cloned.1.call-start = ((), (), s32[]{:S(2)}) async-start(), calls=%async_computation.5 | async-start | bytes 2359296 | tf_op jit(solution)/shard_map/reduce_scatter | solution.py:80
  88.7 1.7 copy-start
  88.8 2.9 %collective-permute-start = (bf16[2,16,64,256]{3,2,1,0:T(8,128)(2,1)S(1)}, bf16[2,16,64,256]{3,2,1,0:T(8,128)(2,1)}, u32[]{:S(2)}, u32[]{:S(2)}) collective-permute-start(bf16[2,16,64,256]{3,2,1,0:T(8,128)(2,1)S(1)} %dynamic-slice_bitcast_fusion.1), channel_id=1, source_target_pairs={{0,128},{128,0},{1,129},{129,1},{2,130},{130,2},{3,131},{131,3},{4... | collective-permute-start | bytes 3145736 | tf_op jit(solution)/shard_map/ppermute | solution.py:65
  90.3 5.2 %collective-permute-start.2 = (bf16[2,16,64,256]{3,2,1,0:T(8,128)(2,1)}, bf16[2,16,64,256]{3,2,1,0:T(8,128)(2,1)}, u32[]{:S(2)}, u32[]{:S(2)}) collective-permute-start(bf16[2,16,64,256]{3,2,1,0:T(8,128)(2,1)} %dynamic-slice_bitcast_fusion), channel_id=1, source_target_pairs={{0,128},{128,0},{1,129},{129,1},{2,130},{130,2},{3,131},{131,3},{4... | collective-permute-start | bytes 3145736 | tf_op jit(solution)/shard_map/ppermute | solution.py:65
  94.4 15.1 %collective-permute-start.1 = (bf16[16,64,256]{2,1,0:T(8,128)(2,1)}, bf16[16,64,256]{2,1,0:T(8,128)(2,1)}, u32[]{:S(2)}, u32[]{:S(2)}) collective-permute-start(bf16[16,64,256]{2,1,0:T(8,128)(2,1)} %dynamic-slice_bitcast_fusion.3), channel_id=1, source_target_pairs={{0,8},{8,0},{16,24},{24,16},{32,40},{40,32},{48,56},{56,48},{64,72... | collective-permute-start | bytes 1572872 | tf_op jit(solution)/shard_map/ppermute | solution.py:69
  95.6 13.9 %copy-start.1 = (bf16[1024,2048]{1,0:T(8,128)(2,1)S(1)}, bf16[1024,2048]{1,0:T(8,128)(2,1)}, u32[]{:S(2)}) copy-start(bf16[1024,2048]{1,0:T(8,128)(2,1)} %param.6) | copy-start | bytes 12582916
  97.4 22.4 %collective-permute-start.3 = (bf16[16,64,256]{2,1,0:T(8,128)(2,1)S(1)}, bf16[16,64,256]{2,1,0:T(8,128)(2,1)S(1)}, u32[]{:S(2)}, u32[]{:S(2)}) collective-permute-start(bf16[16,64,256]{2,1,0:T(8,128)(2,1)S(1)} %dynamic-slice_bitcast_fusion.2), channel_id=1, source_target_pairs={{0,8},{8,0},{16,24},{24,16},{32,40},{40,32},{48,56},{56,48},{64,72... | collective-permute-start | bytes 1572872 | tf_op jit(solution)/shard_map/ppermute | solution.py:69
Sparse Core Ops, SparseCore 0:
  9.8 71.5 all-gather.1
  127.1 41.0 reduce-scatter.1

commit v10 on v8

--- a/solution.py
+++ b/solution.py
@@ -40,11 +40,11 @@
     slices = recv[:, :held, :].reshape(dests * held, lanes)
     index = recv[:, held, : held * 3].astype(jnp.int32).reshape(dests * held, 3)
 
-    occ_all = lax.all_gather(occupied_coeff, "row", axis=0, tiled=True)
-    quarter = 2 * (row_at % 2) + tensor_at
-    occ_q = lax.dynamic_index_in_dim(
-        occ_all.reshape(mu_blocks, quarters, qsize, NOCC), quarter, axis=1, keepdims=False
-    ).reshape(mu_blocks * qsize, NOCC)
+    occ_local = occupied_coeff.reshape(MB, 2, tensor_count, qsize, NOCC)
+    occ_local = lax.dynamic_index_in_dim(occ_local, tensor_at, axis=2, keepdims=False)
+    occ_half = lax.all_gather(occ_local, "row", axis=0, tiled=True)
+    pick = row_at % 2 + jnp.minimum(index[0, 0], 0)
+    occ_q = lax.dynamic_index_in_dim(occ_half, pick, axis=1, keepdims=False).reshape(mu_blocks * qsize, NOCC)
 
     block = (index[:, 0] * NBC + index[:, 2]) * mu_blocks + index[:, 1]
     blocks = aux_blocks * NBC * mu_blocks
@@ -53,13 +53,12 @@
     dense = dense.reshape(aux_blocks * NBC, mu_blocks, qsize, TB).transpose(0, 3, 1, 2)
     dense = dense.reshape(aux_blocks * NBC, TB, mu_blocks * qsize)
 
-    partial = jnp.einsum("bwk,ki->bwi", dense, occ_q, preferred_element_type=jnp.float32)
-    partial = partial.reshape(aux_blocks, NBC, TB, NOCC)
 
     side = row_at % 2
     halves = []
-    for half in jnp.split(partial.astype(jnp.bfloat16), 2, axis=3):
-        pairs = half.reshape(tensor_count, AB, NBC, TB, NOCC // 2)
+    for occ_h in jnp.split(occ_q, 2, axis=1):
+        half = jnp.einsum("bwk,ki->bwi", dense, occ_h, preferred_element_type=jnp.float32)
+        pairs = half.astype(jnp.bfloat16).reshape(tensor_count, AB, NBC, TB, NOCC // 2)
         mine = lax.dynamic_index_in_dim(pairs, tensor_at, axis=0, keepdims=False)
         other = lax.dynamic_index_in_dim(pairs, 1 - tensor_at, axis=0, keepdims=False)
         got_t = lax.ppermute(other, "tensor", perm=[(0, 1), (1, 0)])

time: 192 us -> 194 us (1.010)
  matrix products: 15.4 us -> 18 us
  waiting for transfers between devices: 102 us -> 100 us
    dot_general x1 -> x2, matrix products: 5.77 us -> 8.27 us  [shards(): jnp.einsum('bwk,ki->bwi', dense, occ_h, preferred_element_type=jnp.float32)]
    all_gather x1, waiting for transfers between devices: 3.07 us -> 5.44 us  [shards(): occ_half = lax.all_gather(occ_local, 'row', axis=0, tiled=True)]
    all_to_all x1, waiting for transfers between devices: 36.7 us -> 34.5 us  [shards(): recv = lax.all_to_all(send, owners, split_axis=0, concat_axis=0, tiled=True)]
  transfers between devices with their start and end apart: 7 -> 7, of which waited for: 6 -> 5; matrix products, arithmetic and copies ran while one was open for 18% -> 16% of each run, Pallas kernels for 0% -> 0%
where the time goes in v10:
time: 194 us; the launch traced here: 193 us
  waiting for transfers between devices  100 us (52%)
  local copies, waits for them, and re-layouts  27.9 us (14%)
  matrix products  18 us (9%)
  blocking collectives  15.4 us (8%)
  between operations  14.2 us (7%)
  starting transfers between devices  10.1 us (5%)
  other arithmetic  7.62 us (4%)
    reduce_scatter x1, waiting for transfers between devices, shards(): lax.psum_scatter(z, 'col', scatter_dimension=0, tiled=True)  41.1 us
    all_to_all x1, waiting for transfers between devices, shards(): recv = lax.all_to_all(send, owners, split_axis=0, concat_axis=0, tiled=True)  34.5 us
    ppermute x2, waiting for transfers between devices, shards(): lax.ppermute(give, 'row', perm=[(i, i ^ 1) for i in range(row_count)])  19 us
    all_to_all x1, blocking collectives, shards(): got_rows = lax.all_to_all(w, 'row', split_axis=0, concat_axis=0, tiled=True)  15.4 us
    reshape x1, local copies, waits for them, and re-layouts, shards(): dense.reshape(aux_blocks * NBC, mu_blocks, qsize, TB).transpose(0, 3, 1, 2)  11.6 us
    dot_general x2, matrix products, shards(): jnp.einsum('bwk,ki->bwi', dense, occ_h, preferred_element_type=jnp.float32)  8.27 us
    all_to_all x1, starting transfers between devices, shards(): recv = lax.all_to_all(send, owners, split_axis=0, concat_axis=0, tiled=True)  7.32 us
    dot_general x1, matrix products, shards(): jnp.dot(selector, slices, preferred_element_type=jnp.float32)  6.05 us
  transfers between devices with their start and end apart: 7, of which 5 were waited for; matrix products, arithmetic and copies ran while one was open for 16% of the time, Pallas kernels for 0%

profile of v10, /device:TPU:32, one launch (start us, length us, event | category | flops | bytes accessed | tf_op | source)
XLA Modules:
  0.0 193.3 jit_solution(3172474544025305626)
XLA Ops:
  6.5 0.7 convert.12
  7.3 0.7 subtract_convert_fusion
  8.0 0.1 copy.15
  8.1 0.1 convert_element_type.90
  8.2 3.3 %reshape.96 = bf16[32,8,4,1024]{3,2,1,0:T(4,128)(2,1)S(1)} reshape(bf16[32,8,4096]{2,1,0:T(8,128)(2,1)} %param.4) | data formatting | bytes 4194304 | tf_op jit(solution)/shard_map/reshape | solution.py:33
  11.5 1.2 copy.14
  12.7 0.1 broadcast_in_dim.10
  12.8 1.9 pad_maximum_fusion
  14.6 7.3 %all-to-all-start = ((bf16[32,33,1024]{2,1,0:T(8,128)(2,1)}), bf16[32,33,1024]{2,1,0:T(8,128)(2,1)S(1)}, u32[]{:S(2)}, u32[]{:S(2)}) async-start(bf16[32,33,1024]{2,1,0:T(8,128)(2,1)} %pad_maximum_fusion), calls=%async_computation | async-start | bytes 5242880 | tf_op jit(solution)/shard_map/all_to_all | solution.py:39
  22.0 0.0 all-gather.3.cloned.1.call-start
  22.0 0.6 copy.24
  22.7 0.0 all-gather.3.cloned.1.call-update
  22.7 0.0 reduce-scatter.2.cloned.1.call-start
  22.8 34.5 %all-to-all-done = bf16[32,33,1024]{2,1,0:T(8,128)(2,1)S(1)} async-done(((bf16[32,33,1024]{2,1,0:T(8,128)(2,1)}), bf16[32,33,1024]{2,1,0:T(8,128)(2,1)S(1)}, u32[]{:S(2)}, u32[]{:S(2)}) %all-to-all-start) | async-done | bytes 2162720 | tf_op jit(solution)/shard_map/all_to_all | solution.py:39
  57.2 0.1 fusion.19
  57.3 0.5 reshape.111
  57.8 0.5 slice.40
  58.9 0.2 slice.39
  59.1 0.5 fusion.13
  59.6 6.0 %fusion.2 = bf16[2048,1024]{1,0:T(8,128)(2,1)} fusion(bf16[1024,1024]{1,0:T(8,128)(2,1)S(1)} %bitcast.91, s32[1024]{0:T(1024)S(1)} %fusion.13), kind=kOutput, calls=%fused_computation.3 | convolution fusion | flops 4299161600 | bytes 6295552 | tf_op jit(solution)/shard_map/dot_general | solution.py:52
  65.7 11.6 %reshape.99 = bf16[64,32,16,64]{3,2,1,0:T(8,128)(2,1)} reshape(bf16[2048,1024]{1,0:T(8,128)(2,1)} %fusion.2) | data formatting | bytes 8388608 | tf_op jit(solution)/shard_map/reshape | solution.py:53
  77.3 5.4 %all-gather.3.cloned.1.call-done = bf16[32,2,1,16,512]{4,3,0,2,1:T(8,128)(2,1)} async-done(((bf16[2,2,1,16,512]{4,3,0,2,1:T(8,128)(2,1)}), bf16[32,2,1,16,512]{4,3,0,2,1:T(8,128)(2,1)}) %all-gather.3.cloned.1.call-update) | async-done | bytes 1048592 | tf_op jit(solution)/shard_map/all_gather | solution.py:45
  82.7 1.1 constant_dynamic-slice_fusion
  83.8 0.0 slice-start
  83.8 0.0 slice-start.1
  83.8 5.9 %convolution_convert_fusion.1 = bf16[64,64,256]{2,1,0:T(8,128)(2,1)S(1)} fusion(bf16[64,64,512]{1,2,0:T(8,128)(2,1)} %bitcast.77, bf16[512,512]{1,0:T(8,128)(2,1)S(1)} %bitcast.89), kind=kOutput, calls=%fused_computation.17 | convolution fusion | flops 1074790400 | bytes 6553600 | tf_op jit(solution)/shard_map/bwk,ki->bwi/dot_general | solution.py:60
  89.8 0.1 dynamic-slice_bitcast_fusion.1
  89.9 0.1 collective-permute-start
  90.0 2.4 %convolution_convert_fusion = bf16[64,64,256]{2,1,0:T(8,128)(2,1)S(1)} fusion(bf16[64,64,512]{1,2,0:T(8,128)(2,1)S(1)} %bitcast.80, bf16[512,512]{1,0:T(8,128)(2,1)S(1)} %bitcast.90), kind=kOutput, calls=%fused_computation.16 | convolution fusion | flops 1074790400 | bytes 10747904 | tf_op jit(solution)/shard_map/bwk,ki->bwi/dot_general | solution.py:60
  92.4 1.0 dynamic-slice_bitcast_fusion
  93.4 0.5 collective-permute-start.2
  93.9 1.9 fusion.8
  95.8 0.8 dynamic-slice_bitcast_fusion.3
  96.7 1.0 collective-permute-start.1
  97.7 0.0 collective-permute-done.2
  97.7 1.7 fusion.7
  99.5 1.1 collective-permute-start.3
  100.6 11.2 %collective-permute-done.1 = bf16[16,64,256]{2,1,0:T(8,128)(2,1)} collective-permute-done((bf16[16,64,256]{2,1,0:T(8,128)(2,1)}, bf16[16,64,256]{2,1,0:T(8,128)(2,1)}, u32[]{:S(2)}, u32[]{:S(2)}) %collective-permute-start.1) | collective-permute-done | bytes 524320 | tf_op jit(solution)/shard_map/ppermute | solution.py:68
  111.8 2.3 %fusion.6 = bf16[2048,256]{0,1:T(8,128)(2,1)S(1)} fusion(bf16[16,64,2048]{2,1,0:T(8,128)(2,1)S(1)} %bitcast.94, bf16[16,64,256]{2,1,0:T(8,128)(2,1)} %collective-permute-done.1, bf16[2,16,64,256]{3,2,1,0:T(8,128)(2,1)S(1)} %fusion.8, s32[]{:T(128)S(6)} %select_n.37), kind=kOutput, calls=%fused_computation.10 | convolution fusion | flops 1075314688 | bytes 6291460 | tf_op jit(solution)/shard_map/nwi,nwv->vi/dot_general | solution.py:74
  114.1 7.9 %collective-permute-done.3 = bf16[16,64,256]{2,1,0:T(8,128)(2,1)S(1)} collective-permute-done((bf16[16,64,256]{2,1,0:T(8,128)(2,1)S(1)}, bf16[16,64,256]{2,1,0:T(8,128)(2,1)S(1)}, u32[]{:S(2)}, u32[]{:S(2)}) %collective-permute-start.3) | collective-permute-done | bytes 524320 | tf_op jit(solution)/shard_map/ppermute | solution.py:68
  122.0 1.3 fusion.5
  123.3 0.1 pad_maximum_fusion.1
  123.4 2.5 %copy.19 = bf16[2048,512]{1,0:T(8,128)(2,1)} copy(bf16[2048,512]{0,1:T(8,128)(2,1)S(1)} %pad_maximum_fusion.1) | data formatting | bytes 4194304 | tf_op jit(solution)/shard_map/concatenate | solution.py:73
  125.9 3.2 %copy.20 = bf16[8,16,16,512]{3,2,1,0:T(8,128)(2,1)} copy(bf16[8,16,16,512]{3,2,0,1:T(8,128)(2,1)} %bitcast.87) | data formatting | bytes 4194304 | tf_op jit(solution)/shard_map/transpose | solution.py:77
  129.1 0.0 reduce-scatter.2.cloned.1.call-update
  129.1 41.1 %reduce-scatter.2.cloned.1.call-done = bf16[256,512]{1,0:T(8,128)(2,1)} async-done(((bf16[2048,512]{1,0:T(8,128)(2,1)}), bf16[256,512]{1,0:T(8,128)(2,1)}) %reduce-scatter.2.cloned.1.call-update) | async-done | bytes 262160 | tf_op jit(solution)/shard_map/reduce_scatter | solution.py:79
  170.2 15.4 %all_to_all.10 = bf16[16,16,512]{2,1,0:T(8,128)(2,1)S(1)} all-to-all(bf16[16,16,512]{2,1,0:T(8,128)(2,1)} %bitcast.93), channel_id=1, replica_groups=mesh['tensor'=2,'row'=16,'col'=8] {'row'}, dimensions={0} | all-to-all | bytes 524288 | tf_op jit(solution)/shard_map/all_to_all | solution.py:81
  185.6 0.9 copy.26
  (15 shorter events, 0.1 us)
Async XLA Ops:
  6.5 15.5 %copy-start = (bf16[128,512]{1,0:T(8,128)(2,1)S(1)}, bf16[128,512]{1,0:T(8,128)(2,1)}, u32[]{:S(2)}) copy-start(bf16[128,512]{1,0:T(8,128)(2,1)} %param.7) | copy-start | bytes 393220
  14.6 42.6 %all-to-all-start = ((bf16[32,33,1024]{2,1,0:T(8,128)(2,1)}), bf16[32,33,1024]{2,1,0:T(8,128)(2,1)S(1)}, u32[]{:S(2)}, u32[]{:S(2)}) async-start(bf16[32,33,1024]{2,1,0:T(8,128)(2,1)} %pad_maximum_fusion), calls=%async_computation | async-start | bytes 5242880 | tf_op jit(solution)/shard_map/all_to_all | solution.py:39
  22.0 60.8 %all-gather.3.cloned.1.call-start = ((), (), s32[]{:S(2)}) async-start(), calls=%async_computation.4 | async-start | bytes 1114112 | tf_op jit(solution)/shard_map/all_gather | solution.py:45
  22.7 147.5 %reduce-scatter.2.cloned.1.call-start = ((), (), s32[]{:S(2)}) async-start(), calls=%async_computation.3 | async-start | bytes 2359296 | tf_op jit(solution)/shard_map/reduce_scatter | solution.py:79
  83.8 6.2 %slice-start = ((s8[8388608]{0:T(1024)(128)(4,1)}), s8[4194304]{0:T(1024)(128)(4,1)S(1)}, s32[]{:S(2)}) async-start(s8[8388608]{0:T(1024)(128)(4,1)} %bitcast.78), calls=%async_computation.5 | async-start | bytes 8388608
  83.8 6.2 %slice-start.1 = ((s8[8388608]{0:T(1024)(128)(4,1)}), s8[4194304]{0:T(1024)(128)(4,1)S(1)}, s32[]{:S(2)}) async-start(s8[8388608]{0:T(1024)(128)(4,1)} %bitcast.78), calls=%async_computation.6 | async-start | bytes 8388608
  89.8 2.6 %copy-start.1 = (bf16[64,64,256]{2,1,0:T(8,128)(2,1)}, bf16[64,64,256]{2,1,0:T(8,128)(2,1)S(1)}, u32[]{:S(2)}) copy-start(bf16[64,64,256]{2,1,0:T(8,128)(2,1)S(1)} %convolution_convert_fusion.1) | copy-start | bytes 6291460
  89.9 4.0 %collective-permute-start = (bf16[2,16,64,256]{3,2,1,0:T(8,128)(2,1)S(1)}, bf16[2,16,64,256]{3,2,1,0:T(8,128)(2,1)}, u32[]{:S(2)}, u32[]{:S(2)}) collective-permute-start(bf16[2,16,64,256]{3,2,1,0:T(8,128)(2,1)S(1)} %dynamic-slice_bitcast_fusion.1), channel_id=1, source_target_pairs={{0,128},{128,0},{1,129},{129,1},{2,130},{130,2},{3,131},{131,3},{4... | collective-permute-start | bytes 3145736 | tf_op jit(solution)/shard_map/ppermute | solution.py:64
  93.4 4.3 %collective-permute-start.2 = (bf16[2,16,64,256]{3,2,1,0:T(8,128)(2,1)}, bf16[2,16,64,256]{3,2,1,0:T(8,128)(2,1)}, u32[]{:S(2)}, u32[]{:S(2)}) collective-permute-start(bf16[2,16,64,256]{3,2,1,0:T(8,128)(2,1)} %dynamic-slice_bitcast_fusion), channel_id=1, source_target_pairs={{0,128},{128,0},{1,129},{129,1},{2,130},{130,2},{3,131},{131,3},{4... | collective-permute-start | bytes 3145736 | tf_op jit(solution)/shard_map/ppermute | solution.py:64
  96.7 15.1 %collective-permute-start.1 = (bf16[16,64,256]{2,1,0:T(8,128)(2,1)}, bf16[16,64,256]{2,1,0:T(8,128)(2,1)}, u32[]{:S(2)}, u32[]{:S(2)}) collective-permute-start(bf16[16,64,256]{2,1,0:T(8,128)(2,1)} %dynamic-slice_bitcast_fusion.3), channel_id=1, source_target_pairs={{0,8},{8,0},{16,24},{24,16},{32,40},{40,32},{48,56},{56,48},{64,72... | collective-permute-start | bytes 1572872 | tf_op jit(solution)/shard_map/ppermute | solution.py:68
  97.7 14.1 %copy-start.2 = (bf16[1024,2048]{1,0:T(8,128)(2,1)S(1)}, bf16[1024,2048]{1,0:T(8,128)(2,1)}, u32[]{:S(2)}) copy-start(bf16[1024,2048]{1,0:T(8,128)(2,1)} %param.6) | copy-start | bytes 12582916
  99.5 22.5 %collective-permute-start.3 = (bf16[16,64,256]{2,1,0:T(8,128)(2,1)S(1)}, bf16[16,64,256]{2,1,0:T(8,128)(2,1)S(1)}, u32[]{:S(2)}, u32[]{:S(2)}) collective-permute-start(bf16[16,64,256]{2,1,0:T(8,128)(2,1)S(1)} %dynamic-slice_bitcast_fusion.2), channel_id=1, source_target_pairs={{0,8},{8,0},{16,24},{24,16},{32,40},{40,32},{48,56},{56,48},{64,72... | collective-permute-start | bytes 1572872 | tf_op jit(solution)/shard_map/ppermute | solution.py:68
Sparse Core Ops, SparseCore 0:
  25.3 57.4 all-gather.2
  129.3 40.9 reduce-scatter.1

commit v11 on v8

--- a/solution.py
+++ b/solution.py
@@ -58,8 +58,9 @@
 
     side = row_at % 2
     halves = []
-    for half in jnp.split(partial.astype(jnp.bfloat16), 2, axis=3):
-        pairs = half.reshape(tensor_count, AB, NBC, TB, NOCC // 2)
+    pieces = 4
+    for half in jnp.split(partial.astype(jnp.bfloat16), pieces, axis=3):
+        pairs = half.reshape(tensor_count, AB, NBC, TB, NOCC // pieces)
         mine = lax.dynamic_index_in_dim(pairs, tensor_at, axis=0, keepdims=False)
         other = lax.dynamic_index_in_dim(pairs, 1 - tensor_at, axis=0, keepdims=False)
         got_t = lax.ppermute(other, "tensor", perm=[(0, 1), (1, 0)])

time: 192 us -> 192 us (level)
  starting transfers between devices: 9.68 us -> 13.2 us
  waiting for transfers between devices: 102 us -> 100 us
    ppermute x2 -> x4, starting transfers between devices: 2.11 us -> 4.4 us  [shards(): lax.ppermute(give, 'row', perm=[(i, i ^ 1) for i in range(row_count)])]
    ppermute x2 -> x4, waiting for transfers between devices: 19.1 us -> 18.2 us  [shards(): lax.ppermute(give, 'row', perm=[(i, i ^ 1) for i in range(row_count)])]
  transfers between devices with their start and end apart: 7 -> 11, of which waited for: 6 -> 8; matrix products, arithmetic and copies ran while one was open for 18% -> 16% of each run, Pallas kernels for 0% -> 0%
where the time goes in v11:
time: 192 us; the launch traced here: 191 us
  waiting for transfers between devices  100 us (52%)
  local copies, waits for them, and re-layouts  28 us (15%)
  blocking collectives  15.4 us (8%)
  matrix products  14.8 us (8%)
  between operations  13.6 us (7%)
  starting transfers between devices  13.2 us (7%)
  other arithmetic  5.91 us (3%)
    reduce_scatter x1, waiting for transfers between devices, shards(): lax.psum_scatter(z, 'col', scatter_dimension=0, tiled=True)  41.2 us
    all_to_all x1, waiting for transfers between devices, shards(): recv = lax.all_to_all(send, owners, split_axis=0, concat_axis=0, tiled=True)  36.7 us
    ppermute x4, waiting for transfers between devices, shards(): lax.ppermute(give, 'row', perm=[(i, i ^ 1) for i in range(row_count)])  18.2 us
    all_to_all x1, blocking collectives, shards(): got_rows = lax.all_to_all(w, 'row', split_axis=0, concat_axis=0, tiled=True)  15.4 us
    reshape x1, local copies, waits for them, and re-layouts, shards(): dense.reshape(aux_blocks * NBC, mu_blocks, qsize, TB).transpose(0, 3, 1, 2)  11.7 us
    all_to_all x1, starting transfers between devices, shards(): recv = lax.all_to_all(send, owners, split_axis=0, concat_axis=0, tiled=True)  7.32 us
    dot_general x1, matrix products, shards(): jnp.dot(selector, slices, preferred_element_type=jnp.float32)  6.04 us
    dot_general x1, matrix products, shards(): jnp.einsum('bwk,ki->bwi', dense, occ_q, preferred_element_type=jnp.float32)  5.76 us
  transfers between devices with their start and end apart: 11, of which 8 were waited for; matrix products, arithmetic and copies ran while one was open for 16% of the time, Pallas kernels for 0%

profile of v11, /device:TPU:32, one launch (start us, length us, event | category | flops | bytes accessed | tf_op | source)
XLA Modules:
  0.0 191.3 jit_solution(14939026325379226016)
XLA Ops:
  6.5 0.7 all-gather.2.cloned.1.call-update
  7.3 0.7 convert.16
  8.0 0.7 subtract_convert_fusion
  8.7 0.1 copy.14
  8.8 0.1 convert_element_type.147
  8.9 3.3 %reshape.109 = bf16[32,8,4,1024]{3,2,1,0:T(4,128)(2,1)S(1)} reshape(bf16[32,8,4096]{2,1,0:T(8,128)(2,1)} %param.4) | data formatting | bytes 4194304 | tf_op jit(solution)/shard_map/reshape | solution.py:33
  12.2 1.2 copy.13
  13.4 0.1 broadcast_in_dim.10
  13.5 1.9 pad_maximum_fusion
  15.3 7.3 %all-to-all-start = ((bf16[32,33,1024]{2,1,0:T(8,128)(2,1)}), bf16[32,33,1024]{2,1,0:T(8,128)(2,1)S(1)}, u32[]{:S(2)}, u32[]{:S(2)}) async-start(bf16[32,33,1024]{2,1,0:T(8,128)(2,1)} %pad_maximum_fusion), calls=%async_computation | async-start | bytes 5242880 | tf_op jit(solution)/shard_map/all_to_all | solution.py:39
  22.7 36.7 %all-to-all-done = bf16[32,33,1024]{2,1,0:T(8,128)(2,1)S(1)} async-done(((bf16[32,33,1024]{2,1,0:T(8,128)(2,1)}), bf16[32,33,1024]{2,1,0:T(8,128)(2,1)S(1)}, u32[]{:S(2)}, u32[]{:S(2)}) %all-to-all-start) | async-done | bytes 2162720 | tf_op jit(solution)/shard_map/all_to_all | solution.py:39
  59.4 0.5 reshape.125
  60.0 0.2 slice.35
  60.2 0.5 fusion.15
  60.7 6.0 %fusion.2 = bf16[2048,1024]{1,0:T(8,128)(2,1)} fusion(bf16[1024,1024]{1,0:T(8,128)(2,1)S(1)} %bitcast.139, s32[1024]{0:T(1024)S(1)} %fusion.15), kind=kOutput, calls=%fused_computation.3 | convolution fusion | flops 4299161600 | bytes 6295552 | tf_op jit(solution)/shard_map/dot_general | solution.py:52
  66.7 11.7 %reshape.112 = bf16[64,32,16,64]{3,2,1,0:T(8,128)(2,1)} reshape(bf16[2048,1024]{1,0:T(8,128)(2,1)} %fusion.2) | data formatting | bytes 8388608 | tf_op jit(solution)/shard_map/reshape | solution.py:53
  78.4 2.8 %all-gather.2.cloned.1.call-done = bf16[2048,512]{1,0:T(8,128)(2,1)} async-done(((bf16[128,512]{1,0:T(8,128)(2,1)}), bf16[2048,512]{1,0:T(8,128)(2,1)}) %all-gather.2.cloned.1.call-update) | async-done | bytes 2097168 | tf_op jit(solution)/shard_map/all_gather | solution.py:43
  81.2 1.1 constant_dynamic-slice_fusion
  82.2 5.8 %convolution_convert_fusion = bf16[4,16,64,512]{3,2,1,0:T(8,128)(2,1)S(1)} fusion(bf16[4,16,64,512]{2,3,1,0:T(8,128)(2,1)} %bitcast.125, bf16[512,512,1,1]{1,0,3,2:T(8,128)(2,1)S(1)} %bitcast.138), kind=kOutput, calls=%fused_computation.4 | convolution fusion | flops 2149580800 | bytes 8912896 | tf_op jit(solution)/shard_map/bwk,ki->bwi/dot_general | solution.py:56
  88.0 1.2 fusion.38
  89.2 1.0 copy-done.1
  90.2 0.8 dynamic-slice_bitcast_fusion.3
  91.0 0.6 collective-permute-start.2
  91.7 0.3 collective-permute-start.4
  92.0 0.6 collective-permute-start.6
  92.6 0.7 collective-permute-done
  93.2 1.4 fusion.14
  94.7 1.2 collective-permute-start.1
  96.0 0.2 fusion.13
  96.2 1.0 collective-permute-start.3
  97.1 0.2 fusion.12
  97.4 1.2 collective-permute-start.5
  98.6 0.2 fusion.11
  98.9 1.0 collective-permute-start.7
  99.8 4.1 %collective-permute-done.1 = bf16[16,64,128]{2,1,0:T(8,128)(2,1)S(1)} collective-permute-done((bf16[16,64,128]{2,1,0:T(8,128)(2,1)S(1)}, bf16[16,64,128]{2,1,0:T(8,128)(2,1)S(1)}, u32[]{:S(2)}, u32[]{:S(2)}) %collective-permute-start.1) | collective-permute-done | bytes 262176 | tf_op jit(solution)/shard_map/ppermute | solution.py:70
  103.9 0.7 fusion.10
  104.7 4.9 %collective-permute-done.3 = bf16[16,64,128]{2,1,0:T(8,128)(2,1)S(1)} collective-permute-done((bf16[16,64,128]{2,1,0:T(8,128)(2,1)S(1)}, bf16[16,64,128]{2,1,0:T(8,128)(2,1)S(1)}, u32[]{:S(2)}, u32[]{:S(2)}) %collective-permute-start.3) | collective-permute-done | bytes 262176 | tf_op jit(solution)/shard_map/ppermute | solution.py:70
  109.5 0.7 fusion.9
  110.3 4.9 %collective-permute-done.5 = bf16[16,64,128]{2,1,0:T(8,128)(2,1)S(1)} collective-permute-done((bf16[16,64,128]{2,1,0:T(8,128)(2,1)S(1)}, bf16[16,64,128]{2,1,0:T(8,128)(2,1)S(1)}, u32[]{:S(2)}, u32[]{:S(2)}) %collective-permute-start.5) | collective-permute-done | bytes 262176 | tf_op jit(solution)/shard_map/ppermute | solution.py:70
  115.1 0.7 fusion.8
  115.9 4.4 %collective-permute-done.7 = bf16[16,64,128]{2,1,0:T(8,128)(2,1)S(1)} collective-permute-done((bf16[16,64,128]{2,1,0:T(8,128)(2,1)S(1)}, bf16[16,64,128]{2,1,0:T(8,128)(2,1)S(1)}, u32[]{:S(2)}, u32[]{:S(2)}) %collective-permute-start.7) | collective-permute-done | bytes 262176 | tf_op jit(solution)/shard_map/ppermute | solution.py:70
  120.3 0.7 fusion.7
  121.1 0.1 pad_maximum_fusion.1
  121.2 2.5 %copy.17 = bf16[2048,512]{1,0:T(8,128)(2,1)} copy(bf16[2048,512]{0,1:T(8,128)(2,1)S(1)} %pad_maximum_fusion.1) | data formatting | bytes 4194304 | tf_op jit(solution)/shard_map/concatenate | solution.py:75
  123.7 3.2 %copy.18 = bf16[8,16,16,512]{3,2,1,0:T(8,128)(2,1)} copy(bf16[8,16,16,512]{3,2,0,1:T(8,128)(2,1)} %bitcast.128) | data formatting | bytes 4194304 | tf_op jit(solution)/shard_map/transpose | solution.py:79
  126.9 41.2 %reduce-scatter.2.cloned.1.call-done = bf16[256,512]{1,0:T(8,128)(2,1)} async-done(((bf16[2048,512]{1,0:T(8,128)(2,1)}), bf16[256,512]{1,0:T(8,128)(2,1)}) %reduce-scatter.2.cloned.1.call-update) | async-done | bytes 262160 | tf_op jit(solution)/shard_map/reduce_scatter | solution.py:81
  168.2 15.4 %all_to_all.10 = bf16[16,16,512]{2,1,0:T(8,128)(2,1)S(1)} all-to-all(bf16[16,16,512]{2,1,0:T(8,128)(2,1)} %bitcast.141), channel_id=1, replica_groups=mesh['tensor'=2,'row'=16,'col'=8] {'row'}, dimensions={0} | all-to-all | bytes 524288 | tf_op jit(solution)/shard_map/all_to_all | solution.py:83
  183.6 0.9 copy.24
  (21 shorter events, 0.4 us)
Async XLA Ops:
  6.5 74.6 %all-gather.2.cloned.1.call-start = ((), (), s32[]{:S(2)}) async-start(), calls=%async_computation.3 | async-start | bytes 2228224 | tf_op jit(solution)/shard_map/all_gather | solution.py:43
  15.3 44.1 %all-to-all-start = ((bf16[32,33,1024]{2,1,0:T(8,128)(2,1)}), bf16[32,33,1024]{2,1,0:T(8,128)(2,1)S(1)}, u32[]{:S(2)}, u32[]{:S(2)}) async-start(bf16[32,33,1024]{2,1,0:T(8,128)(2,1)} %pad_maximum_fusion), calls=%async_computation | async-start | bytes 5242880 | tf_op jit(solution)/shard_map/all_to_all | solution.py:39
  22.6 145.5 %reduce-scatter.2.cloned.1.call-start = ((), (), s32[]{:S(2)}) async-start(), calls=%async_computation.4 | async-start | bytes 2359296 | tf_op jit(solution)/shard_map/reduce_scatter | solution.py:81
  89.2 1.0 copy-start.1
  91.0 2.3 %collective-permute-start = (bf16[2,16,64,128]{3,2,1,0:T(8,128)(2,1)}, bf16[2,16,64,128]{3,2,1,0:T(8,128)(2,1)}, u32[]{:S(2)}, u32[]{:S(2)}) collective-permute-start(bf16[2,16,64,128]{3,2,1,0:T(8,128)(2,1)} %dynamic-slice_bitcast_fusion.3), channel_id=1, source_target_pairs={{0,128},{128,0},{1,129},{129,1},{2,130},{130,2},{3,131},{131,3},{4... | collective-permute-start | bytes 1572872 | tf_op jit(solution)/shard_map/ppermute | solution.py:66
  91.0 4.9 %collective-permute-start.2 = (bf16[2,16,64,128]{3,2,1,0:T(8,128)(2,1)S(1)}, bf16[2,16,64,128]{3,2,1,0:T(8,128)(2,1)S(1)}, u32[]{:S(2)}, u32[]{:S(2)}) collective-permute-start(bf16[2,16,64,128]{3,2,1,0:T(8,128)(2,1)S(1)} %dynamic-slice_bitcast_fusion.2), channel_id=1, source_target_pairs={{0,128},{128,0},{1,129},{129,1},{2,130},{130,2},{3,131},{131,3},{4... | collective-permute-start | bytes 1572872 | tf_op jit(solution)/shard_map/ppermute | solution.py:66
  91.7 5.5 %collective-permute-start.4 = (bf16[2,16,64,128]{3,2,1,0:T(8,128)(2,1)S(1)}, bf16[2,16,64,128]{3,2,1,0:T(8,128)(2,1)S(1)}, u32[]{:S(2)}, u32[]{:S(2)}) collective-permute-start(bf16[2,16,64,128]{3,2,1,0:T(8,128)(2,1)S(1)} %dynamic-slice_bitcast_fusion.1), channel_id=1, source_target_pairs={{0,128},{128,0},{1,129},{129,1},{2,130},{130,2},{3,131},{131,3},{4... | collective-permute-start | bytes 1572872 | tf_op jit(solution)/shard_map/ppermute | solution.py:66
  92.0 11.9 %copy-start = (bf16[1024,2048]{1,0:T(8,128)(2,1)S(1)}, bf16[1024,2048]{1,0:T(8,128)(2,1)}, u32[]{:S(2)}) copy-start(bf16[1024,2048]{1,0:T(8,128)(2,1)} %param.6) | copy-start | bytes 12582916
  92.0 6.6 %collective-permute-start.6 = (bf16[2,16,64,128]{3,2,1,0:T(8,128)(2,1)S(1)}, bf16[2,16,64,128]{3,2,1,0:T(8,128)(2,1)S(1)}, u32[]{:S(2)}, u32[]{:S(2)}) collective-permute-start(bf16[2,16,64,128]{3,2,1,0:T(8,128)(2,1)S(1)} %dynamic-slice_bitcast_fusion), channel_id=1, source_target_pairs={{0,128},{128,0},{1,129},{129,1},{2,130},{130,2},{3,131},{131,3},{4... | collective-permute-start | bytes 1572872 | tf_op jit(solution)/shard_map/ppermute | solution.py:66
  94.7 9.2 %collective-permute-start.1 = (bf16[16,64,128]{2,1,0:T(8,128)(2,1)S(1)}, bf16[16,64,128]{2,1,0:T(8,128)(2,1)S(1)}, u32[]{:S(2)}, u32[]{:S(2)}) collective-permute-start(bf16[16,64,128]{2,1,0:T(8,128)(2,1)S(1)} %dynamic-slice_bitcast_fusion.7), channel_id=1, source_target_pairs={{0,8},{8,0},{16,24},{24,16},{32,40},{40,32},{48,56},{56,48},{64,72... | collective-permute-start | bytes 786440 | tf_op jit(solution)/shard_map/ppermute | solution.py:70
  96.2 13.3 %collective-permute-start.3 = (bf16[16,64,128]{2,1,0:T(8,128)(2,1)S(1)}, bf16[16,64,128]{2,1,0:T(8,128)(2,1)S(1)}, u32[]{:S(2)}, u32[]{:S(2)}) collective-permute-start(bf16[16,64,128]{2,1,0:T(8,128)(2,1)S(1)} %dynamic-slice_bitcast_fusion.6), channel_id=1, source_target_pairs={{0,8},{8,0},{16,24},{24,16},{32,40},{40,32},{48,56},{56,48},{64,72... | collective-permute-start | bytes 786440 | tf_op jit(solution)/shard_map/ppermute | solution.py:70
  97.4 17.8 %collective-permute-start.5 = (bf16[16,64,128]{2,1,0:T(8,128)(2,1)S(1)}, bf16[16,64,128]{2,1,0:T(8,128)(2,1)S(1)}, u32[]{:S(2)}, u32[]{:S(2)}) collective-permute-start(bf16[16,64,128]{2,1,0:T(8,128)(2,1)S(1)} %dynamic-slice_bitcast_fusion.5), channel_id=1, source_target_pairs={{0,8},{8,0},{16,24},{24,16},{32,40},{40,32},{48,56},{56,48},{64,72... | collective-permute-start | bytes 786440 | tf_op jit(solution)/shard_map/ppermute | solution.py:70
  98.9 21.5 %collective-permute-start.7 = (bf16[16,64,128]{2,1,0:T(8,128)(2,1)S(1)}, bf16[16,64,128]{2,1,0:T(8,128)(2,1)S(1)}, u32[]{:S(2)}, u32[]{:S(2)}) collective-permute-start(bf16[16,64,128]{2,1,0:T(8,128)(2,1)S(1)} %dynamic-slice_bitcast_fusion.4), channel_id=1, source_target_pairs={{0,8},{8,0},{16,24},{24,16},{32,40},{40,32},{48,56},{56,48},{64,72... | collective-permute-start | bytes 786440 | tf_op jit(solution)/shard_map/ppermute | solution.py:70
Sparse Core Ops, SparseCore 0:
  9.8 71.3 all-gather.1
  127.0 41.0 reduce-scatter.1

commit v12 on v8

--- a/solution.py
+++ b/solution.py
@@ -79,7 +79,12 @@
     z = z.reshape(col_count * row_count * chunk, NOCC)
     w = lax.psum_scatter(z, "col", scatter_dimension=0, tiled=True).reshape(row_count, chunk, NOCC)
 
-    got_rows = lax.all_to_all(w, "row", split_axis=0, concat_axis=0, tiled=True)
+    arrived = [lax.dynamic_index_in_dim(w, row_at, axis=0, keepdims=False)]
+    for shift in range(1, row_count):
+        piece = lax.dynamic_index_in_dim(w, (row_at + shift) % row_count, axis=0, keepdims=False)
+        perm = [(i, (i + shift) % row_count) for i in range(row_count)]
+        arrived.append(lax.ppermute(piece, "row", perm=perm))
+    got_rows = jnp.stack(arrived)[(row_at - jnp.arange(row_count)) % row_count]
     out = got_rows.reshape(PB, 2, chunk, NOCC).transpose(2, 1, 0, 3)
     return out.reshape(chunk, AB * PB, NOCC)
 

time: 192 us -> 212 us (1.10)
  starting transfers between devices: 9.68 us -> 40.2 us
  blocking collectives: 15.4 us -> 0 us
    ppermute x0 -> x15, starting transfers between devices: none -> 30.5 us  [shards(): arrived.append(lax.ppermute(piece, 'row', perm=perm))]
    all_to_all x1 -> x0, blocking collectives: 15.4 us -> none  [shards(): got_rows = lax.all_to_all(w, 'row', split_axis=0, concat_axis=0, tiled=True)]
  transfers between devices with their start and end apart: 7 -> 22, of which waited for: 6 -> 9; matrix products, arithmetic and copies ran while one was open for 18% -> 17% of each run, Pallas kernels for 0% -> 0%
where the time goes in v12:
time: 212 us; the launch traced here: 210 us
  waiting for transfers between devices  104 us (49%)
  starting transfers between devices  40.2 us (19%)
  local copies, waits for them, and re-layouts  29.2 us (14%)
  matrix products  15.5 us (7%)
  between operations  13.9 us (7%)
  other arithmetic  7.58 us (4%)
    reduce_scatter x1, waiting for transfers between devices, shards(): lax.psum_scatter(z, 'col', scatter_dimension=0, tiled=True)  41 us
    all_to_all x1, waiting for transfers between devices, shards(): recv = lax.all_to_all(send, owners, split_axis=0, concat_axis=0, tiled=True)  36.7 us
    ppermute x15, starting transfers between devices, shards(): arrived.append(lax.ppermute(piece, 'row', perm=perm))  30.5 us
    ppermute x2, waiting for transfers between devices, shards(): lax.ppermute(give, 'row', perm=[(i, i ^ 1) for i in range(row_count)])  19.1 us
    reshape x1, local copies, waits for them, and re-layouts, shards(): dense.reshape(aux_blocks * NBC, mu_blocks, qsize, TB).transpose(0, 3, 1, 2)  11.7 us
    all_to_all x1, starting transfers between devices, shards(): recv = lax.all_to_all(send, owners, split_axis=0, concat_axis=0, tiled=True)  7.32 us
    dot_general x1, matrix products, shards(): jnp.dot(selector, slices, preferred_element_type=jnp.float32)  6.06 us
    dot_general x1, matrix products, shards(): jnp.einsum('bwk,ki->bwi', dense, occ_q, preferred_element_type=jnp.float32)  5.77 us
  transfers between devices with their start and end apart: 22, of which 9 were waited for; matrix products, arithmetic and copies ran while one was open for 17% of the time, Pallas kernels for 0%

profile of v12, /device:TPU:32, one launch (start us, length us, event | category | flops | bytes accessed | tf_op | source)
XLA Modules:
  0.0 210.1 jit_solution(9550967064256321688)
XLA Ops:
  6.5 0.7 all-gather.2.cloned.1.call-update
  7.3 0.7 convert.12
  8.0 0.7 subtract_convert_fusion
  8.9 3.3 %reshape.144 = bf16[32,8,4,1024]{3,2,1,0:T(4,128)(2,1)S(1)} reshape(bf16[32,8,4096]{2,1,0:T(8,128)(2,1)} %param.4) | data formatting | bytes 4194304 | tf_op jit(solution)/shard_map/reshape | solution.py:33
  12.2 1.2 copy.13
  13.5 1.8 pad_maximum_fusion
  15.3 7.3 %all-to-all-start = ((bf16[32,33,1024]{2,1,0:T(8,128)(2,1)}), bf16[32,33,1024]{2,1,0:T(8,128)(2,1)S(1)}, u32[]{:S(2)}, u32[]{:S(2)}) async-start(bf16[32,33,1024]{2,1,0:T(8,128)(2,1)} %pad_maximum_fusion), calls=%async_computation | async-start | bytes 5242880 | tf_op jit(solution)/shard_map/all_to_all | solution.py:39
  22.7 36.7 %all-to-all-done = bf16[32,33,1024]{2,1,0:T(8,128)(2,1)S(1)} async-done(((bf16[32,33,1024]{2,1,0:T(8,128)(2,1)}), bf16[32,33,1024]{2,1,0:T(8,128)(2,1)S(1)}, u32[]{:S(2)}, u32[]{:S(2)}) %all-to-all-start) | async-done | bytes 2162720 | tf_op jit(solution)/shard_map/all_to_all | solution.py:39
  59.4 0.5 reshape.158
  60.2 0.5 fusion.13
  60.7 6.1 %fusion.2 = bf16[2048,1024]{1,0:T(8,128)(2,1)} fusion(bf16[1024,1024]{1,0:T(8,128)(2,1)S(1)} %bitcast.147, s32[1024]{0:T(1024)S(1)} %fusion.13), kind=kOutput, calls=%fused_computation.4 | convolution fusion | flops 4299161600 | bytes 6295552 | tf_op jit(solution)/shard_map/dot_general | solution.py:52
  66.7 11.7 %reshape.147 = bf16[64,32,16,64]{3,2,1,0:T(8,128)(2,1)} reshape(bf16[2048,1024]{1,0:T(8,128)(2,1)} %fusion.2) | data formatting | bytes 8388608 | tf_op jit(solution)/shard_map/reshape | solution.py:53
  78.4 2.9 %all-gather.2.cloned.1.call-done = bf16[2048,512]{1,0:T(8,128)(2,1)} async-done(((bf16[128,512]{1,0:T(8,128)(2,1)}), bf16[2048,512]{1,0:T(8,128)(2,1)}) %all-gather.2.cloned.1.call-update) | async-done | bytes 2097168 | tf_op jit(solution)/shard_map/all_gather | solution.py:43
  81.4 1.1 constant_dynamic-slice_fusion
  82.5 5.8 %convolution_convert_fusion = bf16[4,16,64,512]{3,2,1,0:T(8,128)(2,1)S(1)} fusion(bf16[4,16,64,512]{2,3,1,0:T(8,128)(2,1)} %bitcast.137, bf16[512,512,1,1]{1,0,3,2:T(8,128)(2,1)S(1)} %bitcast.146), kind=kOutput, calls=%fused_computation.7 | convolution fusion | flops 2149580800 | bytes 8912896 | tf_op jit(solution)/shard_map/bwk,ki->bwi/dot_general | solution.py:56
  88.8 1.2 dynamic-slice_bitcast_fusion
  90.4 1.2 collective-permute-done
  91.6 1.9 fusion.8
  93.5 0.8 dynamic-slice_bitcast_fusion.3
  94.4 1.2 collective-permute-start.1
  95.5 1.7 fusion.7
  97.3 1.0 collective-permute-start.3
  98.3 11.2 %collective-permute-done.1 = bf16[16,64,256]{2,1,0:T(8,128)(2,1)} collective-permute-done((bf16[16,64,256]{2,1,0:T(8,128)(2,1)}, bf16[16,64,256]{2,1,0:T(8,128)(2,1)}, u32[]{:S(2)}, u32[]{:S(2)}) %collective-permute-start.1) | collective-permute-done | bytes 524320 | tf_op jit(solution)/shard_map/ppermute | solution.py:69
  109.5 2.3 %fusion.6 = bf16[2048,256]{0,1:T(8,128)(2,1)S(1)} fusion(bf16[16,64,2048]{2,1,0:T(8,128)(2,1)S(1)} %bitcast.151, bf16[16,64,256]{2,1,0:T(8,128)(2,1)} %collective-permute-done.1, bf16[2,16,64,256]{3,2,1,0:T(8,128)(2,1)S(1)} %fusion.8, s32[]{:T(128)S(6)} %select_n.167), kind=kOutput, calls=%fused_computation.12 | convolution fusion | flops 1075314688 | bytes 6291460 | tf_op jit(solution)/shard_map/nwi,nwv->vi/dot_general | solution.py:75
  111.8 8.0 %collective-permute-done.3 = bf16[16,64,256]{2,1,0:T(8,128)(2,1)S(1)} collective-permute-done((bf16[16,64,256]{2,1,0:T(8,128)(2,1)S(1)}, bf16[16,64,256]{2,1,0:T(8,128)(2,1)S(1)}, u32[]{:S(2)}, u32[]{:S(2)}) %collective-permute-start.3) | collective-permute-done | bytes 524320 | tf_op jit(solution)/shard_map/ppermute | solution.py:69
  119.8 1.3 fusion.5
  121.2 2.5 %copy.17 = bf16[2048,512]{1,0:T(8,128)(2,1)} copy(bf16[2048,512]{0,1:T(8,128)(2,1)S(1)} %pad_maximum_fusion.1) | data formatting | bytes 4194304 | tf_op jit(solution)/shard_map/concatenate | solution.py:74
  123.8 3.2 %copy.18 = bf16[8,16,16,512]{3,2,1,0:T(8,128)(2,1)} copy(bf16[8,16,16,512]{3,2,0,1:T(8,128)(2,1)} %bitcast.140) | data formatting | bytes 4194304 | tf_op jit(solution)/shard_map/transpose | solution.py:78
  127.2 41.0 %reduce-scatter.2.cloned.1.call-done = bf16[256,512]{1,0:T(8,128)(2,1)} async-done(((bf16[2048,512]{1,0:T(8,128)(2,1)}), bf16[256,512]{1,0:T(8,128)(2,1)}) %reduce-scatter.2.cloned.1.call-update) | async-done | bytes 262160 | tf_op jit(solution)/shard_map/reduce_scatter | solution.py:80
  168.2 0.9 dynamic-slice_bitcast_fusion.4
  169.1 1.7 collective-permute-start.4
  170.8 2.6 %collective-permute-start.5 = (bf16[16,512]{1,0:T(8,128)(2,1)S(1)}, bf16[16,512]{1,0:T(8,128)(2,1)S(1)}, u32[]{:S(2)}, u32[]{:S(2)}) collective-permute-start(bf16[16,512]{1,0:T(8,128)(2,1)S(1)} %get-tuple-element.20), channel_id=1, source_target_pairs={{0,16},{8,24},{16,32},{24,40},{32,48},{40,56},{48,64},{56,72},{64,... | collective-permute-start | bytes 49160 | tf_op jit(solution)/shard_map/ppermute | solution.py:86
  173.4 2.3 %collective-permute-start.6 = (bf16[16,512]{1,0:T(8,128)(2,1)S(1)}, bf16[16,512]{1,0:T(8,128)(2,1)S(1)}, u32[]{:S(2)}, u32[]{:S(2)}) collective-permute-start(bf16[16,512]{1,0:T(8,128)(2,1)S(1)} %get-tuple-element.19), channel_id=1, source_target_pairs={{0,24},{8,32},{16,40},{24,48},{32,56},{40,64},{48,72},{56,80},{64,... | collective-permute-start | bytes 49160 | tf_op jit(solution)/shard_map/ppermute | solution.py:86
  175.8 1.5 collective-permute-start.7
  177.3 1.2 collective-permute-start.8
  178.4 1.6 collective-permute-start.9
  180.1 3.3 %collective-permute-start.10 = (bf16[16,512]{1,0:T(8,128)(2,1)S(1)}, bf16[16,512]{1,0:T(8,128)(2,1)S(1)}, u32[]{:S(2)}, u32[]{:S(2)}) collective-permute-start(bf16[16,512]{1,0:T(8,128)(2,1)S(1)} %get-tuple-element.15), channel_id=1, source_target_pairs={{0,56},{8,64},{16,72},{24,80},{32,88},{40,96},{48,104},{56,112},{6... | collective-permute-start | bytes 49160 | tf_op jit(solution)/shard_map/ppermute | solution.py:86
  183.4 2.0 collective-permute-start.11
  185.4 2.0 collective-permute-start.12
  187.3 3.3 %collective-permute-start.13 = (bf16[16,512]{1,0:T(8,128)(2,1)S(1)}, bf16[16,512]{1,0:T(8,128)(2,1)S(1)}, u32[]{:S(2)}, u32[]{:S(2)}) collective-permute-start(bf16[16,512]{1,0:T(8,128)(2,1)S(1)} %get-tuple-element.12), channel_id=1, source_target_pairs={{0,80},{8,88},{16,96},{24,104},{32,112},{40,120},{48,0},{56,8},{64... | collective-permute-start | bytes 49160 | tf_op jit(solution)/shard_map/ppermute | solution.py:86
  190.6 3.5 %collective-permute-start.14 = (bf16[16,512]{1,0:T(8,128)(2,1)S(1)}, bf16[16,512]{1,0:T(8,128)(2,1)S(1)}, u32[]{:S(2)}, u32[]{:S(2)}) collective-permute-start(bf16[16,512]{1,0:T(8,128)(2,1)S(1)} %get-tuple-element.11), channel_id=1, source_target_pairs={{0,88},{8,96},{16,104},{24,112},{32,120},{40,0},{48,8},{56,16},{64... | collective-permute-start | bytes 49160 | tf_op jit(solution)/shard_map/ppermute | solution.py:86
  194.2 2.1 %collective-permute-start.15 = (bf16[16,512]{1,0:T(8,128)(2,1)S(1)}, bf16[16,512]{1,0:T(8,128)(2,1)S(1)}, u32[]{:S(2)}, u32[]{:S(2)}) collective-permute-start(bf16[16,512]{1,0:T(8,128)(2,1)S(1)} %get-tuple-element.10), channel_id=1, source_target_pairs={{0,96},{8,104},{16,112},{24,120},{32,0},{40,8},{48,16},{56,24},{64... | collective-permute-start | bytes 49160 | tf_op jit(solution)/shard_map/ppermute | solution.py:86
  196.3 0.9 collective-permute-start.17
  197.3 2.4 %collective-permute-start.18 = (bf16[16,512]{1,0:T(8,128)(2,1)S(1)}, bf16[16,512]{1,0:T(8,128)(2,1)S(1)}, u32[]{:S(2)}, u32[]{:S(2)}) collective-permute-start(bf16[16,512]{1,0:T(8,128)(2,1)S(1)} %get-tuple-element.7), channel_id=1, source_target_pairs={{0,120},{8,0},{16,8},{24,16},{32,24},{40,32},{48,40},{56,48},{64,5... | collective-permute-start | bytes 49160 | tf_op jit(solution)/shard_map/ppermute | solution.py:86
  199.7 1.5 collective-permute-done.16
  201.3 0.4 collective-permute-done.17
  201.8 0.6 gather_fusion
  202.4 0.9 copy.24
  (53 shorter events, 1.9 us)
Async XLA Ops:
  6.5 74.8 %all-gather.2.cloned.1.call-start = ((), (), s32[]{:S(2)}) async-start(), calls=%async_computation.2 | async-start | bytes 2228224 | tf_op jit(solution)/shard_map/all_gather | solution.py:43
  15.3 44.1 %all-to-all-start = ((bf16[32,33,1024]{2,1,0:T(8,128)(2,1)}), bf16[32,33,1024]{2,1,0:T(8,128)(2,1)S(1)}, u32[]{:S(2)}, u32[]{:S(2)}) async-start(bf16[32,33,1024]{2,1,0:T(8,128)(2,1)} %pad_maximum_fusion), calls=%async_computation | async-start | bytes 5242880 | tf_op jit(solution)/shard_map/all_to_all | solution.py:39
  22.6 145.6 %reduce-scatter.2.cloned.1.call-start = ((), (), s32[]{:S(2)}) async-start(), calls=%async_computation.3 | async-start | bytes 2359296 | tf_op jit(solution)/shard_map/reduce_scatter | solution.py:80
  88.6 1.6 copy-start
  88.7 2.9 %collective-permute-start = (bf16[2,16,64,256]{3,2,1,0:T(8,128)(2,1)S(1)}, bf16[2,16,64,256]{3,2,1,0:T(8,128)(2,1)}, u32[]{:S(2)}, u32[]{:S(2)}) collective-permute-start(bf16[2,16,64,256]{3,2,1,0:T(8,128)(2,1)S(1)} %dynamic-slice_bitcast_fusion.1), channel_id=1, source_target_pairs={{0,128},{128,0},{1,129},{129,1},{2,130},{130,2},{3,131},{131,3},{4... | collective-permute-start | bytes 3145736 | tf_op jit(solution)/shard_map/ppermute | solution.py:65
  90.3 5.3 %collective-permute-start.2 = (bf16[2,16,64,256]{3,2,1,0:T(8,128)(2,1)}, bf16[2,16,64,256]{3,2,1,0:T(8,128)(2,1)}, u32[]{:S(2)}, u32[]{:S(2)}) collective-permute-start(bf16[2,16,64,256]{3,2,1,0:T(8,128)(2,1)} %dynamic-slice_bitcast_fusion), channel_id=1, source_target_pairs={{0,128},{128,0},{1,129},{129,1},{2,130},{130,2},{3,131},{131,3},{4... | collective-permute-start | bytes 3145736 | tf_op jit(solution)/shard_map/ppermute | solution.py:65
  94.4 15.1 %collective-permute-start.1 = (bf16[16,64,256]{2,1,0:T(8,128)(2,1)}, bf16[16,64,256]{2,1,0:T(8,128)(2,1)}, u32[]{:S(2)}, u32[]{:S(2)}) collective-permute-start(bf16[16,64,256]{2,1,0:T(8,128)(2,1)} %dynamic-slice_bitcast_fusion.3), channel_id=1, source_target_pairs={{0,8},{8,0},{16,24},{24,16},{32,40},{40,32},{48,56},{56,48},{64,72... | collective-permute-start | bytes 1572872 | tf_op jit(solution)/shard_map/ppermute | solution.py:69
  95.5 13.9 %copy-start.1 = (bf16[1024,2048]{1,0:T(8,128)(2,1)S(1)}, bf16[1024,2048]{1,0:T(8,128)(2,1)}, u32[]{:S(2)}) copy-start(bf16[1024,2048]{1,0:T(8,128)(2,1)} %param.6) | copy-start | bytes 12582916
  97.3 22.4 %collective-permute-start.3 = (bf16[16,64,256]{2,1,0:T(8,128)(2,1)S(1)}, bf16[16,64,256]{2,1,0:T(8,128)(2,1)S(1)}, u32[]{:S(2)}, u32[]{:S(2)}) collective-permute-start(bf16[16,64,256]{2,1,0:T(8,128)(2,1)S(1)} %dynamic-slice_bitcast_fusion.2), channel_id=1, source_target_pairs={{0,8},{8,0},{16,24},{24,16},{32,40},{40,32},{48,56},{56,48},{64,72... | collective-permute-start | bytes 1572872 | tf_op jit(solution)/shard_map/ppermute | solution.py:69
  169.1 9.3 %collective-permute-start.4 = (bf16[16,512]{1,0:T(8,128)(2,1)S(1)}, bf16[16,512]{1,0:T(8,128)(2,1)S(1)}, u32[]{:S(2)}, u32[]{:S(2)}) collective-permute-start(bf16[16,512]{1,0:T(8,128)(2,1)S(1)} %get-tuple-element.21), channel_id=1, source_target_pairs={{0,8},{8,16},{16,24},{24,32},{32,40},{40,48},{48,56},{56,64},{64,7... | collective-permute-start | bytes 49160 | tf_op jit(solution)/shard_map/ppermute | solution.py:86
  170.8 9.3 %collective-permute-start.5 = (bf16[16,512]{1,0:T(8,128)(2,1)S(1)}, bf16[16,512]{1,0:T(8,128)(2,1)S(1)}, u32[]{:S(2)}, u32[]{:S(2)}) collective-permute-start(bf16[16,512]{1,0:T(8,128)(2,1)S(1)} %get-tuple-element.20), channel_id=1, source_target_pairs={{0,16},{8,24},{16,32},{24,40},{32,48},{40,56},{48,64},{56,72},{64,... | collective-permute-start | bytes 49160 | tf_op jit(solution)/shard_map/ppermute | solution.py:86
  173.4 9.9 %collective-permute-start.6 = (bf16[16,512]{1,0:T(8,128)(2,1)S(1)}, bf16[16,512]{1,0:T(8,128)(2,1)S(1)}, u32[]{:S(2)}, u32[]{:S(2)}) collective-permute-start(bf16[16,512]{1,0:T(8,128)(2,1)S(1)} %get-tuple-element.19), channel_id=1, source_target_pairs={{0,24},{8,32},{16,40},{24,48},{32,56},{40,64},{48,72},{56,80},{64,... | collective-permute-start | bytes 49160 | tf_op jit(solution)/shard_map/ppermute | solution.py:86
  175.8 9.6 %collective-permute-start.7 = (bf16[16,512]{1,0:T(8,128)(2,1)S(1)}, bf16[16,512]{1,0:T(8,128)(2,1)S(1)}, u32[]{:S(2)}, u32[]{:S(2)}) collective-permute-start(bf16[16,512]{1,0:T(8,128)(2,1)S(1)} %get-tuple-element.18), channel_id=1, source_target_pairs={{0,32},{8,40},{16,48},{24,56},{32,64},{40,72},{48,80},{56,88},{64,... | collective-permute-start | bytes 49160 | tf_op jit(solution)/shard_map/ppermute | solution.py:86
  177.3 10.0 %collective-permute-start.8 = (bf16[16,512]{1,0:T(8,128)(2,1)S(1)}, bf16[16,512]{1,0:T(8,128)(2,1)S(1)}, u32[]{:S(2)}, u32[]{:S(2)}) collective-permute-start(bf16[16,512]{1,0:T(8,128)(2,1)S(1)} %get-tuple-element.17), channel_id=1, source_target_pairs={{0,40},{8,48},{16,56},{24,64},{32,72},{40,80},{48,88},{56,96},{64,... | collective-permute-start | bytes 49160 | tf_op jit(solution)/shard_map/ppermute | solution.py:86
  178.4 12.2 %collective-permute-start.9 = (bf16[16,512]{1,0:T(8,128)(2,1)S(1)}, bf16[16,512]{1,0:T(8,128)(2,1)S(1)}, u32[]{:S(2)}, u32[]{:S(2)}) collective-permute-start(bf16[16,512]{1,0:T(8,128)(2,1)S(1)} %get-tuple-element.16), channel_id=1, source_target_pairs={{0,48},{8,56},{16,64},{24,72},{32,80},{40,88},{48,96},{56,104},{64... | collective-permute-start | bytes 49160 | tf_op jit(solution)/shard_map/ppermute | solution.py:86
  180.1 14.1 %collective-permute-start.10 = (bf16[16,512]{1,0:T(8,128)(2,1)S(1)}, bf16[16,512]{1,0:T(8,128)(2,1)S(1)}, u32[]{:S(2)}, u32[]{:S(2)}) collective-permute-start(bf16[16,512]{1,0:T(8,128)(2,1)S(1)} %get-tuple-element.15), channel_id=1, source_target_pairs={{0,56},{8,64},{16,72},{24,80},{32,88},{40,96},{48,104},{56,112},{6... | collective-permute-start | bytes 49160 | tf_op jit(solution)/shard_map/ppermute | solution.py:86
  183.4 12.9 %collective-permute-start.11 = (bf16[16,512]{1,0:T(8,128)(2,1)S(1)}, bf16[16,512]{1,0:T(8,128)(2,1)S(1)}, u32[]{:S(2)}, u32[]{:S(2)}) collective-permute-start(bf16[16,512]{1,0:T(8,128)(2,1)S(1)} %get-tuple-element.14), channel_id=1, source_target_pairs={{0,64},{8,72},{16,80},{24,88},{32,96},{40,104},{48,112},{56,120},{... | collective-permute-start | bytes 49160 | tf_op jit(solution)/shard_map/ppermute | solution.py:86
  185.4 11.0 %collective-permute-start.12 = (bf16[16,512]{1,0:T(8,128)(2,1)S(1)}, bf16[16,512]{1,0:T(8,128)(2,1)S(1)}, u32[]{:S(2)}, u32[]{:S(2)}) collective-permute-start(bf16[16,512]{1,0:T(8,128)(2,1)S(1)} %get-tuple-element.13), channel_id=1, source_target_pairs={{0,72},{8,80},{16,88},{24,96},{32,104},{40,112},{48,120},{56,0},{6... | collective-permute-start | bytes 49160 | tf_op jit(solution)/shard_map/ppermute | solution.py:86
  187.3 10.0 %collective-permute-start.13 = (bf16[16,512]{1,0:T(8,128)(2,1)S(1)}, bf16[16,512]{1,0:T(8,128)(2,1)S(1)}, u32[]{:S(2)}, u32[]{:S(2)}) collective-permute-start(bf16[16,512]{1,0:T(8,128)(2,1)S(1)} %get-tuple-element.12), channel_id=1, source_target_pairs={{0,80},{8,88},{16,96},{24,104},{32,112},{40,120},{48,0},{56,8},{64... | collective-permute-start | bytes 49160 | tf_op jit(solution)/shard_map/ppermute | solution.py:86
  190.6 9.1 %collective-permute-start.14 = (bf16[16,512]{1,0:T(8,128)(2,1)S(1)}, bf16[16,512]{1,0:T(8,128)(2,1)S(1)}, u32[]{:S(2)}, u32[]{:S(2)}) collective-permute-start(bf16[16,512]{1,0:T(8,128)(2,1)S(1)} %get-tuple-element.11), channel_id=1, source_target_pairs={{0,88},{8,96},{16,104},{24,112},{32,120},{40,0},{48,8},{56,16},{64... | collective-permute-start | bytes 49160 | tf_op jit(solution)/shard_map/ppermute | solution.py:86
  194.2 5.5 %collective-permute-start.15 = (bf16[16,512]{1,0:T(8,128)(2,1)S(1)}, bf16[16,512]{1,0:T(8,128)(2,1)S(1)}, u32[]{:S(2)}, u32[]{:S(2)}) collective-permute-start(bf16[16,512]{1,0:T(8,128)(2,1)S(1)} %get-tuple-element.10), channel_id=1, source_target_pairs={{0,96},{8,104},{16,112},{24,120},{32,0},{40,8},{48,16},{56,24},{64... | collective-permute-start | bytes 49160 | tf_op jit(solution)/shard_map/ppermute | solution.py:86
  196.3 5.0 %collective-permute-start.16 = (bf16[16,512]{1,0:T(8,128)(2,1)S(1)}, bf16[16,512]{1,0:T(8,128)(2,1)S(1)}, u32[]{:S(2)}, u32[]{:S(2)}) collective-permute-start(bf16[16,512]{1,0:T(8,128)(2,1)S(1)} %get-tuple-element.9), channel_id=1, source_target_pairs={{0,104},{8,112},{16,120},{24,0},{32,8},{40,16},{48,24},{56,32},{64... | collective-permute-start | bytes 49160 | tf_op jit(solution)/shard_map/ppermute | solution.py:86
  196.3 5.3 %collective-permute-start.17 = (bf16[16,512]{1,0:T(8,128)(2,1)S(1)}, bf16[16,512]{1,0:T(8,128)(2,1)S(1)}, u32[]{:S(2)}, u32[]{:S(2)}) collective-permute-start(bf16[16,512]{1,0:T(8,128)(2,1)S(1)} %get-tuple-element.8), channel_id=1, source_target_pairs={{0,112},{8,120},{16,0},{24,8},{32,16},{40,24},{48,32},{56,40},{64,... | collective-permute-start | bytes 49160 | tf_op jit(solution)/shard_map/ppermute | solution.py:86
  197.3 4.5 %collective-permute-start.18 = (bf16[16,512]{1,0:T(8,128)(2,1)S(1)}, bf16[16,512]{1,0:T(8,128)(2,1)S(1)}, u32[]{:S(2)}, u32[]{:S(2)}) collective-permute-start(bf16[16,512]{1,0:T(8,128)(2,1)S(1)} %get-tuple-element.7), channel_id=1, source_target_pairs={{0,120},{8,0},{16,8},{24,16},{32,24},{40,32},{48,40},{56,48},{64,5... | collective-permute-start | bytes 49160 | tf_op jit(solution)/shard_map/ppermute | solution.py:86
Sparse Core Ops, SparseCore 0:
  9.8 71.5 all-gather.1
  127.1 41.0 reduce-scatter.1

commit v13 on v8

--- a/solution.py
+++ b/solution.py
@@ -72,10 +72,15 @@
     chunk = NV // (row_count * col_count)
     virt = virtual_coeff.reshape(NBC, TB, NV)
     z = jnp.concatenate(
-        [jnp.einsum("nwi,nwv->vi", h, virt, preferred_element_type=jnp.float32).astype(jnp.bfloat16) for h in halves],
-        axis=1,
+        [
+            jnp.einsum("nwi,nwv->vi", h, virt, preferred_element_type=jnp.float32)
+            .astype(jnp.bfloat16)
+            .reshape(row_count, col_count, chunk, NOCC // 2)
+            .transpose(1, 0, 2, 3)
+            for h in halves
+        ],
+        axis=3,
     )
-    z = z.reshape(row_count, col_count, chunk, NOCC).transpose(1, 0, 2, 3)
     z = z.reshape(col_count * row_count * chunk, NOCC)
     w = lax.psum_scatter(z, "col", scatter_dimension=0, tiled=True).reshape(row_count, chunk, NOCC)
 

time: 192 us -> 191 us (level)
  waiting for transfers between devices: 102 us -> 97.9 us
  matrix products: 15.4 us -> 18.8 us
    ppermute x2, waiting for transfers between devices: 19.1 us -> 15 us  [shards(): lax.ppermute(give, 'row', perm=[(i, i ^ 1) for i in range(row_count)])]
    dot_general x2, matrix products: 3.63 us -> 7 us  [shards(): jnp.einsum('nwi,nwv->vi', h, virt, preferred_element_type=jnp.float32)]
    transpose x1 -> x0, local copies, waits for them, and re-layouts: 3.16 us -> none  [shards(): z = z.reshape(row_count, col_count, chunk, NOCC).transpose(1, 0, 2, 3)]
    convert_element_type x0 -> x2, local copies, waits for them, and re-layouts: none -> 2.09 us  [shards(): z = jnp.concatenate([jnp.einsum('nwi,nwv->vi', h, virt, preferred_element...]
  transfers between devices with their start and end apart: 7 -> 7, of which waited for: 6 -> 6; matrix products, arithmetic and copies ran while one was open for 18% -> 20% of each run, Pallas kernels for 0% -> 0%
where the time goes in v13:
time: 191 us; the launch traced here: 190 us
  waiting for transfers between devices  97.9 us (51%)
  local copies, waits for them, and re-layouts  27.3 us (14%)
  matrix products  18.8 us (10%)
  blocking collectives  15.3 us (8%)
  between operations  13.6 us (7%)
  starting transfers between devices  9.58 us (5%)
  other arithmetic  7.69 us (4%)
    reduce_scatter x1, waiting for transfers between devices, shards(): lax.psum_scatter(z, 'col', scatter_dimension=0, tiled=True)  41.2 us
    all_to_all x1, waiting for transfers between devices, shards(): recv = lax.all_to_all(send, owners, split_axis=0, concat_axis=0, tiled=True)  36.7 us
    all_to_all x1, blocking collectives, shards(): got_rows = lax.all_to_all(w, 'row', split_axis=0, concat_axis=0, tiled=True)  15.3 us
    ppermute x2, waiting for transfers between devices, shards(): lax.ppermute(give, 'row', perm=[(i, i ^ 1) for i in range(row_count)])  15 us
    reshape x1, local copies, waits for them, and re-layouts, shards(): dense.reshape(aux_blocks * NBC, mu_blocks, qsize, TB).transpose(0, 3, 1, 2)  11.6 us
    all_to_all x1, starting transfers between devices, shards(): recv = lax.all_to_all(send, owners, split_axis=0, concat_axis=0, tiled=True)  7.32 us
    dot_general x2, matrix products, shards(): jnp.einsum('nwi,nwv->vi', h, virt, preferred_element_type=jnp.float32)  7 us
    dot_general x1, matrix products, shards(): jnp.dot(selector, slices, preferred_element_type=jnp.float32)  6.03 us
  transfers between devices with their start and end apart: 7, of which 6 were waited for; matrix products, arithmetic and copies ran while one was open for 20% of the time, Pallas kernels for 0%

profile of v13, /device:TPU:32, one launch (start us, length us, event | category | flops | bytes accessed | tf_op | source)
XLA Modules:
  0.0 190.1 jit_solution(1510033327312805603)
XLA Ops:
  6.5 0.7 all-gather.2.cloned.1.call-update
  7.3 0.7 convert.12
  8.0 0.7 subtract_convert_fusion
  8.7 0.1 copy.15
  8.8 0.1 convert_element_type.87
  8.9 3.3 %reshape.98 = bf16[32,8,4,1024]{3,2,1,0:T(4,128)(2,1)S(1)} reshape(bf16[32,8,4096]{2,1,0:T(8,128)(2,1)} %param.4) | data formatting | bytes 4194304 | tf_op jit(solution)/shard_map/reshape | solution.py:33
  12.2 1.2 copy.14
  13.4 0.1 broadcast_in_dim.10
  13.5 1.8 pad_maximum_fusion
  15.3 7.3 %all-to-all-start = ((bf16[32,33,1024]{2,1,0:T(8,128)(2,1)}), bf16[32,33,1024]{2,1,0:T(8,128)(2,1)S(1)}, u32[]{:S(2)}, u32[]{:S(2)}) async-start(bf16[32,33,1024]{2,1,0:T(8,128)(2,1)} %pad_maximum_fusion), calls=%async_computation | async-start | bytes 5242880 | tf_op jit(solution)/shard_map/all_to_all | solution.py:39
  22.6 0.0 reduce-scatter.2.cloned.1.call-start
  22.7 36.7 %all-to-all-done = bf16[32,33,1024]{2,1,0:T(8,128)(2,1)S(1)} async-done(((bf16[32,33,1024]{2,1,0:T(8,128)(2,1)}), bf16[32,33,1024]{2,1,0:T(8,128)(2,1)S(1)}, u32[]{:S(2)}, u32[]{:S(2)}) %all-to-all-start) | async-done | bytes 2162720 | tf_op jit(solution)/shard_map/all_to_all | solution.py:39
  59.4 0.1 fusion.19
  59.4 0.5 reshape.113
  60.0 0.2 slice.35
  60.2 0.5 fusion.13
  60.7 6.0 %fusion.2 = bf16[2048,1024]{1,0:T(8,128)(2,1)} fusion(bf16[1024,1024]{1,0:T(8,128)(2,1)S(1)} %bitcast.89, s32[1024]{0:T(1024)S(1)} %fusion.13), kind=kOutput, calls=%fused_computation.3 | convolution fusion | flops 4299161600 | bytes 6295552 | tf_op jit(solution)/shard_map/dot_general | solution.py:52
  66.7 11.6 %reshape.101 = bf16[64,32,16,64]{3,2,1,0:T(8,128)(2,1)} reshape(bf16[2048,1024]{1,0:T(8,128)(2,1)} %fusion.2) | data formatting | bytes 8388608 | tf_op jit(solution)/shard_map/reshape | solution.py:53
  78.4 3.1 %all-gather.2.cloned.1.call-done = bf16[2048,512]{1,0:T(8,128)(2,1)} async-done(((bf16[128,512]{1,0:T(8,128)(2,1)}), bf16[2048,512]{1,0:T(8,128)(2,1)}) %all-gather.2.cloned.1.call-update) | async-done | bytes 2097168 | tf_op jit(solution)/shard_map/all_gather | solution.py:43
  81.5 1.1 constant_dynamic-slice_fusion
  82.5 5.8 %convolution_convert_fusion = bf16[4,16,64,512]{3,2,1,0:T(8,128)(2,1)S(1)} fusion(bf16[4,16,64,512]{2,3,1,0:T(8,128)(2,1)} %bitcast.78, bf16[512,512,1,1]{1,0,3,2:T(8,128)(2,1)S(1)} %bitcast.88), kind=kOutput, calls=%fused_computation.6 | convolution fusion | flops 2149580800 | bytes 8912896 | tf_op jit(solution)/shard_map/bwk,ki->bwi/dot_general | solution.py:56
  88.3 0.4 fusion.22
  88.7 0.1 dynamic-slice_bitcast_fusion.1
  88.8 0.1 collective-permute-start
  88.9 1.3 dynamic-slice_bitcast_fusion
  90.2 0.2 copy-done
  90.4 0.1 collective-permute-start.2
  90.4 1.2 collective-permute-done
  91.7 1.9 %fusion.8 = bf16[2,16,64,256]{3,2,1,0:T(8,128)(2,1)S(1)} fusion(bf16[2,16,64,256]{3,2,1,0:T(8,128)(2,1)} %collective-permute-done, bf16[2,2,16,64,256]{4,3,2,1,0:T(8,128)(2,1)} %bitcast.85, s32[]{:T(128)S(6)} %select_n.33), kind=kLoop, calls=%fused_computation.16 | loop fusion | flops 2097152 | bytes 3145732 | tf_op jit(solution)/shard_map/convert_element_type | solution.py:66
  93.6 0.8 dynamic-slice_bitcast_fusion.3
  94.4 1.2 collective-permute-start.1
  95.6 0.0 collective-permute-done.2
  95.6 1.7 fusion.7
  97.4 1.0 copy-done.1
  98.3 0.8 dynamic-slice_bitcast_fusion.2
  99.2 0.9 collective-permute-start.3
  100.0 9.5 %collective-permute-done.1 = bf16[16,64,256]{2,1,0:T(8,128)(2,1)} collective-permute-done((bf16[16,64,256]{2,1,0:T(8,128)(2,1)}, bf16[16,64,256]{2,1,0:T(8,128)(2,1)}, u32[]{:S(2)}, u32[]{:S(2)}) %collective-permute-start.1) | collective-permute-done | bytes 524320 | tf_op jit(solution)/shard_map/ppermute | solution.py:69
  109.5 3.4 %fusion.6 = bf16[2048,256]{0,1:T(8,128)(2,1)} fusion(bf16[16,64,2048]{2,1,0:T(8,128)(2,1)S(1)} %bitcast.94, bf16[16,64,256]{2,1,0:T(8,128)(2,1)} %collective-permute-done.1, bf16[2,16,64,256]{3,2,1,0:T(8,128)(2,1)S(1)} %fusion.8, s32[]{:T(128)S(6)} %select_n.35), kind=kOutput, calls=%fused_computation.11 | convolution fusion | flops 1075314688 | bytes 6291460 | tf_op jit(solution)/shard_map/nwi,nwv->vi/dot_general | solution.py:76
  112.9 1.6 copy.18
  114.5 5.5 %collective-permute-done.3 = bf16[16,64,256]{2,1,0:T(8,128)(2,1)} collective-permute-done((bf16[16,64,256]{2,1,0:T(8,128)(2,1)}, bf16[16,64,256]{2,1,0:T(8,128)(2,1)}, u32[]{:S(2)}, u32[]{:S(2)}) %collective-permute-start.3) | collective-permute-done | bytes 524320 | tf_op jit(solution)/shard_map/ppermute | solution.py:69
  120.0 3.6 %fusion.5 = bf16[2048,256]{0,1:T(8,128)(2,1)S(1)} fusion(bf16[16,64,2048]{2,1,0:T(8,128)(2,1)} %bitcast.93, bf16[16,64,256]{2,1,0:T(8,128)(2,1)} %collective-permute-done.3, bf16[2,16,64,256]{3,2,1,0:T(8,128)(2,1)S(1)} %copy-done.2, s32[]{:T(128)S(6)} %select_n.35), kind=kOutput, calls=%fused_computation.10 | convolution fusion | flops 1075314688 | bytes 6291460 | tf_op jit(solution)/shard_map/nwi,nwv->vi/dot_general | solution.py:76
  123.6 0.5 copy.19
  124.1 0.3 pad_maximum_fusion.1
  124.4 1.5 copy.20
  125.9 0.0 reduce-scatter.2.cloned.1.call-update
  125.9 41.2 %reduce-scatter.2.cloned.1.call-done = bf16[256,512]{1,0:T(8,128)(2,1)} async-done(((bf16[2048,512]{1,0:T(8,128)(2,1)}), bf16[256,512]{1,0:T(8,128)(2,1)}) %reduce-scatter.2.cloned.1.call-update) | async-done | bytes 262160 | tf_op jit(solution)/shard_map/reduce_scatter | solution.py:85
  167.2 15.3 %all_to_all.10 = bf16[16,16,512]{2,1,0:T(8,128)(2,1)S(1)} all-to-all(bf16[16,16,512]{2,1,0:T(8,128)(2,1)} %bitcast.91), channel_id=1, replica_groups=mesh['tensor'=2,'row'=16,'col'=8] {'row'}, dimensions={0} | all-to-all | bytes 524288 | tf_op jit(solution)/shard_map/all_to_all | solution.py:87
  182.5 0.9 copy.26
  (10 shorter events, 0.1 us)
Async XLA Ops:
  6.5 74.9 %all-gather.2.cloned.1.call-start = ((), (), s32[]{:S(2)}) async-start(), calls=%async_computation.3 | async-start | bytes 2228224 | tf_op jit(solution)/shard_map/all_gather | solution.py:43
  15.3 44.1 %all-to-all-start = ((bf16[32,33,1024]{2,1,0:T(8,128)(2,1)}), bf16[32,33,1024]{2,1,0:T(8,128)(2,1)S(1)}, u32[]{:S(2)}, u32[]{:S(2)}) async-start(bf16[32,33,1024]{2,1,0:T(8,128)(2,1)} %pad_maximum_fusion), calls=%async_computation | async-start | bytes 5242880 | tf_op jit(solution)/shard_map/all_to_all | solution.py:39
  22.6 144.6 %reduce-scatter.2.cloned.1.call-start = ((), (), s32[]{:S(2)}) async-start(), calls=%async_computation.4 | async-start | bytes 2359296 | tf_op jit(solution)/shard_map/reduce_scatter | solution.py:85
  88.7 1.7 copy-start
  88.8 2.9 %collective-permute-start = (bf16[2,16,64,256]{3,2,1,0:T(8,128)(2,1)S(1)}, bf16[2,16,64,256]{3,2,1,0:T(8,128)(2,1)}, u32[]{:S(2)}, u32[]{:S(2)}) collective-permute-start(bf16[2,16,64,256]{3,2,1,0:T(8,128)(2,1)S(1)} %dynamic-slice_bitcast_fusion.1), channel_id=1, source_target_pairs={{0,128},{128,0},{1,129},{129,1},{2,130},{130,2},{3,131},{131,3},{4... | collective-permute-start | bytes 3145736 | tf_op jit(solution)/shard_map/ppermute | solution.py:65
  90.4 5.3 %collective-permute-start.2 = (bf16[2,16,64,256]{3,2,1,0:T(8,128)(2,1)}, bf16[2,16,64,256]{3,2,1,0:T(8,128)(2,1)}, u32[]{:S(2)}, u32[]{:S(2)}) collective-permute-start(bf16[2,16,64,256]{3,2,1,0:T(8,128)(2,1)} %dynamic-slice_bitcast_fusion), channel_id=1, source_target_pairs={{0,128},{128,0},{1,129},{129,1},{2,130},{130,2},{3,131},{131,3},{4... | collective-permute-start | bytes 3145736 | tf_op jit(solution)/shard_map/ppermute | solution.py:65
  94.4 15.1 %collective-permute-start.1 = (bf16[16,64,256]{2,1,0:T(8,128)(2,1)}, bf16[16,64,256]{2,1,0:T(8,128)(2,1)}, u32[]{:S(2)}, u32[]{:S(2)}) collective-permute-start(bf16[16,64,256]{2,1,0:T(8,128)(2,1)} %dynamic-slice_bitcast_fusion.3), channel_id=1, source_target_pairs={{0,8},{8,0},{16,24},{24,16},{32,40},{40,32},{48,56},{56,48},{64,72... | collective-permute-start | bytes 1572872 | tf_op jit(solution)/shard_map/ppermute | solution.py:69
  95.6 13.9 %copy-start.3 = (bf16[1024,2048]{1,0:T(8,128)(2,1)S(1)}, bf16[1024,2048]{1,0:T(8,128)(2,1)}, u32[]{:S(2)}) copy-start(bf16[1024,2048]{1,0:T(8,128)(2,1)} %param.6) | copy-start | bytes 12582916
  97.4 1.0 copy-start.1
  99.2 20.8 %collective-permute-start.3 = (bf16[16,64,256]{2,1,0:T(8,128)(2,1)}, bf16[16,64,256]{2,1,0:T(8,128)(2,1)}, u32[]{:S(2)}, u32[]{:S(2)}) collective-permute-start(bf16[16,64,256]{2,1,0:T(8,128)(2,1)} %dynamic-slice_bitcast_fusion.2), channel_id=1, source_target_pairs={{0,8},{8,0},{16,24},{24,16},{32,40},{40,32},{48,56},{56,48},{64,72... | collective-permute-start | bytes 1572872 | tf_op jit(solution)/shard_map/ppermute | solution.py:69
  112.9 7.1 %copy-start.2 = (bf16[2,16,64,256]{3,2,1,0:T(8,128)(2,1)S(1)}, bf16[2,16,64,256]{3,2,1,0:T(8,128)(2,1)}, u32[]{:S(2)}) copy-start(bf16[2,16,64,256]{3,2,1,0:T(8,128)(2,1)} %copy-done.1) | copy-start | bytes 3145732
Sparse Core Ops, SparseCore 0:
  9.8 71.6 all-gather.1
  126.1 41.0 reduce-scatter.1
